TPU v7x, 512 devices: a whole 4x8x8 slice. The times are simulated.
512 devices in a mesh: ctx: 32 (over z, x), exp: 16 (over y, core).
Axes of the slice: x: 4, y: 8, z: 8, core: 2. Of those that a mesh axis runs over, the one named last changes fastest.
Arguments:
- stream: bfloat16 [16, 4096, 1024], P('exp', 'ctx'), may hold values from -400 to 400
- queries: bfloat16 [16, 4096, 16, 128], P('exp', 'ctx'), may hold values from -6 to 6
- key_rows: bfloat16 [16, 4096, 2, 128], P('exp', 'ctx'), may hold values from -4 to 4
- value_rows: bfloat16 [16, 4096, 2, 128], P('exp', 'ctx'), may hold values from -6 to 6
- expert_ids: int32 [16, 4096, 2], P('exp', 'ctx'), may hold values from 0 to 127, as said below
- norm_gain: bfloat16 [1024], replicated, may hold values from 0.099609375 to 1.8984375
- router_weight: bfloat16 [1024, 128], replicated, may hold values from -0.1875 to 0.1875
- gate_weight: bfloat16 [98304, 1024], P(('ctx', 'exp')), may hold values from -0.1875 to 0.1875
- up_weight: bfloat16 [98304, 1024], P(('ctx', 'exp')), may hold values from -0.1875 to 0.1875
- down_weight: bfloat16 [98304, 1024], P(('ctx', 'exp')), may hold values from -0.21875 to 0.21875
Outputs:
- attended: bfloat16 [16, 4096, 16, 128], P('exp', 'ctx')
- expert_mix: bfloat16 [16, 4096, 1024], P('exp', 'ctx')
Inputs may be any that keep to these rules, and one draw needn't show every extreme that they name: `expert_ids`: within the rows of one device (aligned blocks of 128 positions of one sequence), a token's 2 experts differ and no expert is named more than 4 times; one expert is named exactly 4 times in every such block.
All inputs are finite; a program needn't handle non-finite values.
Results may differ from a plain program's by a relative error of at most 0.01.
Values may be sent and summed in bfloat16 or wider, within the bound.
No kernel may reach another device: no remote copies, remote signals or barrier semaphores. Data moves between devices by JAX's collectives and lax.ppermute only.
A program may use at most 64 MiB of HBM per device.

v0:
```python
import math

import jax
import jax.numpy as jnp
from jax import lax
from jax.sharding import PartitionSpec as P


def from_partner(value, axis, bit):
    return lax.ppermute(value, axis, [(i, i ^ 1 << bit) for i in range(lax.axis_size(axis))])


def expert_rows(inputs, gate_rows, up_rows, down_rows):
    features = inputs.shape[-1]
    flat_rows = inputs.reshape(-1, features)
    contract = (((1,), (1,)), ((), ()))
    gate_part = lax.dot_general(flat_rows, gate_rows, contract, preferred_element_type=jnp.float32)
    up_part = lax.dot_general(flat_rows, up_rows, contract, preferred_element_type=jnp.float32)
    hidden = (jax.nn.silu(gate_part) * up_part).astype(jnp.bfloat16)
    projected = jnp.dot(hidden, down_rows, preferred_element_type=jnp.float32)
    return projected.reshape(inputs.shape)


def attention(queries, key_rows, value_rows):
    seq_rows = queries.shape[1]
    head_count = queries.shape[2]
    head_size = queries.shape[3]
    kv_count = key_rows.shape[2]
    group_size = head_count // kv_count
    grouped = queries[0].reshape(seq_rows, kv_count, group_size, head_size)
    scaling = 1.0 / math.sqrt(head_size)
    query_pos = lax.axis_index("ctx") * seq_rows + jnp.arange(seq_rows, dtype=jnp.int32)
    initial = (
        jnp.full((kv_count, group_size, seq_rows), -1e30, jnp.float32),
        jnp.zeros((kv_count, group_size, seq_rows), jnp.float32),
        jnp.zeros((kv_count, group_size, seq_rows, head_size), jnp.float32),
    )
    key_piece = lax.all_gather(key_rows, "ctx", axis=1, tiled=True)
    value_piece = lax.all_gather(value_rows, "ctx", axis=1, tiled=True)
    piece_rows = key_piece.shape[1]
    block_rows = math.gcd(piece_rows, 512)
    block_count = piece_rows // block_rows
    key_blocks = key_piece[0].reshape(block_count, block_rows, kv_count, head_size)
    value_blocks = value_piece[0].reshape(block_count, block_rows, kv_count, head_size)

    def advance(status, members):
        running, totals, accumulated = status
        key_block, value_block, offset = members
        scores = (
            jnp.einsum("qhgd,khd->hgqk", grouped, key_block, preferred_element_type=jnp.float32)
            * scaling
        )
        key_pos = offset * block_rows + jnp.arange(block_rows, dtype=jnp.int32)
        visible = key_pos[None, :] <= query_pos[:, None]
        scores = jnp.where(visible, scores, -1e30)
        highest = jnp.maximum(running, jnp.max(scores, axis=-1))
        factor = jnp.exp(running - highest)
        weights = jnp.where(visible, jnp.exp(scores - highest[..., None]), 0.0)
        totals = totals * factor + jnp.sum(weights, axis=-1)
        accumulated = accumulated * factor[..., None] + jnp.einsum(
            "hgqk,khd->hgqd",
            weights.astype(jnp.bfloat16),
            value_block,
            preferred_element_type=jnp.float32,
        )
        return ((highest, totals, accumulated), None)

    status, unused = lax.scan(
        advance, initial, (key_blocks, value_blocks, jnp.arange(block_count, dtype=jnp.int32))
    )
    running, totals, accumulated = status
    result = accumulated / totals[..., None]
    return (
        jnp.transpose(result, (2, 0, 1, 3))
        .reshape(1, seq_rows, head_count, head_size)
        .astype(jnp.bfloat16)
    )


def local(
    stream,
    queries,
    key_rows,
    value_rows,
    expert_ids,
    norm_gain,
    router_weight,
    gate_weight,
    up_weight,
    down_weight,
):
    attended = attention(queries, key_rows, value_rows)
    ctx_count = lax.axis_size("ctx")
    exp_count = lax.axis_size("exp")
    tokens = stream.shape[1]
    features = stream.shape[2]
    top_count = expert_ids.shape[2]
    expert_total = router_weight.shape[1]
    per_ctx = expert_total // ctx_count
    quarters = exp_count // per_ctx
    capacity = 2 * tokens * top_count // expert_total
    widened = stream[0].astype(jnp.float32)
    mean_square = jnp.mean(widened * widened, axis=-1, keepdims=True)
    normed = (widened * lax.rsqrt(mean_square + 1e-06) * norm_gain.astype(jnp.float32)).astype(
        jnp.bfloat16
    )
    logits = jnp.dot(normed, router_weight, preferred_element_type=jnp.float32)
    chosen = expert_ids[0]
    gate_values = jax.nn.sigmoid(jnp.take_along_axis(logits, chosen, axis=1))
    flat_ids = chosen.reshape(-1)
    onehot = (flat_ids[:, None] == jnp.arange(expert_total, dtype=jnp.int32)[None, :]).astype(
        jnp.int32
    )
    earlier = jnp.cumsum(onehot, axis=0) - onehot
    slot_index = jnp.sum(earlier * onehot, axis=1)
    target = (flat_ids % per_ctx * ctx_count + flat_ids // per_ctx) * capacity + slot_index
    source_rows = jnp.repeat(normed, top_count, axis=0)
    outgoing = (
        jnp.zeros((expert_total * capacity, features), jnp.bfloat16).at[target].set(source_rows)
    )
    outgoing = outgoing.reshape(per_ctx, ctx_count, capacity, features)
    arrived = lax.all_to_all(outgoing, "ctx", split_axis=1, concat_axis=1, tiled=True)
    stacked = jnp.stack([gate_weight, up_weight, down_weight], axis=0)
    my_exp = lax.axis_index("exp")
    partner = from_partner(stacked, "exp", 0)
    upper_side = my_exp & 1 == 1
    held = jnp.where(
        upper_side,
        jnp.concatenate([partner, stacked], axis=1),
        jnp.concatenate([stacked, partner], axis=1),
    )
    half_ctx = ctx_count // 2
    halves_rows = arrived.reshape(per_ctx, 1, 2, half_ctx, capacity, features)
    spread_rows = jnp.broadcast_to(
        halves_rows, (per_ctx, quarters // 2, 2, half_ctx, capacity, features)
    )
    spread_rows = spread_rows.reshape(exp_count, half_ctx, capacity, features)
    received = lax.all_to_all(spread_rows, "exp", split_axis=0, concat_axis=0, tiled=True)
    partials = expert_rows(received, held[0], held[1], held[2])
    returned = lax.all_to_all(
        partials.astype(jnp.bfloat16), "exp", split_axis=0, concat_axis=0, tiled=True
    ).astype(partials.dtype)
    summed = jnp.sum(
        returned.reshape(per_ctx, quarters // 2, 2, half_ctx, capacity, features), axis=1
    )
    finished = summed.astype(jnp.bfloat16).reshape(per_ctx, ctx_count, capacity, features)
    came_back = lax.all_to_all(finished, "ctx", split_axis=1, concat_axis=1, tiled=True)
    flat_back = came_back.reshape(expert_total * capacity, features)
    picked = (
        jnp.take(flat_back, target, axis=0).astype(jnp.float32).reshape(tokens, top_count, features)
    )
    mixture = jnp.sum(picked * gate_values[:, :, None], axis=1).astype(jnp.bfloat16)
    return (attended, mixture[None])


def solution(mesh):
    placed = (
        P("exp", "ctx", None),
        P("exp", "ctx", None, None),
        P("exp", "ctx", None, None),
        P("exp", "ctx", None, None),
        P("exp", "ctx", None),
        P(),
        P(),
        P(("ctx", "exp"), None),
        P(("ctx", "exp"), None),
        P(("ctx", "exp"), None),
    )
    return jax.shard_map(
        local,
        mesh=mesh,
        in_specs=placed,
        out_specs=(P("exp", "ctx", None, None), P("exp", "ctx", None)),
        check_vma=False,
    )
```

profile of v0, /device:TPU:56, one launch (start us, length us, event | category | flops | bytes accessed | tf_op | source)
XLA Modules:
  0.0 309.4 jit_solution(2212090198150793443)
XLA Ops:
  12.4 1.9 scatter_custom_fusion
  16.4 13.2 %all-to-all-start = ((bf16[4,32,4,1024]{3,2,0,1:T(4,128)(2,1)}), bf16[4,32,4,1024]{3,2,0,1:T(4,128)(2,1)S(1)}, u32[]{:S(2)}, u32[]{:S(2)}) async-start(bf16[4,32,4,1024]{3,2,0,1:T(4,128)(2,1)} %copy.84), calls=%async_computation | async-start | bytes 2097152 | tf_op jit(solution)/shard_map/all_to_all | solution.py:122
  30.3 27.4 %all-to-all-done = bf16[4,32,4,1024]{3,2,0,1:T(4,128)(2,1)S(1)} async-done(((bf16[4,32,4,1024]{3,2,0,1:T(4,128)(2,1)}), bf16[4,32,4,1024]{3,2,0,1:T(4,128)(2,1)S(1)}, u32[]{:S(2)}, u32[]{:S(2)}) %all-to-all-start) | async-done | bytes 1048608 | tf_op jit(solution)/shard_map/all_to_all | solution.py:122
  58.1 2.1 broadcast_in_dim.66
  60.2 7.0 %all-to-all-start.1 = ((bf16[16,16,4,1024]{3,2,1,0:T(4,128)(2,1)}), bf16[16,16,4,1024]{3,2,1,0:T(4,128)(2,1)S(1)}, u32[]{:S(2)}, u32[]{:S(2)}) async-start(bf16[16,16,4,1024]{3,2,1,0:T(4,128)(2,1)} %bitcast.120), calls=%async_computation.1 | async-start | bytes 4194304 | tf_op jit(solution)/shard_map/all_to_all | solution.py:138
  67.3 2.2 pad_maximum_fusion
  69.4 2.0 collective-permute-start
  72.2 2.3 collective-permute-done
  74.5 3.5 %maximum_select_fusion = bf16[3,384,1024]{2,1,0:T(8,128)(2,1)} fusion(bf16[1,192,1024]{2,1,0:T(8,128)(2,1)S(1)} %bitcast.124, bf16[1,192,1024]{2,1,0:T(8,128)(2,1)S(1)} %bitcast.126, bf16[1,192,1024]{2,1,0:T(8,128)(2,1)} %bitcast.128, bf16[3,192,1024]{2,1,0:T(8,128)(2,1)} %collective-permute-done, pred[]{:T(512)S(6)} %eq.35), kind=kLoop, calls=%fused_computation.30 | loop fusion | flops 20054016 | bytes 4718593 | tf_op jit(solution)/shard_map/jit(_where)/select_n | solution.py:127
  78.0 36.8 %all-to-all-done.1 = bf16[16,16,4,1024]{3,2,1,0:T(4,128)(2,1)S(1)} async-done(((bf16[16,16,4,1024]{3,2,1,0:T(4,128)(2,1)}), bf16[16,16,4,1024]{3,2,1,0:T(4,128)(2,1)S(1)}, u32[]{:S(2)}, u32[]{:S(2)}) %all-to-all-start.1) | async-done | bytes 2097184 | tf_op jit(solution)/shard_map/all_to_all | solution.py:138
  114.8 2.0 reshape.284
  116.9 3.2 %fusion.22 = f32[1024,384]{1,0:T(8,128)S(1)} fusion(bf16[1024,1024]{1,0:T(8,128)(2,1)} %reshape.284, bf16[3,384,1024]{2,1,0:T(8,128)(2,1)} %maximum_select_fusion), kind=kOutput, calls=%fused_computation.40 | convolution fusion | flops 805306368 | bytes 4456448 | tf_op jit(solution)/shard_map/dot_general | solution.py:17
  120.1 2.3 multiply_convert_fusion
  122.4 2.4 dot_general.22
  124.7 3.7 %convolution_convert_fusion = bf16[16,16,4,1024]{3,1,2,0:T(8,128)(2,1)} fusion(bf16[3,384,1024]{2,1,0:T(8,128)(2,1)S(1)} %copy-done.2, bf16[16,16,4,384]{3,2,1,0:T(4,128)(2,1)} %dot_general.22), kind=kOutput, calls=%fused_computation.31 | convolution fusion | flops 806354944 | bytes 3670016 | tf_op jit(solution)/shard_map/dot_general | solution.py:20
  128.5 6.5 %all-to-all-start.2 = ((bf16[16,16,4,1024]{3,1,2,0:T(8,128)(2,1)}), bf16[16,16,4,1024]{3,1,2,0:T(8,128)(2,1)S(1)}, u32[]{:S(2)}, u32[]{:S(2)}) async-start(bf16[16,16,4,1024]{3,1,2,0:T(8,128)(2,1)} %convolution_convert_fusion), calls=%async_computation.2 | async-start | bytes 4194304 | tf_op jit(solution)/shard_map/all_to_all | solution.py:140
  137.0 1.9 gather_fusion.1
  139.3 43.2 %all-to-all-done.2 = bf16[16,16,4,1024]{3,1,2,0:T(8,128)(2,1)S(1)} async-done(((bf16[16,16,4,1024]{3,1,2,0:T(8,128)(2,1)}), bf16[16,16,4,1024]{3,1,2,0:T(8,128)(2,1)S(1)}, u32[]{:S(2)}, u32[]{:S(2)}) %all-to-all-start.2) | async-done | bytes 2097184 | tf_op jit(solution)/shard_map/all_to_all | solution.py:140
  182.5 1.8 reduce
  185.6 1.8 copy.88
  187.4 5.3 %all-to-all-start.3 = ((bf16[4,32,4,1024]{3,2,0,1:T(4,128)(2,1)}), bf16[4,32,4,1024]{3,2,0,1:T(4,128)(2,1)S(1)}, u32[]{:S(2)}, u32[]{:S(2)}) async-start(bf16[4,32,4,1024]{3,2,0,1:T(4,128)(2,1)} %copy.88), calls=%async_computation.3 | async-start | bytes 2097152 | tf_op jit(solution)/shard_map/all_to_all | solution.py:147
  192.8 14.3 %all-gather.5.cloned.1.call-done = bf16[1,4096,2,128]{3,1,2,0:T(8,128)(2,1)} async-done(((bf16[1,128,2,128]{3,1,2,0:T(8,128)(2,1)}), bf16[1,4096,2,128]{3,1,2,0:T(8,128)(2,1)}) %all-gather.5.cloned.1.call-update) | async-done | bytes 2097168 | tf_op jit(solution)/shard_map/all_gather | solution.py:39
  207.0 89.6 %while.15 = (s32[]{:T(128)}, f32[2,8,128]{2,1,0:T(8,128)S(1)}, f32[2,8,128]{2,1,0:T(8,128)S(1)}, f32[2,8,128,128]{3,2,1,0:T(8,128)S(1)}, s32[8]{0:T(128)S(1)}, /...) while((s32[]{:T(128)}, f32[2,8,128]{2,1,0:T(8,128)S(1)}, ...), condition=%wide.region_3.4_spmd.clone, body=%wide.region_0.3_spmd.clone.sunk | while | flops 551365248 | bytes 32904396 | solution.py:68
  208.4 3.7 %fusion.58 = (f32[2,8,128]{2,1,0:T(8,128)S(1)}, f32[2,512,128,8]{2,1,3,0:T(8,128)}) fusion(pred[128,512]{0,1:T(8,128)(4,1)S(1)} %broadcast_compare_fusion.2, bf16[128,2,8,128]{3,0,2,1:T(8,128)(2,1)S(1)} %get-tuple-element.236, bf16[8,512,2,128]{3,1,0,2:T(8,128)(2,1)} %get-tuple-element.235, s32[]{:T(128)S(6)} %copy.107), kind=kOutput, calls=%fused_computation.6.clone.1 | convolution fusion | flops 271579136 | bytes 5054468 | tf_op jit(solution)/shard_map/while/body/eval_jaxpr/qhgd,khd->hgqk/dot_general | solution.py:50
  212.1 3.3 %fusion.59 = f32[2,8,128]{2,1,0:T(8,128)S(1)} fusion(f32[2,512,128,8]{2,1,3,0:T(8,128)} %get-tuple-element.203, f32[2,8,128]{2,1,0:T(8,128)S(1)} %select_maximum_fusion.2, pred[128,512]{0,1:T(8,128)(4,1)S(1)} %broadcast_compare_fusion.2), kind=kLoop, calls=%fused_computation.8.clone.1 | loop fusion | flops 5240832 | bytes 4276224 | tf_op jit(solution)/shard_map/while/body/eval_jaxpr/reduce_sum | solution.py:59
  215.6 2.6 fusion.61
  219.6 3.7 %fusion.58 = (f32[2,8,128]{2,1,0:T(8,128)S(1)}, f32[2,512,128,8]{2,1,3,0:T(8,128)}) fusion(pred[128,512]{0,1:T(8,128)(4,1)S(1)} %broadcast_compare_fusion.2, bf16[128,2,8,128]{3,0,2,1:T(8,128)(2,1)S(1)} %get-tuple-element.236, bf16[8,512,2,128]{3,1,0,2:T(8,128)(2,1)} %get-tuple-element.235, s32[]{:T(128)S(6)} %copy.107), kind=kOutput, calls=%fused_computation.6.clone.1 | convolution fusion | flops 271579136 | bytes 5054468 | tf_op jit(solution)/shard_map/while/body/eval_jaxpr/qhgd,khd->hgqk/dot_general | solution.py:50
  223.3 3.3 %fusion.59 = f32[2,8,128]{2,1,0:T(8,128)S(1)} fusion(f32[2,512,128,8]{2,1,3,0:T(8,128)} %get-tuple-element.203, f32[2,8,128]{2,1,0:T(8,128)S(1)} %select_maximum_fusion.2, pred[128,512]{0,1:T(8,128)(4,1)S(1)} %broadcast_compare_fusion.2), kind=kLoop, calls=%fused_computation.8.clone.1 | loop fusion | flops 5240832 | bytes 4276224 | tf_op jit(solution)/shard_map/while/body/eval_jaxpr/reduce_sum | solution.py:59
  226.8 2.6 fusion.61
  230.8 3.7 %fusion.58 = (f32[2,8,128]{2,1,0:T(8,128)S(1)}, f32[2,512,128,8]{2,1,3,0:T(8,128)}) fusion(pred[128,512]{0,1:T(8,128)(4,1)S(1)} %broadcast_compare_fusion.2, bf16[128,2,8,128]{3,0,2,1:T(8,128)(2,1)S(1)} %get-tuple-element.236, bf16[8,512,2,128]{3,1,0,2:T(8,128)(2,1)} %get-tuple-element.235, s32[]{:T(128)S(6)} %copy.107), kind=kOutput, calls=%fused_computation.6.clone.1 | convolution fusion | flops 271579136 | bytes 5054468 | tf_op jit(solution)/shard_map/while/body/eval_jaxpr/qhgd,khd->hgqk/dot_general | solution.py:50
  234.5 3.3 %fusion.59 = f32[2,8,128]{2,1,0:T(8,128)S(1)} fusion(f32[2,512,128,8]{2,1,3,0:T(8,128)} %get-tuple-element.203, f32[2,8,128]{2,1,0:T(8,128)S(1)} %select_maximum_fusion.2, pred[128,512]{0,1:T(8,128)(4,1)S(1)} %broadcast_compare_fusion.2), kind=kLoop, calls=%fused_computation.8.clone.1 | loop fusion | flops 5240832 | bytes 4276224 | tf_op jit(solution)/shard_map/while/body/eval_jaxpr/reduce_sum | solution.py:59
  238.0 2.6 fusion.61
  242.0 3.7 %fusion.58 = (f32[2,8,128]{2,1,0:T(8,128)S(1)}, f32[2,512,128,8]{2,1,3,0:T(8,128)}) fusion(pred[128,512]{0,1:T(8,128)(4,1)S(1)} %broadcast_compare_fusion.2, bf16[128,2,8,128]{3,0,2,1:T(8,128)(2,1)S(1)} %get-tuple-element.236, bf16[8,512,2,128]{3,1,0,2:T(8,128)(2,1)} %get-tuple-element.235, s32[]{:T(128)S(6)} %copy.107), kind=kOutput, calls=%fused_computation.6.clone.1 | convolution fusion | flops 271579136 | bytes 5054468 | tf_op jit(solution)/shard_map/while/body/eval_jaxpr/qhgd,khd->hgqk/dot_general | solution.py:50
  245.7 3.3 %fusion.59 = f32[2,8,128]{2,1,0:T(8,128)S(1)} fusion(f32[2,512,128,8]{2,1,3,0:T(8,128)} %get-tuple-element.203, f32[2,8,128]{2,1,0:T(8,128)S(1)} %select_maximum_fusion.2, pred[128,512]{0,1:T(8,128)(4,1)S(1)} %broadcast_compare_fusion.2), kind=kLoop, calls=%fused_computation.8.clone.1 | loop fusion | flops 5240832 | bytes 4276224 | tf_op jit(solution)/shard_map/while/body/eval_jaxpr/reduce_sum | solution.py:59
  249.2 2.6 fusion.61
  253.2 3.7 %fusion.58 = (f32[2,8,128]{2,1,0:T(8,128)S(1)}, f32[2,512,128,8]{2,1,3,0:T(8,128)}) fusion(pred[128,512]{0,1:T(8,128)(4,1)S(1)} %broadcast_compare_fusion.2, bf16[128,2,8,128]{3,0,2,1:T(8,128)(2,1)S(1)} %get-tuple-element.236, bf16[8,512,2,128]{3,1,0,2:T(8,128)(2,1)} %get-tuple-element.235, s32[]{:T(128)S(6)} %copy.107), kind=kOutput, calls=%fused_computation.6.clone.1 | convolution fusion | flops 271579136 | bytes 5054468 | tf_op jit(solution)/shard_map/while/body/eval_jaxpr/qhgd,khd->hgqk/dot_general | solution.py:50
  256.9 3.3 %fusion.59 = f32[2,8,128]{2,1,0:T(8,128)S(1)} fusion(f32[2,512,128,8]{2,1,3,0:T(8,128)} %get-tuple-element.203, f32[2,8,128]{2,1,0:T(8,128)S(1)} %select_maximum_fusion.2, pred[128,512]{0,1:T(8,128)(4,1)S(1)} %broadcast_compare_fusion.2), kind=kLoop, calls=%fused_computation.8.clone.1 | loop fusion | flops 5240832 | bytes 4276224 | tf_op jit(solution)/shard_map/while/body/eval_jaxpr/reduce_sum | solution.py:59
  260.4 2.6 fusion.61
  264.4 3.7 %fusion.58 = (f32[2,8,128]{2,1,0:T(8,128)S(1)}, f32[2,512,128,8]{2,1,3,0:T(8,128)}) fusion(pred[128,512]{0,1:T(8,128)(4,1)S(1)} %broadcast_compare_fusion.2, bf16[128,2,8,128]{3,0,2,1:T(8,128)(2,1)S(1)} %get-tuple-element.236, bf16[8,512,2,128]{3,1,0,2:T(8,128)(2,1)} %get-tuple-element.235, s32[]{:T(128)S(6)} %copy.107), kind=kOutput, calls=%fused_computation.6.clone.1 | convolution fusion | flops 271579136 | bytes 5054468 | tf_op jit(solution)/shard_map/while/body/eval_jaxpr/qhgd,khd->hgqk/dot_general | solution.py:50
  268.1 3.3 %fusion.59 = f32[2,8,128]{2,1,0:T(8,128)S(1)} fusion(f32[2,512,128,8]{2,1,3,0:T(8,128)} %get-tuple-element.203, f32[2,8,128]{2,1,0:T(8,128)S(1)} %select_maximum_fusion.2, pred[128,512]{0,1:T(8,128)(4,1)S(1)} %broadcast_compare_fusion.2), kind=kLoop, calls=%fused_computation.8.clone.1 | loop fusion | flops 5240832 | bytes 4276224 | tf_op jit(solution)/shard_map/while/body/eval_jaxpr/reduce_sum | solution.py:59
  271.6 2.6 fusion.61
  275.6 3.7 %fusion.58 = (f32[2,8,128]{2,1,0:T(8,128)S(1)}, f32[2,512,128,8]{2,1,3,0:T(8,128)}) fusion(pred[128,512]{0,1:T(8,128)(4,1)S(1)} %broadcast_compare_fusion.2, bf16[128,2,8,128]{3,0,2,1:T(8,128)(2,1)S(1)} %get-tuple-element.236, bf16[8,512,2,128]{3,1,0,2:T(8,128)(2,1)} %get-tuple-element.235, s32[]{:T(128)S(6)} %copy.107), kind=kOutput, calls=%fused_computation.6.clone.1 | convolution fusion | flops 271579136 | bytes 5054468 | tf_op jit(solution)/shard_map/while/body/eval_jaxpr/qhgd,khd->hgqk/dot_general | solution.py:50
  279.3 3.3 %fusion.59 = f32[2,8,128]{2,1,0:T(8,128)S(1)} fusion(f32[2,512,128,8]{2,1,3,0:T(8,128)} %get-tuple-element.203, f32[2,8,128]{2,1,0:T(8,128)S(1)} %select_maximum_fusion.2, pred[128,512]{0,1:T(8,128)(4,1)S(1)} %broadcast_compare_fusion.2), kind=kLoop, calls=%fused_computation.8.clone.1 | loop fusion | flops 5240832 | bytes 4276224 | tf_op jit(solution)/shard_map/while/body/eval_jaxpr/reduce_sum | solution.py:59
  282.8 2.6 fusion.61
  286.8 3.7 %fusion.58 = (f32[2,8,128]{2,1,0:T(8,128)S(1)}, f32[2,512,128,8]{2,1,3,0:T(8,128)}) fusion(pred[128,512]{0,1:T(8,128)(4,1)S(1)} %broadcast_compare_fusion.2, bf16[128,2,8,128]{3,0,2,1:T(8,128)(2,1)S(1)} %get-tuple-element.236, bf16[8,512,2,128]{3,1,0,2:T(8,128)(2,1)} %get-tuple-element.235, s32[]{:T(128)S(6)} %copy.107), kind=kOutput, calls=%fused_computation.6.clone.1 | convolution fusion | flops 271579136 | bytes 5054468 | tf_op jit(solution)/shard_map/while/body/eval_jaxpr/qhgd,khd->hgqk/dot_general | solution.py:50
  290.5 3.3 %fusion.59 = f32[2,8,128]{2,1,0:T(8,128)S(1)} fusion(f32[2,512,128,8]{2,1,3,0:T(8,128)} %get-tuple-element.203, f32[2,8,128]{2,1,0:T(8,128)S(1)} %select_maximum_fusion.2, pred[128,512]{0,1:T(8,128)(4,1)S(1)} %broadcast_compare_fusion.2), kind=kLoop, calls=%fused_computation.8.clone.1 | loop fusion | flops 5240832 | bytes 4276224 | tf_op jit(solution)/shard_map/while/body/eval_jaxpr/reduce_sum | solution.py:59
  294.0 2.6 fusion.61
  300.2 2.3 multiply_reduce_fusion
  (146 shorter events, 23.0 us)
Async XLA Ops:
  7.2 129.6 %copy-start = (bf16[1024,128]{1,0:T(8,128)(2,1)S(1)}, bf16[1024,128]{1,0:T(8,128)(2,1)}, u32[]{:S(2)}) copy-start(bf16[1024,128]{1,0:T(8,128)(2,1)} %param.18) | copy-start | bytes 786436
  14.8 14.8 %copy-start.7 = (bf16[1,128,2,128]{3,2,1,0:T(2,128)(2,1)S(1)}, bf16[1,128,2,128]{3,2,1,0:T(2,128)(2,1)}, u32[]{:S(2)}) copy-start(bf16[1,128,2,128]{3,2,1,0:T(2,128)(2,1)} %param.14) | copy-start | bytes 196612
  16.4 41.3 %all-to-all-start = ((bf16[4,32,4,1024]{3,2,0,1:T(4,128)(2,1)}), bf16[4,32,4,1024]{3,2,0,1:T(4,128)(2,1)S(1)}, u32[]{:S(2)}, u32[]{:S(2)}) async-start(bf16[4,32,4,1024]{3,2,0,1:T(4,128)(2,1)} %copy.84), calls=%async_computation | async-start | bytes 2097152 | tf_op jit(solution)/shard_map/all_to_all | solution.py:122
  29.5 163.2 %all-gather.3.cloned.1.call-start = ((), (), s32[]{:S(2)}) async-start(), calls=%async_computation.4 | async-start | bytes 2162688 | tf_op jit(solution)/shard_map/all_gather | solution.py:38
  60.2 7.1 %copy-start.4 = (bf16[192,1024]{1,0:T(8,128)(2,1)S(1)}, bf16[192,1024]{1,0:T(8,128)(2,1)}, u32[]{:S(2)}) copy-start(bf16[192,1024]{1,0:T(8,128)(2,1)} %param.21) | copy-start | bytes 1179652
  60.2 7.1 %copy-start.5 = (bf16[192,1024]{1,0:T(8,128)(2,1)S(1)}, bf16[192,1024]{1,0:T(8,128)(2,1)}, u32[]{:S(2)}) copy-start(bf16[192,1024]{1,0:T(8,128)(2,1)} %param.20) | copy-start | bytes 1179652
  60.2 11.3 %copy-start.8 = (bf16[1,128,2,128]{3,2,1,0:T(2,128)(2,1)S(1)}, bf16[1,128,2,128]{3,2,1,0:T(2,128)(2,1)}, u32[]{:S(2)}) copy-start(bf16[1,128,2,128]{3,2,1,0:T(2,128)(2,1)} %param.15) | copy-start | bytes 196612
  60.2 54.6 %all-to-all-start.1 = ((bf16[16,16,4,1024]{3,2,1,0:T(4,128)(2,1)}), bf16[16,16,4,1024]{3,2,1,0:T(4,128)(2,1)S(1)}, u32[]{:S(2)}, u32[]{:S(2)}) async-start(bf16[16,16,4,1024]{3,2,1,0:T(4,128)(2,1)} %bitcast.120), calls=%async_computation.1 | async-start | bytes 4194304 | tf_op jit(solution)/shard_map/all_to_all | solution.py:138
  67.2 139.8 %all-gather.5.cloned.1.call-start = ((), (), s32[]{:S(2)}) async-start(), calls=%async_computation.5 | async-start | bytes 2162688 | tf_op jit(solution)/shard_map/all_gather | solution.py:39
  69.4 5.1 %collective-permute-start = (bf16[3,192,1024]{2,1,0:T(8,128)(2,1)}, bf16[3,192,1024]{2,1,0:T(8,128)(2,1)}, u32[]{:S(2)}, u32[]{:S(2)}) collective-permute-start(bf16[3,192,1024]{2,1,0:T(8,128)(2,1)} %pad_maximum_fusion), channel_id=1, source_target_pairs={{0,1},{1,0},{2,3},{3,2},{4,5},{5,4},{6,7},{7,6},{8,9},{9,8},{10,11... | collective-permute-start | bytes 3538952 | tf_op jit(solution)/shard_map/ppermute | solution.py:10
  116.9 3.2 %copy-start.2 = (bf16[3,384,1024]{2,1,0:T(8,128)(2,1)S(1)}, bf16[3,384,1024]{2,1,0:T(8,128)(2,1)}, u32[]{:S(2)}) copy-start(bf16[3,384,1024]{2,1,0:T(8,128)(2,1)} %maximum_select_fusion) | copy-start | bytes 7077892
  116.9 3.2 %copy-start.3 = (bf16[1024,1024]{1,0:T(8,128)(2,1)S(1)}, bf16[1024,1024]{1,0:T(8,128)(2,1)}, u32[]{:S(2)}) copy-start(bf16[1024,1024]{1,0:T(8,128)(2,1)} %reshape.284) | copy-start | bytes 6291460
  128.4 7.9 %copy-start.9 = (s32[1,128,2]{1,2,0:T(2,128)S(1)}, s32[1,128,2]{1,2,0:T(2,128)}, u32[]{:S(2)}) copy-start(s32[1,128,2]{1,2,0:T(2,128)} %param.16) | copy-start | bytes 3076
  128.5 54.1 %all-to-all-start.2 = ((bf16[16,16,4,1024]{3,1,2,0:T(8,128)(2,1)}), bf16[16,16,4,1024]{3,1,2,0:T(8,128)(2,1)S(1)}, u32[]{:S(2)}, u32[]{:S(2)}) async-start(bf16[16,16,4,1024]{3,1,2,0:T(8,128)(2,1)} %convolution_convert_fusion), calls=%async_computation.2 | async-start | bytes 4194304 | tf_op jit(solution)/shard_map/all_to_all | solution.py:140
  185.6 21.4 %copy-start.6 = (f32[2,8,128,128]{3,2,1,0:T(8,128)S(1)}, f32[2,8,128,128]{3,2,1,0:T(8,128)}, u32[]{:S(2)}) copy-start(f32[2,8,128,128]{3,2,1,0:T(8,128)} %custom-call.4) | copy-start | bytes 3145732
  187.4 110.7 %all-to-all-start.3 = ((bf16[4,32,4,1024]{3,2,0,1:T(4,128)(2,1)}), bf16[4,32,4,1024]{3,2,0,1:T(4,128)(2,1)S(1)}, u32[]{:S(2)}, u32[]{:S(2)}) async-start(bf16[4,32,4,1024]{3,2,0,1:T(4,128)(2,1)} %copy.88), calls=%async_computation.3 | async-start | bytes 2097152 | tf_op jit(solution)/shard_map/all_to_all | solution.py:147
  212.1 3.4 %copy-start.1 = (f32[2,512,128,8]{2,1,3,0:T(8,128)S(1)}, f32[2,512,128,8]{2,1,3,0:T(8,128)}, u32[]{:S(2)}) copy-start(f32[2,512,128,8]{2,1,3,0:T(8,128)} %get-tuple-element.203) | copy-start | bytes 12582916 | tf_op jit(solution)/shard_map/while
  223.3 3.4 %copy-start.1 = (f32[2,512,128,8]{2,1,3,0:T(8,128)S(1)}, f32[2,512,128,8]{2,1,3,0:T(8,128)}, u32[]{:S(2)}) copy-start(f32[2,512,128,8]{2,1,3,0:T(8,128)} %get-tuple-element.203) | copy-start | bytes 12582916 | tf_op jit(solution)/shard_map/while
  234.5 3.4 %copy-start.1 = (f32[2,512,128,8]{2,1,3,0:T(8,128)S(1)}, f32[2,512,128,8]{2,1,3,0:T(8,128)}, u32[]{:S(2)}) copy-start(f32[2,512,128,8]{2,1,3,0:T(8,128)} %get-tuple-element.203) | copy-start | bytes 12582916 | tf_op jit(solution)/shard_map/while
  245.7 3.4 %copy-start.1 = (f32[2,512,128,8]{2,1,3,0:T(8,128)S(1)}, f32[2,512,128,8]{2,1,3,0:T(8,128)}, u32[]{:S(2)}) copy-start(f32[2,512,128,8]{2,1,3,0:T(8,128)} %get-tuple-element.203) | copy-start | bytes 12582916 | tf_op jit(solution)/shard_map/while
  256.9 3.4 %copy-start.1 = (f32[2,512,128,8]{2,1,3,0:T(8,128)S(1)}, f32[2,512,128,8]{2,1,3,0:T(8,128)}, u32[]{:S(2)}) copy-start(f32[2,512,128,8]{2,1,3,0:T(8,128)} %get-tuple-element.203) | copy-start | bytes 12582916 | tf_op jit(solution)/shard_map/while
  268.1 3.4 %copy-start.1 = (f32[2,512,128,8]{2,1,3,0:T(8,128)S(1)}, f32[2,512,128,8]{2,1,3,0:T(8,128)}, u32[]{:S(2)}) copy-start(f32[2,512,128,8]{2,1,3,0:T(8,128)} %get-tuple-element.203) | copy-start | bytes 12582916 | tf_op jit(solution)/shard_map/while
  279.3 3.4 %copy-start.1 = (f32[2,512,128,8]{2,1,3,0:T(8,128)S(1)}, f32[2,512,128,8]{2,1,3,0:T(8,128)}, u32[]{:S(2)}) copy-start(f32[2,512,128,8]{2,1,3,0:T(8,128)} %get-tuple-element.203) | copy-start | bytes 12582916 | tf_op jit(solution)/shard_map/while
  290.5 3.4 %copy-start.1 = (f32[2,512,128,8]{2,1,3,0:T(8,128)S(1)}, f32[2,512,128,8]{2,1,3,0:T(8,128)}, u32[]{:S(2)}) copy-start(f32[2,512,128,8]{2,1,3,0:T(8,128)} %get-tuple-element.203) | copy-start | bytes 12582916 | tf_op jit(solution)/shard_map/while
Sparse Core Ops, SparseCore 0:
  34.1 84.5 all-gather.2
  122.4 84.5 all-gather.4
where the time goes:
time: 311 us; the launch traced here: 309 us
  waiting for transfers between devices  124 us (40%)
  matrix products  60 us (19%)
  other arithmetic  41.4 us (13%)
  starting transfers between devices  34.1 us (11%)
  local copies, waits for them, and re-layouts  29.7 us (10%)
  between operations  14.4 us (5%)
  loops' own time  5.69 us (2%)
    all_to_all x1, waiting for transfers between devices, local(): lax.all_to_all(partials.astype(jnp.bfloat16), 'exp', split_axis=0, concat...  43.2 us
    all_to_all x1, waiting for transfers between devices, local(): lax.all_to_all(spread_rows, 'exp', split_axis=0, concat_axis=0, tiled=True)  36.8 us
    dot_general x8, matrix products, advance(): jnp.einsum('qhgd,khd->hgqk', grouped, key_block, preferred_element_type=j...  29.5 us
    all_to_all x1, waiting for transfers between devices, local(): lax.all_to_all(outgoing, 'ctx', split_axis=1, concat_axis=1, tiled=True)  27.4 us
    reduce_sum x8, other arithmetic, advance(): totals = totals * factor + jnp.sum(weights, axis=-1)  26.6 us
    dot_general x8, matrix products, advance(): jnp.einsum('hgqk,khd->hgqd', weights.astype(jnp.bfloat16), value_block, p...  21.1 us
    all_gather x1, waiting for transfers between devices, attention(): value_piece = lax.all_gather(value_rows, 'ctx', axis=1, tiled=True)  14.3 us
    all_to_all x1, starting transfers between devices, local(): lax.all_to_all(outgoing, 'ctx', split_axis=1, concat_axis=1, tiled=True)  13.2 us
  transfers between devices with their start and end apart: 7, of which 5 were waited for; matrix products, arithmetic and copies ran while one was open for 38% of the time, Pallas kernels for 0%

commit v1 on v0

v1 whole, which is shorter than its diff:
```python
import functools
import math

import jax
import jax.numpy as jnp
from jax import lax
from jax.experimental import pallas as pl
from jax.experimental.pallas import tpu as pltpu
from jax.sharding import PartitionSpec as P


def from_partner(value, axis, flip):
    return lax.ppermute(value, axis, [(i, i ^ flip) for i in range(lax.axis_size(axis))])


def expert_rows(flat_rows, gate_rows, up_rows, down_rows):
    contract = (((1,), (1,)), ((), ()))
    gate_part = lax.dot_general(flat_rows, gate_rows, contract, preferred_element_type=jnp.float32)
    up_part = lax.dot_general(flat_rows, up_rows, contract, preferred_element_type=jnp.float32)
    hidden = (jax.nn.silu(gate_part) * up_part).astype(jnp.bfloat16)
    return jnp.dot(hidden, down_rows, preferred_element_type=jnp.float32)


def _flash_kernel(block, group, scaling, c_ref, q_ref, k_ref, v_ref, o_ref, m_sc, l_sc, acc_sc):
    c = c_ref[0]
    q = q_ref[0]
    rows = q.shape[0]
    m_sc[...] = jnp.full(m_sc.shape, -1e30, jnp.float32)
    l_sc[...] = jnp.zeros(l_sc.shape, jnp.float32)
    acc_sc[...] = jnp.zeros(acc_sc.shape, jnp.float32)

    def update(j, masked):
        start = pl.multiple_of(j * block, block)
        k = k_ref[0, pl.ds(start, block), :]
        v = v_ref[0, pl.ds(start, block), :]
        s = lax.dot_general(q, k, (((1,), (1,)), ((), ())), preferred_element_type=jnp.float32)
        s = s * scaling
        if masked:
            qpos = lax.broadcasted_iota(jnp.int32, (rows, block), 0) // group
            kpos = lax.broadcasted_iota(jnp.int32, (rows, block), 1)
            s = jnp.where(kpos <= qpos, s, -1e30)
        m_prev = m_sc[...]
        m_new = jnp.maximum(m_prev, jnp.max(s, axis=1, keepdims=True))
        alpha = jnp.exp(m_prev - m_new)
        p = jnp.exp(s - m_new)
        l_sc[...] = alpha * l_sc[...] + jnp.sum(p, axis=1, keepdims=True)
        acc_sc[...] = alpha * acc_sc[...] + jnp.dot(
            p.astype(jnp.bfloat16), v, preferred_element_type=jnp.float32
        )
        m_sc[...] = m_new

    def body(j, carry):
        update(j, False)
        return carry

    lax.fori_loop(0, c, body, 0)
    update(c, True)
    o_ref[0] = (acc_sc[...] / l_sc[...]).astype(o_ref.dtype)


def attention(queries, key_rows, value_rows):
    seq_rows = queries.shape[1]
    head_count = queries.shape[2]
    head_size = queries.shape[3]
    kv_count = key_rows.shape[2]
    group_size = head_count // kv_count
    scaling = 1.0 / math.sqrt(head_size)
    grouped = (
        queries[0]
        .reshape(seq_rows, kv_count, group_size, head_size)
        .transpose(1, 0, 2, 3)
        .reshape(kv_count, seq_rows * group_size, head_size)
    )
    keys_local = key_rows[0].transpose(1, 0, 2)
    values_local = value_rows[0].transpose(1, 0, 2)
    keys_all = lax.all_gather(keys_local, "ctx", axis=1, tiled=True)
    values_all = lax.all_gather(values_local, "ctx", axis=1, tiled=True)
    total_rows = keys_all.shape[1]
    q_rows = seq_rows * group_size
    me = lax.axis_index("ctx").astype(jnp.int32).reshape(1)
    ctx_count = lax.axis_size("ctx")
    flops = 4 * kv_count * q_rows * total_rows * head_size // 2
    out = pl.pallas_call(
        functools.partial(_flash_kernel, seq_rows, group_size, scaling),
        grid_spec=pltpu.PrefetchScalarGridSpec(
            num_scalar_prefetch=1,
            grid=(kv_count,),
            in_specs=[
                pl.BlockSpec((1, q_rows, head_size), lambda g, c: (g, 0, 0)),
                pl.BlockSpec((1, total_rows, head_size), lambda g, c: (g, 0, 0)),
                pl.BlockSpec((1, total_rows, head_size), lambda g, c: (g, 0, 0)),
            ],
            out_specs=pl.BlockSpec((1, q_rows, head_size), lambda g, c: (g, 0, 0)),
            scratch_shapes=[
                pltpu.VMEM((q_rows, 1), jnp.float32),
                pltpu.VMEM((q_rows, 1), jnp.float32),
                pltpu.VMEM((q_rows, head_size), jnp.float32),
            ],
        ),
        out_shape=jax.ShapeDtypeStruct((kv_count, q_rows, head_size), jnp.bfloat16),
        cost_estimate=pl.CostEstimate(
            flops=flops,
            transcendentals=kv_count * q_rows * total_rows // 2,
            bytes_accessed=4 * kv_count * total_rows * head_size + 4 * kv_count * q_rows * head_size,
        ),
    )(me, grouped, keys_all, values_all)
    del ctx_count
    return (
        out.reshape(kv_count, seq_rows, group_size, head_size)
        .transpose(1, 0, 2, 3)
        .reshape(1, seq_rows, head_count, head_size)
    )


def local(
    stream,
    queries,
    key_rows,
    value_rows,
    expert_ids,
    norm_gain,
    router_weight,
    gate_weight,
    up_weight,
    down_weight,
):
    ctx_count = lax.axis_size("ctx")
    exp_count = lax.axis_size("exp")
    tokens = stream.shape[1]
    features = stream.shape[2]
    top_count = expert_ids.shape[2]
    expert_total = router_weight.shape[1]
    per_ctx = expert_total // ctx_count
    quarters = exp_count // per_ctx
    capacity = 2 * tokens * top_count // expert_total

    stacked = jnp.stack([gate_weight, up_weight, down_weight], axis=0)
    across = from_partner(stacked, "exp", 2)
    pair = jnp.concatenate([stacked, across], axis=1)
    beside = from_partner(pair, "exp", 1)
    held = jnp.concatenate([pair, beside], axis=1)

    attended = attention(queries, key_rows, value_rows)

    widened = stream[0].astype(jnp.float32)
    mean_square = jnp.mean(widened * widened, axis=-1, keepdims=True)
    normed = (widened * lax.rsqrt(mean_square + 1e-06) * norm_gain.astype(jnp.float32)).astype(
        jnp.bfloat16
    )
    logits = jnp.dot(normed, router_weight, preferred_element_type=jnp.float32)
    chosen = expert_ids[0]
    gate_values = jax.nn.sigmoid(jnp.take_along_axis(logits, chosen, axis=1))
    flat_ids = chosen.reshape(-1)
    onehot = (flat_ids[:, None] == jnp.arange(expert_total, dtype=jnp.int32)[None, :]).astype(
        jnp.int32
    )
    earlier = jnp.cumsum(onehot, axis=0) - onehot
    slot_index = jnp.sum(earlier * onehot, axis=1)
    target = (flat_ids % per_ctx * ctx_count + flat_ids // per_ctx) * capacity + slot_index
    source_rows = jnp.repeat(normed, top_count, axis=0)
    outgoing = (
        jnp.zeros((expert_total * capacity, features), jnp.bfloat16).at[target].set(source_rows)
    )
    outgoing = outgoing.reshape(per_ctx, ctx_count, capacity, features)
    arrived = lax.all_to_all(outgoing, "ctx", split_axis=1, concat_axis=1, tiled=True)
    share = ctx_count // quarters
    to_holders = arrived.reshape(exp_count, share, capacity, features)
    received = lax.all_to_all(to_holders, "exp", split_axis=0, concat_axis=0, tiled=True)
    computed = expert_rows(received.reshape(-1, features), held[0], held[1], held[2])
    computed = computed.astype(jnp.bfloat16).reshape(exp_count, share, capacity, features)
    returned = lax.all_to_all(computed, "exp", split_axis=0, concat_axis=0, tiled=True)
    finished = returned.reshape(per_ctx, ctx_count, capacity, features)
    came_back = lax.all_to_all(finished, "ctx", split_axis=1, concat_axis=1, tiled=True)
    flat_back = came_back.reshape(expert_total * capacity, features)
    picked = (
        jnp.take(flat_back, target, axis=0).astype(jnp.float32).reshape(tokens, top_count, features)
    )
    mixture = jnp.sum(picked * gate_values[:, :, None], axis=1).astype(jnp.bfloat16)
    return (attended, mixture[None])


def solution(mesh):
    placed = (
        P("exp", "ctx", None),
        P("exp", "ctx", None, None),
        P("exp", "ctx", None, None),
        P("exp", "ctx", None, None),
        P("exp", "ctx", None),
        P(),
        P(),
        P(("ctx", "exp"), None),
        P(("ctx", "exp"), None),
        P(("ctx", "exp"), None),
    )
    return jax.shard_map(
        local,
        mesh=mesh,
        in_specs=placed,
        out_specs=(P("exp", "ctx", None, None), P("exp", "ctx", None)),
        check_vma=False,
    )
```

time: 311 us -> 304 us (0.977)
  the two profiles are of different devices: /device:TPU:56 before, /device:TPU:454 now
where the time goes in v1:
time: 304 us; the launch traced here: 303 us
  Pallas kernels  103 us (34%)
  waiting for transfers between devices  80.3 us (26%)
  blocking collectives  31.9 us (10%)
  starting transfers between devices  28.2 us (9%)
  local copies, waits for them, and re-layouts  24.1 us (8%)
  between operations  14.4 us (5%)
  other arithmetic  12 us (4%)
  matrix products  9.51 us (3%)
    pallas_call x1, Pallas kernels, attention(): pl.pallas_call(functools.partial(_flash_kernel, seq_rows, group_size, sca...  103 us
    all_gather x1, waiting for transfers between devices, attention(): values_all = lax.all_gather(values_local, 'ctx', axis=1, tiled=True)  37.4 us
    all_to_all x1, blocking collectives, local(): lax.all_to_all(computed, 'exp', split_axis=0, concat_axis=0, tiled=True)  31.9 us
    all_to_all x1, waiting for transfers between devices, local(): lax.all_to_all(to_holders, 'exp', split_axis=0, concat_axis=0, tiled=True)  21.4 us
    all_to_all x1, waiting for transfers between devices, local(): lax.all_to_all(outgoing, 'ctx', split_axis=1, concat_axis=1, tiled=True)  11.7 us
    ppermute x2, waiting for transfers between devices, from_partner(): lax.ppermute(value, axis, [(i, i ^ flip) for i in range(lax.axis_size(axi...  9.85 us
    all_to_all x1, starting transfers between devices, local(): lax.all_to_all(finished, 'ctx', split_axis=1, concat_axis=1, tiled=True)  9.65 us
    all_to_all x1, starting transfers between devices, local(): lax.all_to_all(outgoing, 'ctx', split_axis=1, concat_axis=1, tiled=True)  7.13 us
  transfers between devices with their start and end apart: 7, of which 4 were waited for; matrix products, arithmetic and copies ran while one was open for 13% of the time, Pallas kernels for 34%

profile of v1, /device:TPU:454, one launch (start us, length us, event | category | flops | bytes accessed | tf_op | source)
XLA Modules:
  0.0 303.1 jit_solution(5870405702343586501)
XLA Ops:
  7.3 2.5 pad_maximum_fusion.2
  9.7 3.5 %collective-permute-start = (bf16[3,192,1024]{2,1,0:T(8,128)(2,1)}, bf16[3,192,1024]{2,1,0:T(8,128)(2,1)S(1)}, u32[]{:S(2)}, u32[]{:S(2)}) collective-permute-start(bf16[3,192,1024]{2,1,0:T(8,128)(2,1)} %pad_maximum_fusion.2), channel_id=1, source_target_pairs={{0,2},{1,3},{2,0},{3,1},{4,6},{5,7},{6,4},{7,5},{8,10},{9,11},{10,... | collective-permute-start | bytes 3538952 | tf_op jit(solution)/shard_map/ppermute | solution.py:13
  13.2 0.6 copy.120
  14.0 0.1 eq.28
  14.2 0.2 fusion.10
  14.7 0.1 reshape_squeeze.12
  14.8 0.1 reshape_squeeze.13
  15.2 0.7 copy-done.3
  15.8 0.3 broadcast_in_dim.28
  16.1 0.2 reshape.292
  16.3 0.2 fusion.12
  16.5 1.9 scatter_custom_fusion
  18.5 1.2 reshape.267
  19.7 2.8 copy.104
  22.5 7.1 %all-to-all-start = ((bf16[4,32,4,1024]{3,2,0,1:T(4,128)(2,1)}), bf16[4,32,4,1024]{3,2,0,1:T(4,128)(2,1)S(1)}, u32[]{:S(2)}, u32[]{:S(2)}) async-start(bf16[4,32,4,1024]{3,2,0,1:T(4,128)(2,1)} %copy.104), calls=%async_computation | async-start | bytes 2097152 | tf_op jit(solution)/shard_map/all_to_all | solution.py:165
  29.7 9.8 %collective-permute-done = bf16[3,192,1024]{2,1,0:T(8,128)(2,1)S(1)} collective-permute-done((bf16[3,192,1024]{2,1,0:T(8,128)(2,1)}, bf16[3,192,1024]{2,1,0:T(8,128)(2,1)S(1)}, u32[]{:S(2)}, u32[]{:S(2)}) %collective-permute-start) | collective-permute-done | bytes 1179680 | tf_op jit(solution)/shard_map/ppermute | solution.py:13
  39.5 2.7 pad_maximum_fusion.1
  42.2 1.9 collective-permute-start.1
  44.1 11.7 %all-to-all-done = bf16[4,32,4,1024]{3,2,0,1:T(4,128)(2,1)S(1)} async-done(((bf16[4,32,4,1024]{3,2,0,1:T(4,128)(2,1)}), bf16[4,32,4,1024]{3,2,0,1:T(4,128)(2,1)S(1)}, u32[]{:S(2)}, u32[]{:S(2)}) %all-to-all-start) | async-done | bytes 1048608 | tf_op jit(solution)/shard_map/all_to_all | solution.py:165
  55.8 0.6 copy.105
  56.4 1.1 copy.106
  57.4 6.0 %all-to-all-start.1 = ((bf16[16,8,4,1024]{3,1,2,0:T(8,128)(2,1)}), bf16[16,8,4,1024]{3,1,2,0:T(8,128)(2,1)S(1)}, u32[]{:S(2)}, u32[]{:S(2)}) async-start(bf16[16,8,4,1024]{3,1,2,0:T(8,128)(2,1)} %copy.106), calls=%async_computation.1 | async-start | bytes 2097152 | tf_op jit(solution)/shard_map/all_to_all | solution.py:168
  63.5 1.5 copy.119
  65.0 3.7 %pad_maximum_fusion = bf16[3,768,1024]{2,1,0:T(8,128)(2,1)} fusion(bf16[3,384,1024]{2,1,0:T(8,128)(2,1)} %collective-permute-done.1, bf16[3,192,1024]{2,1,0:T(8,128)(2,1)S(1)} %collective-permute-done, bf16[1,192,1024]{2,1,0:T(8,128)(2,1)S(1)} %bitcast.92, bf16[1,192,1024]{2,1,0:T(8,128)(2,1)S(1)} %bitcast.95, bf16[1,192,1024]{2,1,0:T(8,128)(2,1)} %bitcast.98), kind=kLoop, calls=%fused_computation.3 | loop fusion | flops 23592960 | bytes 9437184 | tf_op jit(solution)/shard_map/concatenate | solution.py:141
  68.8 21.4 %all-to-all-done.1 = bf16[16,8,4,1024]{3,1,2,0:T(8,128)(2,1)S(1)} async-done(((bf16[16,8,4,1024]{3,1,2,0:T(8,128)(2,1)}), bf16[16,8,4,1024]{3,1,2,0:T(8,128)(2,1)S(1)}, u32[]{:S(2)}, u32[]{:S(2)}) %all-to-all-start.1) | async-done | bytes 1048608 | tf_op jit(solution)/shard_map/all_to_all | solution.py:168
  90.1 0.9 copy.107
  91.0 0.3 reshape.269
  91.3 3.6 %fusion.1 = f32[512,768]{1,0:T(8,128)} fusion(bf16[512,1024]{1,0:T(8,128)(2,1)S(1)} %reshape.269, bf16[3,768,1024]{2,1,0:T(8,128)(2,1)} %pad_maximum_fusion), kind=kOutput, calls=%fused_computation.8 | convolution fusion | flops 805306368 | bytes 4194304 | tf_op jit(solution)/shard_map/dot_general | solution.py:19
  94.9 5.7 %fusion.3 = bf16[512,1024]{1,0:T(8,128)(2,1)} fusion(bf16[3,768,1024]{2,1,0:T(8,128)(2,1)} %pad_maximum_fusion, f32[512,768]{1,0:T(8,128)} %fusion.1, bf16[512,1024]{1,0:T(8,128)(2,1)S(1)} %reshape.269), kind=kOutput, calls=%fused_computation.12 | convolution fusion | flops 1613496320 | bytes 6815744 | tf_op jit(solution)/shard_map/dot_general | solution.py:21
  100.6 1.5 reshape.270
  102.1 0.4 copy.108
  102.4 31.9 %all_to_all.20 = bf16[16,8,4,1024]{3,1,2,0:T(8,128)(2,1)S(1)} all-to-all(bf16[16,8,4,1024]{3,1,2,0:T(8,128)(2,1)S(1)} %copy.108), channel_id=1, replica_groups=mesh['ctx'=32,'exp'=16] {'exp'}, dimensions={0} | all-to-all | bytes 2097152 | tf_op jit(solution)/shard_map/all_to_all | solution.py:171
  134.4 1.8 copy.110
  136.2 9.7 %all-to-all-start.3 = ((bf16[4,32,4,1024]{3,2,0,1:T(4,128)(2,1)}), bf16[4,32,4,1024]{3,2,0,1:T(4,128)(2,1)S(1)}, u32[]{:S(2)}, u32[]{:S(2)}) async-start(bf16[4,32,4,1024]{3,2,0,1:T(4,128)(2,1)} %copy.110), calls=%async_computation.3 | async-start | bytes 2097152 | tf_op jit(solution)/shard_map/all_to_all | solution.py:173
  145.8 0.1 reduce_sum.32
  146.1 0.1 copy.102
  146.4 0.1 reshape.282
  146.5 0.2 fusion.23
  146.7 1.9 gather_fusion.1
  149.0 0.8 copy_bitcast_fusion.1.q_ref
  149.9 37.4 %all-gather.5.cloned.1.call-done.v_ref = bf16[2,4096,128]{2,1,0:T(8,128)(2,1)} async-done(((bf16[2,128,128]{2,1,0:T(8,128)(2,1)}), bf16[2,4096,128]{2,1,0:T(8,128)(2,1)}) %all-gather.5.cloned.1.call-update) | async-done | bytes 2097168 | tf_op jit(solution)/shard_map/all_gather | solution.py:77
  187.2 102.6 %shard_map.113 = bf16[2,1024,128]{2,1,0:T(8,128)(2,1)} custom-call(s32[1]{0:T(128)} %bitcast.c_ref, bf16[2,1024,128]{2,1,0:T(8,128)(2,1)} %copy_bitcast_fusion.1.q_ref, bf16[2,4096,128]{2,1,0:T(8,128)(2,1)} %all-gather.3.cloned.1.call-done.k_ref, bf16[2,4096,128]{2,1,0:T(8,128)(2,1)} %all-gather.5.cloned.1.call-done.v_ref), custom_call_target="tpu_custom_call" | custom-call | flops 2147483648 | bytes 5242880 | tf_op jit(solution)/shard_map/pallas_call | solution.py:83
  289.9 1.9 copy_bitcast_fusion
  291.8 0.4 copy.111
  292.2 0.3 reshape.272
  292.5 1.2 gather_fusion
  293.7 0.2 gather.11
  293.9 2.3 multiply_reduce_fusion
  (49 shorter events, 1.4 us)
Async XLA Ops:
  7.2 141.9 %copy-start = (bf16[1,128,16,128]{3,2,1,0:T(8,128)(2,1)S(1)}, bf16[1,128,16,128]{3,2,1,0:T(8,128)(2,1)}, u32[]{:S(2)}) copy-start(bf16[1,128,16,128]{3,2,1,0:T(8,128)(2,1)} %param.11) | copy-start | bytes 1572868
  7.2 6.0 %copy-start.7 = (bf16[1,128,2,128]{3,2,1,0:T(2,128)(2,1)S(1)}, bf16[1,128,2,128]{3,2,1,0:T(2,128)(2,1)}, u32[]{:S(2)}) copy-start(bf16[1,128,2,128]{3,2,1,0:T(2,128)(2,1)} %param.12) | copy-start | bytes 196612
  7.2 6.7 %copy-start.8 = (s32[1,128,2]{1,2,0:T(2,128)S(1)}, s32[1,128,2]{1,2,0:T(2,128)}, u32[]{:S(2)}) copy-start(s32[1,128,2]{1,2,0:T(2,128)} %param.14) | copy-start | bytes 3076
  7.2 7.3 %copy-start.5 = (bf16[1,128,1024]{2,1,0:T(8,128)(2,1)S(1)}, bf16[1,128,1024]{2,1,0:T(8,128)(2,1)}, u32[]{:S(2)}) copy-start(bf16[1,128,1024]{2,1,0:T(8,128)(2,1)} %param.10) | copy-start | bytes 786436
  7.2 7.8 %copy-start.9 = (bf16[1024]{0:T(1024)(128)(2,1)S(1)}, bf16[1024]{0:T(1024)(128)(2,1)}, u32[]{:S(2)}) copy-start(bf16[1024]{0:T(1024)(128)(2,1)} %param.15) | copy-start | bytes 6148
  7.2 142.6 %all-gather.3.cloned.1.call-start = ((), (), s32[]{:S(2)}) async-start(), calls=%async_computation.4 | async-start | bytes 2162688 | tf_op jit(solution)/shard_map/all_gather | solution.py:76
  9.7 29.8 %collective-permute-start = (bf16[3,192,1024]{2,1,0:T(8,128)(2,1)}, bf16[3,192,1024]{2,1,0:T(8,128)(2,1)S(1)}, u32[]{:S(2)}, u32[]{:S(2)}) collective-permute-start(bf16[3,192,1024]{2,1,0:T(8,128)(2,1)} %pad_maximum_fusion.2), channel_id=1, source_target_pairs={{0,2},{1,3},{2,0},{3,1},{4,6},{5,7},{6,4},{7,5},{8,10},{9,11},{10,... | collective-permute-start | bytes 3538952 | tf_op jit(solution)/shard_map/ppermute | solution.py:13
  15.1 0.7 copy-start.3
  19.7 19.8 %copy-start.1 = (bf16[192,1024]{1,0:T(8,128)(2,1)S(1)}, bf16[192,1024]{1,0:T(8,128)(2,1)}, u32[]{:S(2)}) copy-start(bf16[192,1024]{1,0:T(8,128)(2,1)} %param.19) | copy-start | bytes 1179652
  19.7 19.8 %copy-start.2 = (bf16[192,1024]{1,0:T(8,128)(2,1)S(1)}, bf16[192,1024]{1,0:T(8,128)(2,1)}, u32[]{:S(2)}) copy-start(bf16[192,1024]{1,0:T(8,128)(2,1)} %param.18) | copy-start | bytes 1179652
  22.5 33.3 %all-to-all-start = ((bf16[4,32,4,1024]{3,2,0,1:T(4,128)(2,1)}), bf16[4,32,4,1024]{3,2,0,1:T(4,128)(2,1)S(1)}, u32[]{:S(2)}, u32[]{:S(2)}) async-start(bf16[4,32,4,1024]{3,2,0,1:T(4,128)(2,1)} %copy.104), calls=%async_computation | async-start | bytes 2097152 | tf_op jit(solution)/shard_map/all_to_all | solution.py:165
  42.2 22.8 %collective-permute-start.1 = (bf16[3,384,1024]{2,1,0:T(8,128)(2,1)}, bf16[3,384,1024]{2,1,0:T(8,128)(2,1)}, u32[]{:S(2)}, u32[]{:S(2)}) collective-permute-start(bf16[3,384,1024]{2,1,0:T(8,128)(2,1)} %pad_maximum_fusion.1), channel_id=1, source_target_pairs={{0,1},{1,0},{2,3},{3,2},{4,5},{5,4},{6,7},{7,6},{8,9},{9,8},{10,11... | collective-permute-start | bytes 7077896 | tf_op jit(solution)/shard_map/ppermute | solution.py:13
  57.4 32.7 %all-to-all-start.1 = ((bf16[16,8,4,1024]{3,1,2,0:T(8,128)(2,1)}), bf16[16,8,4,1024]{3,1,2,0:T(8,128)(2,1)S(1)}, u32[]{:S(2)}, u32[]{:S(2)}) async-start(bf16[16,8,4,1024]{3,1,2,0:T(8,128)(2,1)} %copy.106), calls=%async_computation.1 | async-start | bytes 2097152 | tf_op jit(solution)/shard_map/all_to_all | solution.py:168
  63.5 123.8 %all-gather.5.cloned.1.call-start = ((), (), s32[]{:S(2)}) async-start(), calls=%async_computation.5 | async-start | bytes 2162688 | tf_op jit(solution)/shard_map/all_gather | solution.py:77
  134.4 12.1 %copy-start.4 = (bf16[128,1024]{1,0:T(8,128)(2,1)S(1)}, bf16[128,1024]{1,0:T(8,128)(2,1)}, u32[]{:S(2)}) copy-start(bf16[128,1024]{1,0:T(8,128)(2,1)} %copy-done.3) | copy-start | bytes 786436
  134.4 12.1 %copy-start.6 = (bf16[1024,128]{1,0:T(8,128)(2,1)S(1)}, bf16[1024,128]{1,0:T(8,128)(2,1)}, u32[]{:S(2)}) copy-start(bf16[1024,128]{1,0:T(8,128)(2,1)} %param.16) | copy-start | bytes 786436
  136.2 155.6 %all-to-all-start.3 = ((bf16[4,32,4,1024]{3,2,0,1:T(4,128)(2,1)}), bf16[4,32,4,1024]{3,2,0,1:T(4,128)(2,1)S(1)}, u32[]{:S(2)}, u32[]{:S(2)}) async-start(bf16[4,32,4,1024]{3,2,0,1:T(4,128)(2,1)} %copy.110), calls=%async_computation.3 | async-start | bytes 2097152 | tf_op jit(solution)/shard_map/all_to_all | solution.py:173
Sparse Core Ops, SparseCore 0:
  14.0 82.4 all-gather.2
  99.6 87.5 all-gather.4

commit v2 on v1

--- a/solution.py
+++ b/solution.py
@@ -21,10 +21,10 @@
     return jnp.dot(hidden, down_rows, preferred_element_type=jnp.float32)
 
 
-def _flash_kernel(block, group, scaling, c_ref, q_ref, k_ref, v_ref, o_ref, m_sc, l_sc, acc_sc):
+def _flash_kernel(block, group, scaling, c_ref, qt_ref, k_ref, vt_ref, o_ref, m_sc, l_sc, acc_sc):
     c = c_ref[0]
-    q = q_ref[0]
-    rows = q.shape[0]
+    qt = qt_ref[0]
+    width = qt.shape[1]
     m_sc[...] = jnp.full(m_sc.shape, -1e30, jnp.float32)
     l_sc[...] = jnp.zeros(l_sc.shape, jnp.float32)
     acc_sc[...] = jnp.zeros(acc_sc.shape, jnp.float32)
@@ -32,20 +32,19 @@
     def update(j, masked):
         start = pl.multiple_of(j * block, block)
         k = k_ref[0, pl.ds(start, block), :]
-        v = v_ref[0, pl.ds(start, block), :]
-        s = lax.dot_general(q, k, (((1,), (1,)), ((), ())), preferred_element_type=jnp.float32)
-        s = s * scaling
+        vt = vt_ref[0, :, pl.ds(start, block)]
+        s = jnp.dot(k, qt, preferred_element_type=jnp.float32) * scaling
         if masked:
-            qpos = lax.broadcasted_iota(jnp.int32, (rows, block), 0) // group
-            kpos = lax.broadcasted_iota(jnp.int32, (rows, block), 1)
+            kpos = lax.broadcasted_iota(jnp.int32, (block, width), 0)
+            qpos = lax.broadcasted_iota(jnp.int32, (block, width), 1) // group
             s = jnp.where(kpos <= qpos, s, -1e30)
         m_prev = m_sc[...]
-        m_new = jnp.maximum(m_prev, jnp.max(s, axis=1, keepdims=True))
+        m_new = jnp.maximum(m_prev, jnp.max(s, axis=0, keepdims=True))
         alpha = jnp.exp(m_prev - m_new)
         p = jnp.exp(s - m_new)
-        l_sc[...] = alpha * l_sc[...] + jnp.sum(p, axis=1, keepdims=True)
+        l_sc[...] = alpha * l_sc[...] + jnp.sum(p, axis=0, keepdims=True)
         acc_sc[...] = alpha * acc_sc[...] + jnp.dot(
-            p.astype(jnp.bfloat16), v, preferred_element_type=jnp.float32
+            vt, p.astype(jnp.bfloat16), preferred_element_type=jnp.float32
         )
         m_sc[...] = m_new
 
@@ -65,49 +64,46 @@
     kv_count = key_rows.shape[2]
     group_size = head_count // kv_count
     scaling = 1.0 / math.sqrt(head_size)
-    grouped = (
+    width = seq_rows * group_size
+    grouped_t = (
         queries[0]
         .reshape(seq_rows, kv_count, group_size, head_size)
-        .transpose(1, 0, 2, 3)
-        .reshape(kv_count, seq_rows * group_size, head_size)
+        .transpose(1, 3, 0, 2)
+        .reshape(kv_count, head_size, width)
     )
-    keys_local = key_rows[0].transpose(1, 0, 2)
-    values_local = value_rows[0].transpose(1, 0, 2)
-    keys_all = lax.all_gather(keys_local, "ctx", axis=1, tiled=True)
-    values_all = lax.all_gather(values_local, "ctx", axis=1, tiled=True)
+    local_kv = jnp.stack([key_rows[0], value_rows[0]], axis=0).transpose(0, 2, 1, 3)
+    gathered = lax.all_gather(local_kv, "ctx", axis=2, tiled=True)
+    keys_all = gathered[0]
+    values_t = gathered[1].transpose(0, 2, 1)
     total_rows = keys_all.shape[1]
-    q_rows = seq_rows * group_size
     me = lax.axis_index("ctx").astype(jnp.int32).reshape(1)
-    ctx_count = lax.axis_size("ctx")
-    flops = 4 * kv_count * q_rows * total_rows * head_size // 2
     out = pl.pallas_call(
         functools.partial(_flash_kernel, seq_rows, group_size, scaling),
         grid_spec=pltpu.PrefetchScalarGridSpec(
             num_scalar_prefetch=1,
             grid=(kv_count,),
             in_specs=[
-                pl.BlockSpec((1, q_rows, head_size), lambda g, c: (g, 0, 0)),
+                pl.BlockSpec((1, head_size, width), lambda g, c: (g, 0, 0)),
                 pl.BlockSpec((1, total_rows, head_size), lambda g, c: (g, 0, 0)),
-                pl.BlockSpec((1, total_rows, head_size), lambda g, c: (g, 0, 0)),
+                pl.BlockSpec((1, head_size, total_rows), lambda g, c: (g, 0, 0)),
             ],
-            out_specs=pl.BlockSpec((1, q_rows, head_size), lambda g, c: (g, 0, 0)),
+            out_specs=pl.BlockSpec((1, head_size, width), lambda g, c: (g, 0, 0)),
             scratch_shapes=[
-                pltpu.VMEM((q_rows, 1), jnp.float32),
-                pltpu.VMEM((q_rows, 1), jnp.float32),
-                pltpu.VMEM((q_rows, head_size), jnp.float32),
+                pltpu.VMEM((1, width), jnp.float32),
+                pltpu.VMEM((1, width), jnp.float32),
+                pltpu.VMEM((head_size, width), jnp.float32),
             ],
         ),
-        out_shape=jax.ShapeDtypeStruct((kv_count, q_rows, head_size), jnp.bfloat16),
+        out_shape=jax.ShapeDtypeStruct((kv_count, head_size, width), jnp.bfloat16),
         cost_estimate=pl.CostEstimate(
-            flops=flops,
-            transcendentals=kv_count * q_rows * total_rows // 2,
-            bytes_accessed=4 * kv_count * total_rows * head_size + 4 * kv_count * q_rows * head_size,
+            flops=2 * kv_count * width * total_rows * head_size,
+            transcendentals=kv_count * width * total_rows // 2,
+            bytes_accessed=4 * kv_count * total_rows * head_size + 4 * kv_count * width * head_size,
         ),
-    )(me, grouped, keys_all, values_all)
-    del ctx_count
+    )(me, grouped_t, keys_all, values_t)
     return (
-        out.reshape(kv_count, seq_rows, group_size, head_size)
-        .transpose(1, 0, 2, 3)
+        out.reshape(kv_count, head_size, seq_rows, group_size)
+        .transpose(2, 0, 3, 1)
         .reshape(1, seq_rows, head_count, head_size)
     )
 

time: 304 us -> 224 us (0.74)
  the two profiles are of different devices: /device:TPU:454 before, /device:TPU:455 now
where the time goes in v2:
time: 224 us; the launch traced here: 223 us
  waiting for transfers between devices  55.7 us (25%)
  Pallas kernels  35.3 us (16%)
  starting transfers between devices  32.3 us (14%)
  blocking collectives  31.9 us (14%)
  local copies, waits for them, and re-layouts  31.3 us (14%)
  between operations  14.4 us (6%)
  other arithmetic  12.7 us (6%)
  matrix products  9.51 us (4%)
    pallas_call x1, Pallas kernels, attention(): pl.pallas_call(functools.partial(_flash_kernel, seq_rows, group_size, sca...  35.3 us
    all_to_all x1, blocking collectives, local(): lax.all_to_all(computed, 'exp', split_axis=0, concat_axis=0, tiled=True)  31.9 us
    all_to_all x1, waiting for transfers between devices, local(): lax.all_to_all(to_holders, 'exp', split_axis=0, concat_axis=0, tiled=True)  24.1 us
    all_to_all x1, waiting for transfers between devices, local(): lax.all_to_all(finished, 'ctx', split_axis=1, concat_axis=1, tiled=True)  20.1 us
    all_to_all x1, starting transfers between devices, local(): lax.all_to_all(to_holders, 'exp', split_axis=0, concat_axis=0, tiled=True)  10.3 us
    all_to_all x1, starting transfers between devices, local(): lax.all_to_all(finished, 'ctx', split_axis=1, concat_axis=1, tiled=True)  8.77 us
    ppermute x2, waiting for transfers between devices, from_partner(): lax.ppermute(value, axis, [(i, i ^ flip) for i in range(lax.axis_size(axi...  7.95 us
    ppermute x2, starting transfers between devices, from_partner(): lax.ppermute(value, axis, [(i, i ^ flip) for i in range(lax.axis_size(axi...  6.64 us
  transfers between devices with their start and end apart: 6, of which 4 were waited for; matrix products, arithmetic and copies ran while one was open for 19% of the time, Pallas kernels for 0%

profile of v2, /device:TPU:455, one launch (start us, length us, event | category | flops | bytes accessed | tf_op | source)
XLA Modules:
  0.0 223.2 jit_solution(11422683437236494754)
XLA Ops:
  7.2 2.5 %pad_maximum_fusion.2 = bf16[3,192,1024]{2,1,0:T(8,128)(2,1)} fusion(bf16[1,192,1024]{2,1,0:T(8,128)(2,1)} %bitcast.88, bf16[1,192,1024]{2,1,0:T(8,128)(2,1)} %bitcast.91, bf16[1,192,1024]{2,1,0:T(8,128)(2,1)} %bitcast.94), kind=kLoop, calls=%fused_computation.15 | loop fusion | flops 1179648 | bytes 2359296 | tf_op jit(solution)/shard_map/stack | solution.py:133
  9.7 3.2 %collective-permute-start = (bf16[3,192,1024]{2,1,0:T(8,128)(2,1)}, bf16[3,192,1024]{2,1,0:T(8,128)(2,1)S(1)}, u32[]{:S(2)}, u32[]{:S(2)}) collective-permute-start(bf16[3,192,1024]{2,1,0:T(8,128)(2,1)} %pad_maximum_fusion.2), channel_id=1, source_target_pairs={{0,2},{1,3},{2,0},{3,1},{4,6},{5,7},{6,4},{7,5},{8,10},{9,11},{10,... | collective-permute-start | bytes 3538952 | tf_op jit(solution)/shard_map/ppermute | solution.py:13
  13.2 0.2 fusion.10
  14.0 0.1 reshape_squeeze.13
  14.2 0.3 broadcast_in_dim.28
  14.4 0.2 reshape.292
  14.6 0.2 fusion.12
  14.9 1.9 scatter_custom_fusion
  16.8 1.2 reshape.267
  18.0 2.8 %copy.135 = bf16[4,32,4,1024]{3,2,0,1:T(4,128)(2,1)} copy(bf16[4,32,4,1024]{3,2,1,0:T(4,128)(2,1)} %reshape.267) | data formatting | bytes 2097152 | tf_op jit(solution)/shard_map/reshape | solution.py:160
  20.9 6.6 %all-to-all-start = ((bf16[4,32,4,1024]{3,2,0,1:T(4,128)(2,1)}), bf16[4,32,4,1024]{3,2,0,1:T(4,128)(2,1)S(1)}, u32[]{:S(2)}, u32[]{:S(2)}) async-start(bf16[4,32,4,1024]{3,2,0,1:T(4,128)(2,1)} %copy.135), calls=%async_computation | async-start | bytes 2097152 | tf_op jit(solution)/shard_map/all_to_all | solution.py:161
  27.5 1.6 copy.122
  29.1 1.6 copy.123
  30.6 7.9 %collective-permute-done = bf16[3,192,1024]{2,1,0:T(8,128)(2,1)S(1)} collective-permute-done((bf16[3,192,1024]{2,1,0:T(8,128)(2,1)}, bf16[3,192,1024]{2,1,0:T(8,128)(2,1)S(1)}, u32[]{:S(2)}, u32[]{:S(2)}) %collective-permute-start) | collective-permute-done | bytes 1179680 | tf_op jit(solution)/shard_map/ppermute | solution.py:13
  38.6 2.6 %pad_maximum_fusion.1 = bf16[3,384,1024]{2,1,0:T(8,128)(2,1)} fusion(bf16[3,192,1024]{2,1,0:T(8,128)(2,1)S(1)} %collective-permute-done, bf16[1,192,1024]{2,1,0:T(8,128)(2,1)S(1)} %bitcast.89, bf16[1,192,1024]{2,1,0:T(8,128)(2,1)S(1)} %bitcast.92, bf16[1,192,1024]{2,1,0:T(8,128)(2,1)} %bitcast.95), kind=kLoop, calls=%fused_computation.4 | loop fusion | flops 9437184 | bytes 4718592 | tf_op jit(solution)/shard_map/concatenate | solution.py:135
  41.2 3.4 %collective-permute-start.1 = (bf16[3,384,1024]{2,1,0:T(8,128)(2,1)}, bf16[3,384,1024]{2,1,0:T(8,128)(2,1)}, u32[]{:S(2)}, u32[]{:S(2)}) collective-permute-start(bf16[3,384,1024]{2,1,0:T(8,128)(2,1)} %pad_maximum_fusion.1), channel_id=1, source_target_pairs={{0,1},{1,0},{2,3},{3,2},{4,5},{5,4},{6,7},{7,6},{8,9},{9,8},{10,11... | collective-permute-start | bytes 7077896 | tf_op jit(solution)/shard_map/ppermute | solution.py:13
  44.7 0.7 maximum_bitcast_fusion
  45.4 3.5 %all-to-all-done = bf16[4,32,4,1024]{3,2,0,1:T(4,128)(2,1)S(1)} async-done(((bf16[4,32,4,1024]{3,2,0,1:T(4,128)(2,1)}), bf16[4,32,4,1024]{3,2,0,1:T(4,128)(2,1)S(1)}, u32[]{:S(2)}, u32[]{:S(2)}) %all-to-all-start) | async-done | bytes 1048608 | tf_op jit(solution)/shard_map/all_to_all | solution.py:161
  48.9 0.6 copy.136
  49.5 1.1 copy.137
  50.5 10.3 %all-to-all-start.1 = ((bf16[16,8,4,1024]{3,1,2,0:T(8,128)(2,1)}), bf16[16,8,4,1024]{3,1,2,0:T(8,128)(2,1)S(1)}, u32[]{:S(2)}, u32[]{:S(2)}) async-start(bf16[16,8,4,1024]{3,1,2,0:T(8,128)(2,1)} %copy.137), calls=%async_computation.1 | async-start | bytes 2097152 | tf_op jit(solution)/shard_map/all_to_all | solution.py:164
  60.8 3.8 %pad_maximum_fusion = bf16[3,768,1024]{2,1,0:T(8,128)(2,1)} fusion(bf16[3,384,1024]{2,1,0:T(8,128)(2,1)} %collective-permute-done.1, bf16[3,192,1024]{2,1,0:T(8,128)(2,1)S(1)} %collective-permute-done, bf16[1,192,1024]{2,1,0:T(8,128)(2,1)S(1)} %bitcast.90, bf16[1,192,1024]{2,1,0:T(8,128)(2,1)S(1)} %bitcast.93, bf16[1,192,1024]{2,1,0:T(8,128)(2,1)} %bitcast.96), kind=kLoop, calls=%fused_computation.3 | loop fusion | flops 23592960 | bytes 9437184 | tf_op jit(solution)/shard_map/concatenate | solution.py:137
  64.6 24.1 %all-to-all-done.1 = bf16[16,8,4,1024]{3,1,2,0:T(8,128)(2,1)S(1)} async-done(((bf16[16,8,4,1024]{3,1,2,0:T(8,128)(2,1)}), bf16[16,8,4,1024]{3,1,2,0:T(8,128)(2,1)S(1)}, u32[]{:S(2)}, u32[]{:S(2)}) %all-to-all-start.1) | async-done | bytes 1048608 | tf_op jit(solution)/shard_map/all_to_all | solution.py:164
  88.8 0.9 copy.138
  89.6 0.3 reshape.269
  89.9 3.6 %fusion.1 = f32[512,768]{1,0:T(8,128)} fusion(bf16[512,1024]{1,0:T(8,128)(2,1)S(1)} %reshape.269, bf16[3,768,1024]{2,1,0:T(8,128)(2,1)} %pad_maximum_fusion), kind=kOutput, calls=%fused_computation.10 | convolution fusion | flops 805306368 | bytes 4194304 | tf_op jit(solution)/shard_map/dot_general | solution.py:19
  93.5 5.7 %fusion.3 = bf16[512,1024]{1,0:T(8,128)(2,1)} fusion(bf16[3,768,1024]{2,1,0:T(8,128)(2,1)} %pad_maximum_fusion, f32[512,768]{1,0:T(8,128)} %fusion.1, bf16[512,1024]{1,0:T(8,128)(2,1)S(1)} %reshape.269), kind=kOutput, calls=%fused_computation.14 | convolution fusion | flops 1613496320 | bytes 6815744 | tf_op jit(solution)/shard_map/dot_general | solution.py:21
  99.2 1.5 reshape.270
  100.7 0.4 copy.139
  101.1 31.9 %all_to_all.20 = bf16[16,8,4,1024]{3,1,2,0:T(8,128)(2,1)S(1)} all-to-all(bf16[16,8,4,1024]{3,1,2,0:T(8,128)(2,1)S(1)} %copy.139), channel_id=1, replica_groups=mesh['ctx'=32,'exp'=16] {'exp'}, dimensions={0} | all-to-all | bytes 2097152 | tf_op jit(solution)/shard_map/all_to_all | solution.py:167
  133.1 1.8 copy.141
  134.9 8.8 %all-to-all-start.3 = ((bf16[4,32,4,1024]{3,2,0,1:T(4,128)(2,1)}), bf16[4,32,4,1024]{3,2,0,1:T(4,128)(2,1)S(1)}, u32[]{:S(2)}, u32[]{:S(2)}) async-start(bf16[4,32,4,1024]{3,2,0,1:T(4,128)(2,1)} %copy.141), calls=%async_computation.3 | async-start | bytes 2097152 | tf_op jit(solution)/shard_map/all_to_all | solution.py:169
  143.9 0.1 copy.133
  144.1 0.1 reshape.282
  144.3 0.2 fusion.23
  144.5 1.9 gather_fusion.1
  146.8 1.0 copy.124.qt_ref
  147.9 20.1 %all-to-all-done.3 = bf16[4,32,4,1024]{3,2,0,1:T(4,128)(2,1)S(1)} async-done(((bf16[4,32,4,1024]{3,2,0,1:T(4,128)(2,1)}), bf16[4,32,4,1024]{3,2,0,1:T(4,128)(2,1)S(1)}, u32[]{:S(2)}, u32[]{:S(2)}) %all-to-all-start.3) | async-done | bytes 1048608 | tf_op jit(solution)/shard_map/all_to_all | solution.py:169
  167.9 0.4 copy.142
  168.3 0.3 reshape.272
  168.6 1.2 gather_fusion
  169.8 0.2 gather.11
  170.0 2.3 %multiply_reduce_fusion = bf16[128,1024]{1,0:T(8,128)(2,1)} fusion(bf16[128,2,1024]{2,1,0:T(2,128)(2,1)S(1)} %gather.11, pred[128,2]{1,0:T(8,128)(4,1)S(1)} %copy.133, f32[128,2]{1,0:T(8,128)S(1)} %copy.145), kind=kLoop, calls=%fused_computation.16 | loop fusion | flops 917504 | bytes 787712 | tf_op jit(solution)/shard_map/reduce_sum | solution.py:174
  172.4 4.0 %slice_bitcast_fusion = (bf16[2,128,4096]{2,1,0:T(8,128)(2,1)}, bf16[2,4096,128]{1,2,0:T(8,128)(2,1)S(1)}) fusion(bf16[2,2,4096,128]{2,3,1,0:T(8,128)(2,1)} %all-gather.2.cloned.1.call-done), kind=kLoop, calls=%fused_computation.5 | loop fusion | bytes 8388608 | tf_op jit(solution)/shard_map/transpose | solution.py:77
  176.3 2.4 %copy.125.k_ref = bf16[2,4096,128]{2,1,0:T(8,128)(2,1)} copy(bf16[2,4096,128]{1,2,0:T(8,128)(2,1)S(1)} %get-tuple-element.3) | data formatting | bytes 4194304 | tf_op jit(solution)/shard_map/squeeze | solution.py:76
  178.8 35.3 %shard_map.113 = bf16[2,128,1024]{2,1,0:T(8,128)(2,1)} custom-call(s32[1]{0:T(128)} %bitcast.c_ref, bf16[2,128,1024]{2,1,0:T(8,128)(2,1)} %copy.124.qt_ref, bf16[2,4096,128]{2,1,0:T(8,128)(2,1)} %copy.125.k_ref, bf16[2,128,4096]{2,1,0:T(8,128)(2,1)} %get-tuple-element.2.vt_ref), custom_call_target="tpu_custom_call" | custom-call | flops 2147483648 | bytes 5242880 | tf_op jit(solution)/shard_map/pallas_call | solution.py:80
  214.1 1.3 copy.126
  215.4 0.9 copy_bitcast_fusion
  (53 shorter events, 1.8 us)
Async XLA Ops:
  7.2 139.6 %copy-start = (bf16[1,128,16,128]{3,2,1,0:T(8,128)(2,1)S(1)}, bf16[1,128,16,128]{3,2,1,0:T(8,128)(2,1)}, u32[]{:S(2)}) copy-start(bf16[1,128,16,128]{3,2,1,0:T(8,128)(2,1)} %param.11) | copy-start | bytes 1572868
  7.2 5.7 %copy-start.9 = (s32[1,128,2]{1,2,0:T(2,128)S(1)}, s32[1,128,2]{1,2,0:T(2,128)}, u32[]{:S(2)}) copy-start(s32[1,128,2]{1,2,0:T(2,128)} %param.14) | copy-start | bytes 3076
  7.2 6.3 %copy-start.10 = (bf16[1024]{0:T(1024)(128)(2,1)S(1)}, bf16[1024]{0:T(1024)(128)(2,1)}, u32[]{:S(2)}) copy-start(bf16[1024]{0:T(1024)(128)(2,1)} %param.15) | copy-start | bytes 6148
  7.2 6.3 %copy-start.5 = (bf16[1,128,1024]{2,1,0:T(8,128)(2,1)S(1)}, bf16[1,128,1024]{2,1,0:T(8,128)(2,1)}, u32[]{:S(2)}) copy-start(bf16[1,128,1024]{2,1,0:T(8,128)(2,1)} %param.10) | copy-start | bytes 786436
  9.7 28.9 %collective-permute-start = (bf16[3,192,1024]{2,1,0:T(8,128)(2,1)}, bf16[3,192,1024]{2,1,0:T(8,128)(2,1)S(1)}, u32[]{:S(2)}, u32[]{:S(2)}) collective-permute-start(bf16[3,192,1024]{2,1,0:T(8,128)(2,1)} %pad_maximum_fusion.2), channel_id=1, source_target_pairs={{0,2},{1,3},{2,0},{3,1},{4,6},{5,7},{6,4},{7,5},{8,10},{9,11},{10,... | collective-permute-start | bytes 3538952 | tf_op jit(solution)/shard_map/ppermute | solution.py:13
  13.8 1.0 copy-start.3
  18.0 20.6 %copy-start.1 = (bf16[192,1024]{1,0:T(8,128)(2,1)S(1)}, bf16[192,1024]{1,0:T(8,128)(2,1)}, u32[]{:S(2)}) copy-start(bf16[192,1024]{1,0:T(8,128)(2,1)} %param.19) | copy-start | bytes 1179652
  18.0 20.6 %copy-start.2 = (bf16[192,1024]{1,0:T(8,128)(2,1)S(1)}, bf16[192,1024]{1,0:T(8,128)(2,1)}, u32[]{:S(2)}) copy-start(bf16[192,1024]{1,0:T(8,128)(2,1)} %param.18) | copy-start | bytes 1179652
  20.9 28.0 %all-to-all-start = ((bf16[4,32,4,1024]{3,2,0,1:T(4,128)(2,1)}), bf16[4,32,4,1024]{3,2,0,1:T(4,128)(2,1)S(1)}, u32[]{:S(2)}, u32[]{:S(2)}) async-start(bf16[4,32,4,1024]{3,2,0,1:T(4,128)(2,1)} %copy.135), calls=%async_computation | async-start | bytes 2097152 | tf_op jit(solution)/shard_map/all_to_all | solution.py:161
  27.4 144.9 %all-gather.2.cloned.1.call-start = ((), (), s32[]{:S(2)}) async-start(), calls=%async_computation.4 | async-start | bytes 4325376 | tf_op jit(solution)/shard_map/all_gather | solution.py:75
  30.6 14.1 %copy-start.7 = (bf16[1,128,2,128]{1,3,2,0:T(8,128)(2,1)S(1)}, bf16[1,128,2,128]{1,3,2,0:T(8,128)(2,1)}, u32[]{:S(2)}) copy-start(bf16[1,128,2,128]{1,3,2,0:T(8,128)(2,1)} %copy.122) | copy-start | bytes 196612
  30.6 14.1 %copy-start.8 = (bf16[1,128,2,128]{1,3,2,0:T(8,128)(2,1)S(1)}, bf16[1,128,2,128]{1,3,2,0:T(8,128)(2,1)}, u32[]{:S(2)}) copy-start(bf16[1,128,2,128]{1,3,2,0:T(8,128)(2,1)} %copy.123) | copy-start | bytes 196612
  41.2 19.6 %collective-permute-start.1 = (bf16[3,384,1024]{2,1,0:T(8,128)(2,1)}, bf16[3,384,1024]{2,1,0:T(8,128)(2,1)}, u32[]{:S(2)}, u32[]{:S(2)}) collective-permute-start(bf16[3,384,1024]{2,1,0:T(8,128)(2,1)} %pad_maximum_fusion.1), channel_id=1, source_target_pairs={{0,1},{1,0},{2,3},{3,2},{4,5},{5,4},{6,7},{7,6},{8,9},{9,8},{10,11... | collective-permute-start | bytes 7077896 | tf_op jit(solution)/shard_map/ppermute | solution.py:13
  50.5 38.2 %all-to-all-start.1 = ((bf16[16,8,4,1024]{3,1,2,0:T(8,128)(2,1)}), bf16[16,8,4,1024]{3,1,2,0:T(8,128)(2,1)S(1)}, u32[]{:S(2)}, u32[]{:S(2)}) async-start(bf16[16,8,4,1024]{3,1,2,0:T(8,128)(2,1)} %copy.137), calls=%async_computation.1 | async-start | bytes 2097152 | tf_op jit(solution)/shard_map/all_to_all | solution.py:164
  133.0 11.2 %copy-start.4 = (bf16[128,1024]{1,0:T(8,128)(2,1)S(1)}, bf16[128,1024]{1,0:T(8,128)(2,1)}, u32[]{:S(2)}) copy-start(bf16[128,1024]{1,0:T(8,128)(2,1)} %copy-done.3) | copy-start | bytes 786436
  133.1 11.2 %copy-start.6 = (bf16[1024,128]{1,0:T(8,128)(2,1)S(1)}, bf16[1024,128]{1,0:T(8,128)(2,1)}, u32[]{:S(2)}) copy-start(bf16[1024,128]{1,0:T(8,128)(2,1)} %param.16) | copy-start | bytes 786436
  134.9 33.1 %all-to-all-start.3 = ((bf16[4,32,4,1024]{3,2,0,1:T(4,128)(2,1)}), bf16[4,32,4,1024]{3,2,0,1:T(4,128)(2,1)S(1)}, u32[]{:S(2)}, u32[]{:S(2)}) async-start(bf16[4,32,4,1024]{3,2,0,1:T(4,128)(2,1)} %copy.141), calls=%async_computation.3 | async-start | bytes 2097152 | tf_op jit(solution)/shard_map/all_to_all | solution.py:169
Sparse Core Ops, SparseCore 0:
  45.6 82.8 all-gather.1

commit v3 on v2

--- a/solution.py
+++ b/solution.py
@@ -29,10 +29,10 @@
     l_sc[...] = jnp.zeros(l_sc.shape, jnp.float32)
     acc_sc[...] = jnp.zeros(acc_sc.shape, jnp.float32)
 
-    def update(j, masked):
-        start = pl.multiple_of(j * block, block)
-        k = k_ref[0, pl.ds(start, block), :]
-        vt = vt_ref[0, :, pl.ds(start, block)]
+    def update(j, masked, size=block):
+        start = pl.multiple_of(j * size, size)
+        k = k_ref[0, pl.ds(start, size), :]
+        vt = vt_ref[0, :, pl.ds(start, size)]
         s = jnp.dot(k, qt, preferred_element_type=jnp.float32) * scaling
         if masked:
             kpos = lax.broadcasted_iota(jnp.int32, (block, width), 0)
@@ -48,11 +48,19 @@
         )
         m_sc[...] = m_new
 
+    wide = 4 * block
+    span = wide // block
+
+    def body_wide(j, carry):
+        update(j, False, wide)
+        return carry
+
     def body(j, carry):
         update(j, False)
         return carry
 
-    lax.fori_loop(0, c, body, 0)
+    lax.fori_loop(0, c // span, body_wide, 0)
+    lax.fori_loop(c // span * span, c, body, 0)
     update(c, True)
     o_ref[0] = (acc_sc[...] / l_sc[...]).astype(o_ref.dtype)
 
@@ -167,6 +175,7 @@
     returned = lax.all_to_all(computed, "exp", split_axis=0, concat_axis=0, tiled=True)
     finished = returned.reshape(per_ctx, ctx_count, capacity, features)
     came_back = lax.all_to_all(finished, "ctx", split_axis=1, concat_axis=1, tiled=True)
+    attended, came_back = lax.optimization_barrier((attended, came_back))
     flat_back = came_back.reshape(expert_total * capacity, features)
     picked = (
         jnp.take(flat_back, target, axis=0).astype(jnp.float32).reshape(tokens, top_count, features)

time: 224 us -> 199 us (0.89)
  the two profiles are of different devices: /device:TPU:455 before, /device:TPU:1 now
where the time goes in v3:
time: 199 us; the launch traced here: 198 us
  waiting for transfers between devices  83.7 us (42%)
  starting transfers between devices  41 us (21%)
  local copies, waits for them, and re-layouts  33 us (17%)
  between operations  14.5 us (7%)
  other arithmetic  12.7 us (6%)
  matrix products  9.52 us (5%)
  Pallas kernels  3.61 us (2%)
    all_to_all x1, waiting for transfers between devices, local(): lax.all_to_all(computed, 'exp', split_axis=0, concat_axis=0, tiled=True)  26.1 us
    all_to_all x1, waiting for transfers between devices, local(): lax.all_to_all(to_holders, 'exp', split_axis=0, concat_axis=0, tiled=True)  24.1 us
    all_to_all x1, waiting for transfers between devices, local(): lax.all_to_all(outgoing, 'ctx', split_axis=1, concat_axis=1, tiled=True)  21 us
    all_to_all x1, starting transfers between devices, local(): lax.all_to_all(outgoing, 'ctx', split_axis=1, concat_axis=1, tiled=True)  12.9 us
    all_to_all x1, waiting for transfers between devices, local(): lax.all_to_all(finished, 'ctx', split_axis=1, concat_axis=1, tiled=True)  12.4 us
    ppermute x2, starting transfers between devices, from_partner(): lax.ppermute(value, axis, [(i, i ^ flip) for i in range(lax.axis_size(axi...  11.4 us
    all_to_all x1, starting transfers between devices, local(): lax.all_to_all(to_holders, 'exp', split_axis=0, concat_axis=0, tiled=True)  8.24 us
    dot_general x1, matrix products, expert_rows(): return jnp.dot(hidden, down_rows, preferred_element_type=jnp.float32)  5.7 us
  transfers between devices with their start and end apart: 7, of which 4 were waited for; matrix products, arithmetic and copies ran while one was open for 23% of the time, Pallas kernels for 2%

profile of v3, /device:TPU:1, one launch (start us, length us, event | category | flops | bytes accessed | tf_op | source)
XLA Modules:
  0.0 198.0 jit_solution(13417680980030766455)
XLA Ops:
  7.3 1.0 copy.123
  8.3 1.0 copy.122
  9.3 0.7 maximum_bitcast_fusion
  10.0 2.4 %pad_maximum_fusion.2 = bf16[3,192,1024]{2,1,0:T(8,128)(2,1)} fusion(bf16[1,192,1024]{2,1,0:T(8,128)(2,1)} %bitcast.88, bf16[1,192,1024]{2,1,0:T(8,128)(2,1)} %bitcast.91, bf16[1,192,1024]{2,1,0:T(8,128)(2,1)} %bitcast.94), kind=kLoop, calls=%fused_computation.15 | loop fusion | flops 1179648 | bytes 2359296 | tf_op jit(solution)/shard_map/stack | solution.py:141
  12.4 4.0 %collective-permute-start = (bf16[3,192,1024]{2,1,0:T(8,128)(2,1)}, bf16[3,192,1024]{2,1,0:T(8,128)(2,1)S(1)}, u32[]{:S(2)}, u32[]{:S(2)}) collective-permute-start(bf16[3,192,1024]{2,1,0:T(8,128)(2,1)} %pad_maximum_fusion.2), channel_id=1, source_target_pairs={{0,2},{1,3},{2,0},{3,1},{4,6},{5,7},{6,4},{7,5},{8,10},{9,11},{10,... | collective-permute-start | bytes 3538952 | tf_op jit(solution)/shard_map/ppermute | solution.py:13
  16.8 0.2 fusion.10
  17.3 0.1 reshape_squeeze.7
  17.7 0.7 copy-done.3
  18.4 0.3 broadcast_in_dim.27
  18.6 0.2 reshape.292
  18.8 0.2 fusion.12
  19.1 1.9 scatter_custom_fusion
  21.0 1.2 reshape.267
  22.2 2.8 %copy.133 = bf16[4,32,4,1024]{3,2,0,1:T(4,128)(2,1)} copy(bf16[4,32,4,1024]{3,2,1,0:T(4,128)(2,1)} %reshape.267) | data formatting | bytes 2097152 | tf_op jit(solution)/shard_map/reshape | solution.py:168
  25.0 12.9 %all-to-all-start = ((bf16[4,32,4,1024]{3,2,0,1:T(4,128)(2,1)}), bf16[4,32,4,1024]{3,2,0,1:T(4,128)(2,1)S(1)}, u32[]{:S(2)}, u32[]{:S(2)}) async-start(bf16[4,32,4,1024]{3,2,0,1:T(4,128)(2,1)} %copy.133), calls=%async_computation | async-start | bytes 2097152 | tf_op jit(solution)/shard_map/all_to_all | solution.py:169
  38.0 2.7 %pad_maximum_fusion.1 = bf16[3,384,1024]{2,1,0:T(8,128)(2,1)} fusion(bf16[3,192,1024]{2,1,0:T(8,128)(2,1)S(1)} %collective-permute-done, bf16[1,192,1024]{2,1,0:T(8,128)(2,1)S(1)} %bitcast.89, bf16[1,192,1024]{2,1,0:T(8,128)(2,1)S(1)} %bitcast.92, bf16[1,192,1024]{2,1,0:T(8,128)(2,1)} %bitcast.95), kind=kLoop, calls=%fused_computation.4 | loop fusion | flops 9437184 | bytes 4718592 | tf_op jit(solution)/shard_map/concatenate | solution.py:143
  40.6 7.4 %collective-permute-start.1 = (bf16[3,384,1024]{2,1,0:T(8,128)(2,1)}, bf16[3,384,1024]{2,1,0:T(8,128)(2,1)}, u32[]{:S(2)}, u32[]{:S(2)}) collective-permute-start(bf16[3,384,1024]{2,1,0:T(8,128)(2,1)} %pad_maximum_fusion.1), channel_id=1, source_target_pairs={{0,1},{1,0},{2,3},{3,2},{4,5},{5,4},{6,7},{7,6},{8,9},{9,8},{10,11... | collective-permute-start | bytes 7077896 | tf_op jit(solution)/shard_map/ppermute | solution.py:13
  48.1 21.0 %all-to-all-done = bf16[4,32,4,1024]{3,2,0,1:T(4,128)(2,1)S(1)} async-done(((bf16[4,32,4,1024]{3,2,0,1:T(4,128)(2,1)}), bf16[4,32,4,1024]{3,2,0,1:T(4,128)(2,1)S(1)}, u32[]{:S(2)}, u32[]{:S(2)}) %all-to-all-start) | async-done | bytes 1048608 | tf_op jit(solution)/shard_map/all_to_all | solution.py:169
  69.0 0.6 copy.134
  69.6 1.1 copy.135
  70.7 8.2 %all-to-all-start.1 = ((bf16[16,8,4,1024]{3,1,2,0:T(8,128)(2,1)}), bf16[16,8,4,1024]{3,1,2,0:T(8,128)(2,1)S(1)}, u32[]{:S(2)}, u32[]{:S(2)}) async-start(bf16[16,8,4,1024]{3,1,2,0:T(8,128)(2,1)} %copy.135), calls=%async_computation.1 | async-start | bytes 2097152 | tf_op jit(solution)/shard_map/all_to_all | solution.py:172
  78.9 3.8 %pad_maximum_fusion = bf16[3,768,1024]{2,1,0:T(8,128)(2,1)} fusion(bf16[3,384,1024]{2,1,0:T(8,128)(2,1)} %collective-permute-done.1, bf16[3,192,1024]{2,1,0:T(8,128)(2,1)S(1)} %collective-permute-done, bf16[1,192,1024]{2,1,0:T(8,128)(2,1)S(1)} %bitcast.90, bf16[1,192,1024]{2,1,0:T(8,128)(2,1)S(1)} %bitcast.93, bf16[1,192,1024]{2,1,0:T(8,128)(2,1)} %bitcast.96), kind=kLoop, calls=%fused_computation.3 | loop fusion | flops 23592960 | bytes 9437184 | tf_op jit(solution)/shard_map/concatenate | solution.py:145
  82.7 24.1 %all-to-all-done.1 = bf16[16,8,4,1024]{3,1,2,0:T(8,128)(2,1)S(1)} async-done(((bf16[16,8,4,1024]{3,1,2,0:T(8,128)(2,1)}), bf16[16,8,4,1024]{3,1,2,0:T(8,128)(2,1)S(1)}, u32[]{:S(2)}, u32[]{:S(2)}) %all-to-all-start.1) | async-done | bytes 1048608 | tf_op jit(solution)/shard_map/all_to_all | solution.py:172
  106.8 0.9 copy.136
  107.7 0.3 reshape.269
  108.0 3.6 %fusion.1 = f32[512,768]{1,0:T(8,128)} fusion(bf16[512,1024]{1,0:T(8,128)(2,1)S(1)} %reshape.269, bf16[3,768,1024]{2,1,0:T(8,128)(2,1)} %pad_maximum_fusion), kind=kOutput, calls=%fused_computation.10 | convolution fusion | flops 805306368 | bytes 4194304 | tf_op jit(solution)/shard_map/dot_general | solution.py:19
  111.6 5.7 %fusion.3 = bf16[512,1024]{1,0:T(8,128)(2,1)} fusion(bf16[3,768,1024]{2,1,0:T(8,128)(2,1)} %pad_maximum_fusion, f32[512,768]{1,0:T(8,128)} %fusion.1, bf16[512,1024]{1,0:T(8,128)(2,1)S(1)} %reshape.269), kind=kOutput, calls=%fused_computation.14 | convolution fusion | flops 1613496320 | bytes 6815744 | tf_op jit(solution)/shard_map/dot_general | solution.py:21
  117.3 1.5 reshape.270
  118.8 1.3 copy.137
  120.1 3.7 %all-to-all-start.2 = ((bf16[16,8,4,1024]{3,1,2,0:T(8,128)(2,1)}), bf16[16,8,4,1024]{3,1,2,0:T(8,128)(2,1)S(1)}, u32[]{:S(2)}, u32[]{:S(2)}) async-start(bf16[16,8,4,1024]{3,1,2,0:T(8,128)(2,1)} %copy.137), calls=%async_computation.2 | async-start | bytes 2097152 | tf_op jit(solution)/shard_map/all_to_all | solution.py:175
  124.0 1.0 copy.124.qt_ref
  125.4 0.1 reshape.282
  125.6 26.1 %all-to-all-done.2 = bf16[16,8,4,1024]{3,1,2,0:T(8,128)(2,1)S(1)} async-done(((bf16[16,8,4,1024]{3,1,2,0:T(8,128)(2,1)}), bf16[16,8,4,1024]{3,1,2,0:T(8,128)(2,1)S(1)}, u32[]{:S(2)}, u32[]{:S(2)}) %all-to-all-start.2) | async-done | bytes 1048608 | tf_op jit(solution)/shard_map/all_to_all | solution.py:175
  151.8 1.8 copy.139
  153.6 4.7 %all-to-all-start.3 = ((bf16[4,32,4,1024]{3,2,0,1:T(4,128)(2,1)}), bf16[4,32,4,1024]{3,2,0,1:T(4,128)(2,1)}, u32[]{:S(2)}, u32[]{:S(2)}) async-start(bf16[4,32,4,1024]{3,2,0,1:T(4,128)(2,1)} %copy.139), calls=%async_computation.3 | async-start | bytes 2097152 | tf_op jit(solution)/shard_map/all_to_all | solution.py:177
  158.3 0.2 fusion.23
  158.5 1.9 gather_fusion.1
  160.8 4.0 %slice_bitcast_fusion = (bf16[2,128,4096]{2,1,0:T(8,128)(2,1)}, bf16[2,4096,128]{1,2,0:T(8,128)(2,1)S(1)}) fusion(bf16[2,2,4096,128]{2,3,1,0:T(8,128)(2,1)} %all-gather.2.cloned.1.call-done), kind=kLoop, calls=%fused_computation.5 | loop fusion | bytes 8388608 | tf_op jit(solution)/shard_map/transpose | solution.py:85
  164.8 2.4 %copy.125.k_ref = bf16[2,4096,128]{2,1,0:T(8,128)(2,1)} copy(bf16[2,4096,128]{1,2,0:T(8,128)(2,1)S(1)} %get-tuple-element.7) | data formatting | bytes 4194304 | tf_op jit(solution)/shard_map/squeeze | solution.py:84
  167.2 3.6 %shard_map.113 = bf16[2,128,1024]{2,1,0:T(8,128)(2,1)} custom-call(s32[1]{0:T(128)} %bitcast.c_ref, bf16[2,128,1024]{2,1,0:T(8,128)(2,1)} %copy.124.qt_ref, bf16[2,4096,128]{2,1,0:T(8,128)(2,1)} %copy.125.k_ref, bf16[2,128,4096]{2,1,0:T(8,128)(2,1)} %get-tuple-element.6.vt_ref), custom_call_target="tpu_custom_call" | custom-call | flops 2147483648 | bytes 5242880 | tf_op jit(solution)/shard_map/pallas_call | solution.py:88
  170.8 1.3 copy.126
  172.2 0.9 copy_bitcast_fusion
  173.0 12.4 %all-to-all-done.3 = bf16[4,32,4,1024]{3,2,0,1:T(4,128)(2,1)} async-done(((bf16[4,32,4,1024]{3,2,0,1:T(4,128)(2,1)}), bf16[4,32,4,1024]{3,2,0,1:T(4,128)(2,1)}, u32[]{:S(2)}, u32[]{:S(2)}) %all-to-all-start.3) | async-done | bytes 1048608 | tf_op jit(solution)/shard_map/all_to_all | solution.py:177
  185.5 1.6 copy.142
  187.1 0.3 reshape.272
  187.4 1.2 gather_fusion
  188.6 0.2 gather.11
  188.8 2.3 %multiply_reduce_fusion = bf16[128,1024]{1,0:T(8,128)(2,1)} fusion(bf16[128,2,1024]{2,1,0:T(2,128)(2,1)S(1)} %gather.11, pred[128,2]{1,0:T(8,128)(4,1)S(1)} %copy.141, f32[128,2]{1,0:T(8,128)S(1)} %copy.145), kind=kLoop, calls=%fused_computation.16 | loop fusion | flops 917504 | bytes 787712 | tf_op jit(solution)/shard_map/reduce_sum | solution.py:183
  (50 shorter events, 1.9 us)
Async XLA Ops:
  7.2 116.8 %copy-start = (bf16[1,128,16,128]{3,2,1,0:T(8,128)(2,1)S(1)}, bf16[1,128,16,128]{3,2,1,0:T(8,128)(2,1)}, u32[]{:S(2)}) copy-start(bf16[1,128,16,128]{3,2,1,0:T(8,128)(2,1)} %param.11) | copy-start | bytes 1572868
  7.2 9.2 %copy-start.7 = (s32[1,128,2]{1,2,0:T(2,128)S(1)}, s32[1,128,2]{1,2,0:T(2,128)}, u32[]{:S(2)}) copy-start(s32[1,128,2]{1,2,0:T(2,128)} %param.14) | copy-start | bytes 3076
  7.2 9.8 %copy-start.5 = (bf16[1,128,1024]{2,1,0:T(8,128)(2,1)S(1)}, bf16[1,128,1024]{2,1,0:T(8,128)(2,1)}, u32[]{:S(2)}) copy-start(bf16[1,128,1024]{2,1,0:T(8,128)(2,1)} %param.10) | copy-start | bytes 786436
  7.2 10.3 %copy-start.8 = (bf16[1024]{0:T(1024)(128)(2,1)S(1)}, bf16[1024]{0:T(1024)(128)(2,1)}, u32[]{:S(2)}) copy-start(bf16[1024]{0:T(1024)(128)(2,1)} %param.15) | copy-start | bytes 6148
  7.2 153.6 %all-gather.2.cloned.1.call-start = ((), (), s32[]{:S(2)}) async-start(), calls=%async_computation.4 | async-start | bytes 4325376 | tf_op jit(solution)/shard_map/all_gather | solution.py:83
  12.4 25.6 %collective-permute-start = (bf16[3,192,1024]{2,1,0:T(8,128)(2,1)}, bf16[3,192,1024]{2,1,0:T(8,128)(2,1)S(1)}, u32[]{:S(2)}, u32[]{:S(2)}) collective-permute-start(bf16[3,192,1024]{2,1,0:T(8,128)(2,1)} %pad_maximum_fusion.2), channel_id=1, source_target_pairs={{0,2},{1,3},{2,0},{3,1},{4,6},{5,7},{6,4},{7,5},{8,10},{9,11},{10,... | collective-permute-start | bytes 3538952 | tf_op jit(solution)/shard_map/ppermute | solution.py:13
  17.7 0.7 copy-start.3
  22.2 15.8 %copy-start.1 = (bf16[192,1024]{1,0:T(8,128)(2,1)S(1)}, bf16[192,1024]{1,0:T(8,128)(2,1)}, u32[]{:S(2)}) copy-start(bf16[192,1024]{1,0:T(8,128)(2,1)} %param.19) | copy-start | bytes 1179652
  22.2 15.8 %copy-start.2 = (bf16[192,1024]{1,0:T(8,128)(2,1)S(1)}, bf16[192,1024]{1,0:T(8,128)(2,1)}, u32[]{:S(2)}) copy-start(bf16[192,1024]{1,0:T(8,128)(2,1)} %param.18) | copy-start | bytes 1179652
  25.0 44.0 %all-to-all-start = ((bf16[4,32,4,1024]{3,2,0,1:T(4,128)(2,1)}), bf16[4,32,4,1024]{3,2,0,1:T(4,128)(2,1)S(1)}, u32[]{:S(2)}, u32[]{:S(2)}) async-start(bf16[4,32,4,1024]{3,2,0,1:T(4,128)(2,1)} %copy.133), calls=%async_computation | async-start | bytes 2097152 | tf_op jit(solution)/shard_map/all_to_all | solution.py:169
  40.6 38.3 %collective-permute-start.1 = (bf16[3,384,1024]{2,1,0:T(8,128)(2,1)}, bf16[3,384,1024]{2,1,0:T(8,128)(2,1)}, u32[]{:S(2)}, u32[]{:S(2)}) collective-permute-start(bf16[3,384,1024]{2,1,0:T(8,128)(2,1)} %pad_maximum_fusion.1), channel_id=1, source_target_pairs={{0,1},{1,0},{2,3},{3,2},{4,5},{5,4},{6,7},{7,6},{8,9},{9,8},{10,11... | collective-permute-start | bytes 7077896 | tf_op jit(solution)/shard_map/ppermute | solution.py:13
  70.7 36.2 %all-to-all-start.1 = ((bf16[16,8,4,1024]{3,1,2,0:T(8,128)(2,1)}), bf16[16,8,4,1024]{3,1,2,0:T(8,128)(2,1)S(1)}, u32[]{:S(2)}, u32[]{:S(2)}) async-start(bf16[16,8,4,1024]{3,1,2,0:T(8,128)(2,1)} %copy.135), calls=%async_computation.1 | async-start | bytes 2097152 | tf_op jit(solution)/shard_map/all_to_all | solution.py:172
  120.1 31.6 %all-to-all-start.2 = ((bf16[16,8,4,1024]{3,1,2,0:T(8,128)(2,1)}), bf16[16,8,4,1024]{3,1,2,0:T(8,128)(2,1)S(1)}, u32[]{:S(2)}, u32[]{:S(2)}) async-start(bf16[16,8,4,1024]{3,1,2,0:T(8,128)(2,1)} %copy.137), calls=%async_computation.2 | async-start | bytes 2097152 | tf_op jit(solution)/shard_map/all_to_all | solution.py:175
  151.8 6.5 %copy-start.4 = (bf16[128,1024]{1,0:T(8,128)(2,1)S(1)}, bf16[128,1024]{1,0:T(8,128)(2,1)}, u32[]{:S(2)}) copy-start(bf16[128,1024]{1,0:T(8,128)(2,1)} %copy-done.3) | copy-start | bytes 786436
  151.8 6.5 %copy-start.6 = (bf16[1024,128]{1,0:T(8,128)(2,1)S(1)}, bf16[1024,128]{1,0:T(8,128)(2,1)}, u32[]{:S(2)}) copy-start(bf16[1024,128]{1,0:T(8,128)(2,1)} %param.16) | copy-start | bytes 786436
  153.6 31.9 %all-to-all-start.3 = ((bf16[4,32,4,1024]{3,2,0,1:T(4,128)(2,1)}), bf16[4,32,4,1024]{3,2,0,1:T(4,128)(2,1)}, u32[]{:S(2)}, u32[]{:S(2)}) async-start(bf16[4,32,4,1024]{3,2,0,1:T(4,128)(2,1)} %copy.139), calls=%async_computation.3 | async-start | bytes 2097152 | tf_op jit(solution)/shard_map/all_to_all | solution.py:177
Sparse Core Ops, SparseCore 0:
  11.1 102.5 all-gather.1

commit v4 on v3

--- a/solution.py
+++ b/solution.py
@@ -160,21 +160,15 @@
     )
     earlier = jnp.cumsum(onehot, axis=0) - onehot
     slot_index = jnp.sum(earlier * onehot, axis=1)
-    target = (flat_ids % per_ctx * ctx_count + flat_ids // per_ctx) * capacity + slot_index
+    target = flat_ids * capacity + slot_index
     source_rows = jnp.repeat(normed, top_count, axis=0)
     outgoing = (
         jnp.zeros((expert_total * capacity, features), jnp.bfloat16).at[target].set(source_rows)
     )
-    outgoing = outgoing.reshape(per_ctx, ctx_count, capacity, features)
-    arrived = lax.all_to_all(outgoing, "ctx", split_axis=1, concat_axis=1, tiled=True)
-    share = ctx_count // quarters
-    to_holders = arrived.reshape(exp_count, share, capacity, features)
-    received = lax.all_to_all(to_holders, "exp", split_axis=0, concat_axis=0, tiled=True)
-    computed = expert_rows(received.reshape(-1, features), held[0], held[1], held[2])
-    computed = computed.astype(jnp.bfloat16).reshape(exp_count, share, capacity, features)
-    returned = lax.all_to_all(computed, "exp", split_axis=0, concat_axis=0, tiled=True)
-    finished = returned.reshape(per_ctx, ctx_count, capacity, features)
-    came_back = lax.all_to_all(finished, "ctx", split_axis=1, concat_axis=1, tiled=True)
+    grid_axes = ("ctx", "exp")
+    received = lax.all_to_all(outgoing, grid_axes, split_axis=0, concat_axis=0, tiled=True)
+    computed = expert_rows(received, held[0], held[1], held[2]).astype(jnp.bfloat16)
+    came_back = lax.all_to_all(computed, grid_axes, split_axis=0, concat_axis=0, tiled=True)
     attended, came_back = lax.optimization_barrier((attended, came_back))
     flat_back = came_back.reshape(expert_total * capacity, features)
     picked = (

time: 199 us -> 214 us (1.075)
  the two profiles are of different devices: /device:TPU:1 before, /device:TPU:455 now
where the time goes in v4:
time: 214 us
  waiting for transfers between devices  46.2 us (22%)
  blocking collectives  44 us (21%)
  local copies, waits for them, and re-layouts  40.2 us (19%)
  starting transfers between devices  23.4 us (11%)
  Pallas kernels  22.3 us (10%)
  other arithmetic  15 us (7%)
  between operations  14.4 us (7%)
  matrix products  8.21 us (4%)
    all_to_all x1, blocking collectives, local(): lax.all_to_all(outgoing, grid_axes, split_axis=0, concat_axis=0, tiled=True)  44 us
    ppermute x2, waiting for transfers between devices, from_partner(): lax.ppermute(value, axis, [(i, i ^ flip) for i in range(lax.axis_size(axi...  24.6 us
    pallas_call x1, Pallas kernels, attention(): pl.pallas_call(functools.partial(_flash_kernel, seq_rows, group_size, sca...  22.3 us
    all_to_all x1, waiting for transfers between devices, local(): lax.all_to_all(computed, grid_axes, split_axis=0, concat_axis=0, tiled=True)  21.6 us
    unnamed x35, local copies, waits for them, and re-layouts  17.3 us
    all_to_all x1, starting transfers between devices, local(): lax.all_to_all(computed, grid_axes, split_axis=0, concat_axis=0, tiled=True)  16.7 us
    ppermute x2, starting transfers between devices, from_partner(): lax.ppermute(value, axis, [(i, i ^ flip) for i in range(lax.axis_size(axi...  6.64 us
    dot_general x1, matrix products, expert_rows(): return jnp.dot(hidden, down_rows, preferred_element_type=jnp.float32)  5.77 us
  transfers between devices with their start and end apart: 4, of which 2 were waited for; matrix products, arithmetic and copies ran while one was open for 21% of the time, Pallas kernels for 0%

profile of v4, /device:TPU:455, one launch (start us, length us, event | category | flops | bytes accessed | tf_op | source)
XLA Modules:
  0.0 213.7 jit_solution(12340740265673644870)
XLA Ops:
  7.3 1.0 copy.77
  8.3 1.0 copy.78
  9.3 0.7 maximum_bitcast_fusion
  10.0 2.5 %pad_maximum_fusion.2 = bf16[3,192,1024]{2,1,0:T(8,128)(2,1)} fusion(bf16[1,192,1024]{2,1,0:T(8,128)(2,1)} %bitcast.97, bf16[1,192,1024]{2,1,0:T(8,128)(2,1)} %bitcast.100, bf16[1,192,1024]{2,1,0:T(8,128)(2,1)} %bitcast.103), kind=kLoop, calls=%fused_computation.16 | loop fusion | flops 1179648 | bytes 2359296 | tf_op jit(solution)/shard_map/stack | solution.py:141
  12.5 3.2 %collective-permute-start = (bf16[3,192,1024]{2,1,0:T(8,128)(2,1)}, bf16[3,192,1024]{2,1,0:T(8,128)(2,1)S(1)}, u32[]{:S(2)}, u32[]{:S(2)}) collective-permute-start(bf16[3,192,1024]{2,1,0:T(8,128)(2,1)} %pad_maximum_fusion.2), channel_id=1, source_target_pairs={{0,2},{1,3},{2,0},{3,1},{4,6},{5,7},{6,4},{7,5},{8,10},{9,11},{10,... | collective-permute-start | bytes 3538952 | tf_op jit(solution)/shard_map/ppermute | solution.py:13
  15.8 0.1 eq.31
  15.9 0.1 eq.27
  16.2 0.2 fusion.20
  16.5 0.1 fusion.12
  16.7 0.1 fusion.14
  16.8 24.6 %collective-permute-done = bf16[3,192,1024]{2,1,0:T(8,128)(2,1)S(1)} collective-permute-done((bf16[3,192,1024]{2,1,0:T(8,128)(2,1)}, bf16[3,192,1024]{2,1,0:T(8,128)(2,1)S(1)}, u32[]{:S(2)}, u32[]{:S(2)}) %collective-permute-start) | collective-permute-done | bytes 1179680 | tf_op jit(solution)/shard_map/ppermute | solution.py:13
  41.4 1.6 pad_maximum_fusion.1
  43.0 3.4 %collective-permute-start.1 = (bf16[3,384,1024]{2,1,0:T(8,128)(2,1)}, bf16[3,384,1024]{2,1,0:T(8,128)(2,1)}, u32[]{:S(2)}, u32[]{:S(2)}) collective-permute-start(bf16[3,384,1024]{2,1,0:T(8,128)(2,1)} %pad_maximum_fusion.1), channel_id=1, source_target_pairs={{0,1},{1,0},{2,3},{3,2},{4,5},{5,4},{6,7},{7,6},{8,9},{9,8},{10,11... | collective-permute-start | bytes 7077896 | tf_op jit(solution)/shard_map/ppermute | solution.py:13
  46.5 0.2 fusion.22
  46.8 0.1 mul.62
  46.9 1.1 broadcast_in_dim.27
  48.0 2.1 reshape.180
  50.1 2.4 %scatter_custom_fusion = bf16[512,1024]{1,0:T(8,128)(2,1)S(1)} fusion(s32[256]{0:T(256)S(1)} %bitcast.111, bf16[256,1024]{1,0:T(8,128)(2,1)} %reshape.180, bf16[]{:T(256)} %constant.29.clone.1), kind=kCustom, calls=%fused_computation.30 | custom fusion | bytes 1049088 | tf_op jit(solution)/shard_map/scatter | solution.py:166
  52.5 0.5 broadcast.151
  53.0 2.2 %reduce = bf16[512,1024]{1,0:T(8,128)(2,1)} reduce(bf16[512,1,1024]{2,0,1:T(8,128)(2,1)S(1)} %bitcast.96, bf16[]{:T(256)} %broadcast.151), dimensions={1}, to_apply=%copy.88.reduce_sub_computation | reduce | bytes 2097154 | tf_op jit(solution)/shard_map/all_to_all | solution.py:169
  55.2 2.7 %reshape.186 = bf16[512,2,512]{2,1,0:T(2,128)(2,1)} reshape(bf16[512,1024]{1,0:T(8,128)(2,1)} %reduce) | data formatting | bytes 2097152
  57.8 44.0 %all_to_all.24 = bf16[512,2,512]{2,1,0:T(2,128)(2,1)S(1)} all-to-all(bf16[512,2,512]{2,1,0:T(2,128)(2,1)} %reshape.186), channel_id=1, replica_groups=mesh['ctx'=32,'exp'=16] {'ctx','exp'}, dimensions={0} | all-to-all | bytes 2097152 | tf_op jit(solution)/shard_map/all_to_all | solution.py:169
  101.8 3.4 %reshape.187 = bf16[512,1,1024]{2,1,0:T(2,128)(2,1)} reshape(bf16[512,2,512]{2,1,0:T(2,128)(2,1)S(1)} %all_to_all.24) | data formatting | bytes 2097152
  105.2 2.3 %pad_maximum_fusion = bf16[3,768,1024]{2,1,0:T(8,128)(2,1)S(1)} fusion(bf16[3,384,1024]{2,1,0:T(8,128)(2,1)} %collective-permute-done.1, bf16[3,192,1024]{2,1,0:T(8,128)(2,1)S(1)} %collective-permute-done, bf16[1,192,1024]{2,1,0:T(8,128)(2,1)S(1)} %bitcast.99, bf16[1,192,1024]{2,1,0:T(8,128)(2,1)S(1)} %bitcast.102, bf16[1,192,1024]{2,1,0:T(8,128)(2,1)} %bitcast.104), kind=kLoop, calls=%fused_computation.3 | loop fusion | flops 23592960 | bytes 9437184 | tf_op jit(solution)/shard_map/concatenate | solution.py:145
  107.5 2.1 copy-done.1
  109.6 2.2 %fusion.2 = f32[512,768]{1,0:T(8,128)} fusion(bf16[3,768,1024]{2,1,0:T(8,128)(2,1)S(1)} %pad_maximum_fusion, bf16[512,1,1024]{2,1,0:T(2,128)(2,1)S(1)} %copy-done.7), kind=kOutput, calls=%fused_computation.12 | convolution fusion | flops 805306368 | bytes 5242880 | tf_op jit(solution)/shard_map/dot_general | solution.py:18
  111.8 5.8 %fusion.4 = bf16[512,1,1024]{2,0,1:T(8,128)(2,1)} fusion(bf16[3,768,1024]{2,1,0:T(8,128)(2,1)} %copy-done.1, f32[512,768]{1,0:T(8,128)} %fusion.2, bf16[512,1,1024]{2,1,0:T(2,128)(2,1)S(1)} %copy-done.8), kind=kOutput, calls=%fused_computation.15 | convolution fusion | flops 1613496320 | bytes 6815744 | tf_op jit(solution)/shard_map/dot_general | solution.py:21
  117.6 2.7 %reduce.1 = bf16[512,1024]{1,0:T(8,128)(2,1)S(1)} reduce(bf16[512,1,1024]{2,0,1:T(8,128)(2,1)} %fusion.4, bf16[]{:T(256)} %broadcast.151), dimensions={1}, to_apply=%copy.89.reduce_sub_computation | reduce | bytes 2097154 | tf_op jit(solution)/shard_map/all_to_all | solution.py:171
  120.3 1.6 reshape.188
  121.9 16.7 %all-to-all-start.1 = ((bf16[512,2,512]{2,1,0:T(2,128)(2,1)}), bf16[512,2,512]{2,1,0:T(2,128)(2,1)S(1)}, u32[]{:S(2)}, u32[]{:S(2)}) async-start(bf16[512,2,512]{2,1,0:T(2,128)(2,1)} %reshape.188), calls=%async_computation.1 | async-start | bytes 2097152 | tf_op jit(solution)/shard_map/all_to_all | solution.py:171
  138.6 0.1 reduce_sum.34
  138.8 1.0 copy.79.qt_ref
  139.9 0.1 copy.91
  140.2 0.1 reshape.170
  140.4 0.2 fusion.31
  140.6 1.9 gather_fusion.1
  142.5 0.1 reshape.173
  142.9 21.6 %all-to-all-done.1 = bf16[512,2,512]{2,1,0:T(2,128)(2,1)S(1)} async-done(((bf16[512,2,512]{2,1,0:T(2,128)(2,1)}), bf16[512,2,512]{2,1,0:T(2,128)(2,1)S(1)}, u32[]{:S(2)}, u32[]{:S(2)}) %all-to-all-start.1) | async-done | bytes 1048608 | tf_op jit(solution)/shard_map/all_to_all | solution.py:171
  164.5 3.3 %reshape.189 = bf16[512,1,1024]{2,1,0:T(2,128)(2,1)} reshape(bf16[512,2,512]{2,1,0:T(2,128)(2,1)S(1)} %all-to-all-done.1) | data formatting | bytes 2097152
  167.8 2.0 copy.109
  169.8 4.7 %slice_bitcast_fusion = (bf16[2,128,4096]{2,1,0:T(8,128)(2,1)}, bf16[2,4096,128]{1,2,0:T(8,128)(2,1)}) fusion(bf16[2,2,4096,128]{2,3,1,0:T(8,128)(2,1)} %all-gather.2.cloned.1.call-done), kind=kLoop, calls=%fused_computation.5 | loop fusion | bytes 8388608 | tf_op jit(solution)/shard_map/transpose | solution.py:85
  174.5 4.1 %copy.80.k_ref = bf16[2,4096,128]{2,1,0:T(8,128)(2,1)} copy(bf16[2,4096,128]{1,2,0:T(8,128)(2,1)} %get-tuple-element.7) | data formatting | bytes 4194304 | tf_op jit(solution)/shard_map/squeeze | solution.py:84
  178.6 22.3 %shard_map.113 = bf16[2,128,1024]{2,1,0:T(8,128)(2,1)} custom-call(s32[1]{0:T(128)} %bitcast.c_ref, bf16[2,128,1024]{2,1,0:T(8,128)(2,1)} %copy.79.qt_ref, bf16[2,4096,128]{2,1,0:T(8,128)(2,1)} %copy.80.k_ref, bf16[2,128,4096]{2,1,0:T(8,128)(2,1)} %get-tuple-element.6.vt_ref), custom_call_target="tpu_custom_call" | custom-call | flops 2147483648 | bytes 5242880 | tf_op jit(solution)/shard_map/pallas_call | solution.py:88
  200.9 1.3 copy.81
  202.2 0.9 copy_bitcast_fusion.1
  203.1 1.2 gather_fusion
  204.3 0.2 gather.11
  204.5 2.3 %multiply_reduce_fusion = bf16[128,1024]{1,0:T(8,128)(2,1)} fusion(bf16[128,2,1024]{2,1,0:T(2,128)(2,1)S(1)} %gather.11, pred[128,2]{1,0:T(8,128)(4,1)S(1)} %copy.91, f32[128,2]{1,0:T(8,128)S(1)} %copy.94), kind=kLoop, calls=%fused_computation.20 | loop fusion | flops 917504 | bytes 787712 | tf_op jit(solution)/shard_map/reduce_sum | solution.py:177
  (51 shorter events, 1.0 us)
Async XLA Ops:
  7.2 131.6 %copy-start = (bf16[1,128,16,128]{3,2,1,0:T(8,128)(2,1)S(1)}, bf16[1,128,16,128]{3,2,1,0:T(8,128)(2,1)}, u32[]{:S(2)}) copy-start(bf16[1,128,16,128]{3,2,1,0:T(8,128)(2,1)} %param.11) | copy-start | bytes 1572868
  7.2 8.5 %copy-start.11 = (s32[1,128,2]{1,2,0:T(2,128)S(1)}, s32[1,128,2]{1,2,0:T(2,128)}, u32[]{:S(2)}) copy-start(s32[1,128,2]{1,2,0:T(2,128)} %param.14) | copy-start | bytes 3076
  7.2 9.3 %copy-start.12 = (bf16[1024]{0:T(1024)(128)(2,1)S(1)}, bf16[1024]{0:T(1024)(128)(2,1)}, u32[]{:S(2)}) copy-start(bf16[1024]{0:T(1024)(128)(2,1)} %param.15) | copy-start | bytes 6148
  7.2 9.3 %copy-start.9 = (bf16[1,128,1024]{2,1,0:T(8,128)(2,1)S(1)}, bf16[1,128,1024]{2,1,0:T(8,128)(2,1)}, u32[]{:S(2)}) copy-start(bf16[1,128,1024]{2,1,0:T(8,128)(2,1)} %param.10) | copy-start | bytes 786436
  7.2 162.6 %all-gather.2.cloned.1.call-start = ((), (), s32[]{:S(2)}) async-start(), calls=%async_computation.2 | async-start | bytes 4325376 | tf_op jit(solution)/shard_map/all_gather | solution.py:83
  10.0 31.4 %copy-start.2 = (bf16[192,1024]{1,0:T(8,128)(2,1)S(1)}, bf16[192,1024]{1,0:T(8,128)(2,1)}, u32[]{:S(2)}) copy-start(bf16[192,1024]{1,0:T(8,128)(2,1)} %param.19) | copy-start | bytes 1179652
  10.0 31.4 %copy-start.3 = (bf16[192,1024]{1,0:T(8,128)(2,1)S(1)}, bf16[192,1024]{1,0:T(8,128)(2,1)}, u32[]{:S(2)}) copy-start(bf16[192,1024]{1,0:T(8,128)(2,1)} %param.18) | copy-start | bytes 1179652
  10.0 31.4 %copy-start.4 = (bf16[192,1024]{1,0:T(8,128)(2,1)S(1)}, bf16[192,1024]{1,0:T(8,128)(2,1)}, u32[]{:S(2)}) copy-start(bf16[192,1024]{1,0:T(8,128)(2,1)} %param.17) | copy-start | bytes 1179652
  12.5 28.9 %collective-permute-start = (bf16[3,192,1024]{2,1,0:T(8,128)(2,1)}, bf16[3,192,1024]{2,1,0:T(8,128)(2,1)S(1)}, u32[]{:S(2)}, u32[]{:S(2)}) collective-permute-start(bf16[3,192,1024]{2,1,0:T(8,128)(2,1)} %pad_maximum_fusion.2), channel_id=1, source_target_pairs={{0,2},{1,3},{2,0},{3,1},{4,6},{5,7},{6,4},{7,5},{8,10},{9,11},{10,... | collective-permute-start | bytes 3538952 | tf_op jit(solution)/shard_map/ppermute | solution.py:13
  16.8 30.1 %copy-start.5 = (bf16[128,1024]{1,0:T(8,128)(2,1)}, bf16[128,1024]{1,0:T(8,128)(2,1)S(1)}, u32[]{:S(2)}) copy-start(bf16[128,1024]{1,0:T(8,128)(2,1)S(1)} %fusion.14) | copy-start | bytes 786436
  43.0 62.2 %collective-permute-start.1 = (bf16[3,384,1024]{2,1,0:T(8,128)(2,1)}, bf16[3,384,1024]{2,1,0:T(8,128)(2,1)}, u32[]{:S(2)}, u32[]{:S(2)}) collective-permute-start(bf16[3,384,1024]{2,1,0:T(8,128)(2,1)} %pad_maximum_fusion.1), channel_id=1, source_target_pairs={{0,1},{1,0},{2,3},{3,2},{4,5},{5,4},{6,7},{7,6},{8,9},{9,8},{10,11... | collective-permute-start | bytes 7077896 | tf_op jit(solution)/shard_map/ppermute | solution.py:13
  105.2 4.4 %copy-start.7 = (bf16[512,1,1024]{2,1,0:T(2,128)(2,1)S(1)}, bf16[512,1,1024]{2,1,0:T(2,128)(2,1)}, u32[]{:S(2)}) copy-start(bf16[512,1,1024]{2,1,0:T(2,128)(2,1)} %reshape.187) | copy-start | bytes 3145732
  107.5 2.1 copy-start.1
  109.6 2.2 %copy-start.8 = (bf16[512,1,1024]{2,1,0:T(2,128)(2,1)S(1)}, bf16[512,1,1024]{2,1,0:T(2,128)(2,1)}, u32[]{:S(2)}) copy-start(bf16[512,1,1024]{2,1,0:T(2,128)(2,1)} %reshape.187) | copy-start | bytes 3145732
  121.9 18.5 %copy-start.6 = (bf16[128,1024]{1,0:T(8,128)(2,1)S(1)}, bf16[128,1024]{1,0:T(8,128)(2,1)}, u32[]{:S(2)}) copy-start(bf16[128,1024]{1,0:T(8,128)(2,1)} %copy-done.5) | copy-start | bytes 786436
  121.9 18.5 %copy-start.10 = (bf16[1024,128]{1,0:T(8,128)(2,1)S(1)}, bf16[1024,128]{1,0:T(8,128)(2,1)}, u32[]{:S(2)}) copy-start(bf16[1024,128]{1,0:T(8,128)(2,1)} %param.16) | copy-start | bytes 786436
  121.9 42.6 %all-to-all-start.1 = ((bf16[512,2,512]{2,1,0:T(2,128)(2,1)}), bf16[512,2,512]{2,1,0:T(2,128)(2,1)S(1)}, u32[]{:S(2)}, u32[]{:S(2)}) async-start(bf16[512,2,512]{2,1,0:T(2,128)(2,1)} %reshape.188), calls=%async_computation.1 | async-start | bytes 2097152 | tf_op jit(solution)/shard_map/all_to_all | solution.py:171
Sparse Core Ops, SparseCore 0:
  11.1 106.0 all-gather.1

commit v5 on v4

--- a/solution.py
+++ b/solution.py
@@ -65,11 +65,17 @@
     o_ref[0] = (acc_sc[...] / l_sc[...]).astype(o_ref.dtype)
 
 
-def attention(queries, key_rows, value_rows):
+def gather_attention_inputs(queries, key_rows, value_rows):
+    local_kv = jnp.stack([key_rows[0], value_rows[0]], axis=0).transpose(0, 2, 1, 3)
+    gathered = lax.all_gather(local_kv, "ctx", axis=2, tiled=True)
+    return queries, gathered
+
+
+def attention(queries, gathered):
     seq_rows = queries.shape[1]
     head_count = queries.shape[2]
     head_size = queries.shape[3]
-    kv_count = key_rows.shape[2]
+    kv_count = gathered.shape[1]
     group_size = head_count // kv_count
     scaling = 1.0 / math.sqrt(head_size)
     width = seq_rows * group_size
@@ -79,8 +85,6 @@
         .transpose(1, 3, 0, 2)
         .reshape(kv_count, head_size, width)
     )
-    local_kv = jnp.stack([key_rows[0], value_rows[0]], axis=0).transpose(0, 2, 1, 3)
-    gathered = lax.all_gather(local_kv, "ctx", axis=2, tiled=True)
     keys_all = gathered[0]
     values_t = gathered[1].transpose(0, 2, 1)
     total_rows = keys_all.shape[1]
@@ -138,13 +142,9 @@
     quarters = exp_count // per_ctx
     capacity = 2 * tokens * top_count // expert_total
 
+    attention_inputs = gather_attention_inputs(queries, key_rows, value_rows)
     stacked = jnp.stack([gate_weight, up_weight, down_weight], axis=0)
     across = from_partner(stacked, "exp", 2)
-    pair = jnp.concatenate([stacked, across], axis=1)
-    beside = from_partner(pair, "exp", 1)
-    held = jnp.concatenate([pair, beside], axis=1)
-
-    attended = attention(queries, key_rows, value_rows)
 
     widened = stream[0].astype(jnp.float32)
     mean_square = jnp.mean(widened * widened, axis=-1, keepdims=True)
@@ -165,9 +165,15 @@
     outgoing = (
         jnp.zeros((expert_total * capacity, features), jnp.bfloat16).at[target].set(source_rows)
     )
+    across, outgoing = lax.optimization_barrier((across, outgoing))
+    pair = jnp.concatenate([stacked, across], axis=1)
+    beside = from_partner(pair, "exp", 1)
+    held = jnp.concatenate([pair, beside], axis=1)
     grid_axes = ("ctx", "exp")
     received = lax.all_to_all(outgoing, grid_axes, split_axis=0, concat_axis=0, tiled=True)
     computed = expert_rows(received, held[0], held[1], held[2]).astype(jnp.bfloat16)
+    attention_inputs, computed = lax.optimization_barrier((attention_inputs, computed))
+    attended = attention(*attention_inputs)
     came_back = lax.all_to_all(computed, grid_axes, split_axis=0, concat_axis=0, tiled=True)
     attended, came_back = lax.optimization_barrier((attended, came_back))
     flat_back = came_back.reshape(expert_total * capacity, features)

time: 214 us -> 204 us (0.953)
  the two profiles are of different devices: /device:TPU:455 before, /device:TPU:1 now
where the time goes in v5:
time: 204 us; the launch traced here: 203 us
  waiting for transfers between devices  64.1 us (31%)
  starting transfers between devices  56 us (27%)
  local copies, waits for them, and re-layouts  40.1 us (20%)
  other arithmetic  16.1 us (8%)
  between operations  14.3 us (7%)
  matrix products  9.14 us (4%)
  Pallas kernels  3.59 us (2%)
    all_to_all x1, waiting for transfers between devices, local(): lax.all_to_all(outgoing, grid_axes, split_axis=0, concat_axis=0, tiled=True)  29.8 us
    all_to_all x1, starting transfers between devices, local(): lax.all_to_all(computed, grid_axes, split_axis=0, concat_axis=0, tiled=True)  23.1 us
    unnamed x25, local copies, waits for them, and re-layouts  21.4 us
    all_to_all x1, starting transfers between devices, local(): lax.all_to_all(outgoing, grid_axes, split_axis=0, concat_axis=0, tiled=True)  20.9 us
    all_to_all x1, waiting for transfers between devices, local(): lax.all_to_all(computed, grid_axes, split_axis=0, concat_axis=0, tiled=True)  18.3 us
    ppermute x2, waiting for transfers between devices, from_partner(): lax.ppermute(value, axis, [(i, i ^ flip) for i in range(lax.axis_size(axi...  15.8 us
    ppermute x2, starting transfers between devices, from_partner(): lax.ppermute(value, axis, [(i, i ^ flip) for i in range(lax.axis_size(axi...  12 us
    dot_general x1, matrix products, expert_rows(): return jnp.dot(hidden, down_rows, preferred_element_type=jnp.float32)  5.75 us
  transfers between devices with their start and end apart: 5, of which 4 were waited for; matrix products, arithmetic and copies ran while one was open for 21% of the time, Pallas kernels for 2%

profile of v5, /device:TPU:1, one launch (start us, length us, event | category | flops | bytes accessed | tf_op | source)
XLA Modules:
  0.0 203.4 jit_solution(13220260979484573966)
XLA Ops:
  7.3 1.0 copy.76
  8.3 1.0 copy.77
  9.3 0.7 maximum_bitcast_fusion
  10.0 2.4 %pad_maximum_fusion.2 = bf16[3,192,1024]{2,1,0:T(8,128)(2,1)} fusion(bf16[1,192,1024]{2,1,0:T(8,128)(2,1)} %bitcast.94, bf16[1,192,1024]{2,1,0:T(8,128)(2,1)} %bitcast.97, bf16[1,192,1024]{2,1,0:T(8,128)(2,1)} %bitcast.100), kind=kLoop, calls=%fused_computation.15 | loop fusion | flops 1179648 | bytes 2359296 | tf_op jit(solution)/shard_map/stack | solution.py:146
  12.3 4.0 %collective-permute-start = (bf16[3,192,1024]{2,1,0:T(8,128)(2,1)}, bf16[3,192,1024]{2,1,0:T(8,128)(2,1)S(1)}, u32[]{:S(2)}, u32[]{:S(2)}) collective-permute-start(bf16[3,192,1024]{2,1,0:T(8,128)(2,1)} %pad_maximum_fusion.2), channel_id=1, source_target_pairs={{0,2},{1,3},{2,0},{3,1},{4,6},{5,7},{6,4},{7,5},{8,10},{9,11},{10,... | collective-permute-start | bytes 3538952 | tf_op jit(solution)/shard_map/ppermute | solution.py:13
  16.5 0.1 eq.31
  16.7 0.2 fusion.19
  17.0 0.1 eq.27
  17.3 0.1 mul.62
  17.6 0.1 fusion.13
  17.8 0.3 broadcast_in_dim.27
  18.1 1.0 reshape.180
  19.1 0.2 fusion.21
  19.3 2.4 %scatter_custom_fusion = bf16[512,1024]{1,0:T(8,128)(2,1)S(1)} fusion(s32[256]{0:T(256)S(1)} %bitcast.109, bf16[256,1024]{1,0:T(8,128)(2,1)} %reshape.180, bf16[]{:T(256)} %constant.29.clone.1), kind=kCustom, calls=%fused_computation.29 | custom fusion | bytes 1049088 | tf_op jit(solution)/shard_map/scatter | solution.py:166
  21.7 15.8 %collective-permute-done = bf16[3,192,1024]{2,1,0:T(8,128)(2,1)S(1)} collective-permute-done((bf16[3,192,1024]{2,1,0:T(8,128)(2,1)}, bf16[3,192,1024]{2,1,0:T(8,128)(2,1)S(1)}, u32[]{:S(2)}, u32[]{:S(2)}) %collective-permute-start) | collective-permute-done | bytes 1179680 | tf_op jit(solution)/shard_map/ppermute | solution.py:13
  37.4 2.7 %pad_maximum_fusion.1 = bf16[3,384,1024]{2,1,0:T(8,128)(2,1)} fusion(bf16[3,192,1024]{2,1,0:T(8,128)(2,1)S(1)} %collective-permute-done, bf16[1,192,1024]{2,1,0:T(8,128)(2,1)S(1)} %bitcast.95, bf16[1,192,1024]{2,1,0:T(8,128)(2,1)} %bitcast.98, bf16[1,192,1024]{2,1,0:T(8,128)(2,1)} %bitcast.101), kind=kLoop, calls=%fused_computation.4 | loop fusion | flops 9437184 | bytes 4718592 | tf_op jit(solution)/shard_map/concatenate | solution.py:169
  40.2 7.9 %collective-permute-start.1 = (bf16[3,384,1024]{2,1,0:T(8,128)(2,1)}, bf16[3,384,1024]{2,1,0:T(8,128)(2,1)}, u32[]{:S(2)}, u32[]{:S(2)}) collective-permute-start(bf16[3,384,1024]{2,1,0:T(8,128)(2,1)} %pad_maximum_fusion.1), channel_id=1, source_target_pairs={{0,1},{1,0},{2,3},{3,2},{4,5},{5,4},{6,7},{7,6},{8,9},{9,8},{10,11... | collective-permute-start | bytes 7077896 | tf_op jit(solution)/shard_map/ppermute | solution.py:13
  48.1 0.5 broadcast.151
  48.6 2.1 %reduce = bf16[512,1024]{1,0:T(8,128)(2,1)} reduce(bf16[512,1,1024]{2,0,1:T(8,128)(2,1)S(1)} %bitcast.93, bf16[]{:T(256)} %broadcast.151), dimensions={1}, to_apply=%copy.83.reduce_sub_computation | reduce | bytes 2097154 | tf_op jit(solution)/shard_map/all_to_all | solution.py:173
  50.8 2.6 %reshape.186 = bf16[512,2,512]{2,1,0:T(2,128)(2,1)} reshape(bf16[512,1024]{1,0:T(8,128)(2,1)} %reduce) | data formatting | bytes 2097152
  53.4 20.9 %all-to-all-start = ((bf16[512,2,512]{2,1,0:T(2,128)(2,1)}), bf16[512,2,512]{2,1,0:T(2,128)(2,1)S(1)}, u32[]{:S(2)}, u32[]{:S(2)}) async-start(bf16[512,2,512]{2,1,0:T(2,128)(2,1)} %reshape.186), calls=%async_computation | async-start | bytes 2097152 | tf_op jit(solution)/shard_map/all_to_all | solution.py:173
  74.6 0.1 copy.91
  74.8 0.1 reshape.170
  75.0 1.2 fusion.30
  76.2 1.9 gather_fusion.1
  78.1 0.1 reshape.173
  78.3 29.8 %all-to-all-done = bf16[512,2,512]{2,1,0:T(2,128)(2,1)S(1)} async-done(((bf16[512,2,512]{2,1,0:T(2,128)(2,1)}), bf16[512,2,512]{2,1,0:T(2,128)(2,1)S(1)}, u32[]{:S(2)}, u32[]{:S(2)}) %all-to-all-start) | async-done | bytes 1048608 | tf_op jit(solution)/shard_map/all_to_all | solution.py:173
  108.1 3.4 %reshape.187 = bf16[512,1,1024]{2,1,0:T(2,128)(2,1)} reshape(bf16[512,2,512]{2,1,0:T(2,128)(2,1)S(1)} %all-to-all-done) | data formatting | bytes 2097152
  111.5 2.4 %pad_maximum_fusion = bf16[3,768,1024]{2,1,0:T(8,128)(2,1)S(1)} fusion(bf16[3,384,1024]{2,1,0:T(8,128)(2,1)} %collective-permute-done.1, bf16[3,192,1024]{2,1,0:T(8,128)(2,1)S(1)} %collective-permute-done, bf16[1,192,1024]{2,1,0:T(8,128)(2,1)S(1)} %bitcast.96, bf16[1,192,1024]{2,1,0:T(8,128)(2,1)} %bitcast.99, bf16[1,192,1024]{2,1,0:T(8,128)(2,1)} %bitcast.102), kind=kLoop, calls=%fused_computation.3 | loop fusion | flops 23592960 | bytes 9437184 | tf_op jit(solution)/shard_map/concatenate | solution.py:171
  113.9 2.1 %copy-done.1 = bf16[3,768,1024]{2,1,0:T(8,128)(2,1)} copy-done((bf16[3,768,1024]{2,1,0:T(8,128)(2,1)}, bf16[3,768,1024]{2,1,0:T(8,128)(2,1)S(1)}, u32[]{:S(2)}) %copy-start.1) | copy-done | bytes 4718616
  116.0 2.2 %fusion.2 = f32[512,768]{1,0:T(8,128)} fusion(bf16[3,768,1024]{2,1,0:T(8,128)(2,1)S(1)} %pad_maximum_fusion, bf16[512,1,1024]{2,1,0:T(2,128)(2,1)S(1)} %copy-done.3), kind=kOutput, calls=%fused_computation.12 | convolution fusion | flops 805306368 | bytes 5242880 | tf_op jit(solution)/shard_map/dot_general | solution.py:18
  118.2 5.8 %fusion.3 = bf16[512,1024]{1,0:T(8,128)(2,1)} fusion(bf16[3,768,1024]{2,1,0:T(8,128)(2,1)} %copy-done.1, f32[512,768]{1,0:T(8,128)} %fusion.2, bf16[512,1,1024]{2,1,0:T(2,128)(2,1)S(1)} %copy-done.4), kind=kOutput, calls=%fused_computation.14 | convolution fusion | flops 1613496320 | bytes 6815744 | tf_op jit(solution)/shard_map/dot_general | solution.py:21
  124.0 0.2 all-gather.2.cloned.1.call-done
  124.2 2.7 %reduce.1 = bf16[512,1024]{1,0:T(8,128)(2,1)S(1)} reduce(bf16[512,1,1024]{2,0,1:T(8,128)(2,1)} %bitcast.103, bf16[]{:T(256)} %broadcast.151), dimensions={1}, to_apply=%copy.89.reduce_sub_computation | reduce | bytes 2097154 | tf_op jit(solution)/shard_map/all_to_all | solution.py:177
  126.9 1.6 reshape.188
  128.5 23.1 %all-to-all-start.1 = ((bf16[512,2,512]{2,1,0:T(2,128)(2,1)}), bf16[512,2,512]{2,1,0:T(2,128)(2,1)}, u32[]{:S(2)}, u32[]{:S(2)}) async-start(bf16[512,2,512]{2,1,0:T(2,128)(2,1)} %reshape.188), calls=%async_computation.1 | async-start | bytes 2097152 | tf_op jit(solution)/shard_map/all_to_all | solution.py:177
  151.7 4.0 %slice_bitcast_fusion = (bf16[2,128,4096]{2,1,0:T(8,128)(2,1)}, bf16[2,4096,128]{1,2,0:T(8,128)(2,1)S(1)}) fusion(bf16[2,2,4096,128]{2,3,1,0:T(8,128)(2,1)} %all-gather.2.cloned.1.call-done), kind=kLoop, calls=%fused_computation.5 | loop fusion | bytes 8388608 | tf_op jit(solution)/shard_map/transpose | solution.py:89
  155.7 2.5 %copy.86.k_ref = bf16[2,4096,128]{2,1,0:T(8,128)(2,1)} copy(bf16[2,4096,128]{1,2,0:T(8,128)(2,1)S(1)} %get-tuple-element.17) | data formatting | bytes 4194304 | tf_op jit(solution)/shard_map/squeeze | solution.py:88
  158.2 1.0 copy.85.qt_ref
  159.2 3.6 %shard_map.113 = bf16[2,128,1024]{2,1,0:T(8,128)(2,1)} custom-call(s32[1]{0:T(128)} %bitcast.c_ref, bf16[2,128,1024]{2,1,0:T(8,128)(2,1)} %copy.85.qt_ref, bf16[2,4096,128]{2,1,0:T(8,128)(2,1)} %copy.86.k_ref, bf16[2,128,4096]{2,1,0:T(8,128)(2,1)} %get-tuple-element.16.vt_ref), custom_call_target="tpu_custom_call" | custom-call | flops 2147483648 | bytes 5242880 | tf_op jit(solution)/shard_map/pallas_call | solution.py:92
  162.8 1.3 copy.87
  164.1 0.9 copy_bitcast_fusion.1
  165.0 18.3 %all-to-all-done.1 = bf16[512,2,512]{2,1,0:T(2,128)(2,1)} async-done(((bf16[512,2,512]{2,1,0:T(2,128)(2,1)}), bf16[512,2,512]{2,1,0:T(2,128)(2,1)}, u32[]{:S(2)}, u32[]{:S(2)}) %all-to-all-start.1) | async-done | bytes 1048608 | tf_op jit(solution)/shard_map/all_to_all | solution.py:177
  183.3 7.5 %reshape.189 = bf16[512,1,1024]{2,1,0:T(2,128)(2,1)} reshape(bf16[512,2,512]{2,1,0:T(2,128)(2,1)} %all-to-all-done.1) | data formatting | bytes 2097152
  190.8 2.0 copy.109
  192.8 1.2 gather_fusion
  194.0 0.2 gather.11
  194.2 2.3 %multiply_reduce_fusion = bf16[128,1024]{1,0:T(8,128)(2,1)} fusion(bf16[128,2,1024]{2,1,0:T(2,128)(2,1)S(1)} %gather.11, pred[128,2]{1,0:T(8,128)(4,1)S(1)} %copy.91, f32[128,2]{1,0:T(8,128)S(1)} %copy.94), kind=kLoop, calls=%fused_computation.19 | loop fusion | flops 917504 | bytes 787712 | tf_op jit(solution)/shard_map/reduce_sum | solution.py:183
  (42 shorter events, 1.2 us)
Async XLA Ops:
  7.2 151.0 %copy-start = (bf16[1,128,16,128]{3,2,1,0:T(8,128)(2,1)S(1)}, bf16[1,128,16,128]{3,2,1,0:T(8,128)(2,1)}, u32[]{:S(2)}) copy-start(bf16[1,128,16,128]{3,2,1,0:T(8,128)(2,1)} %param.11) | copy-start | bytes 1572868
  7.2 9.2 %copy-start.6 = (s32[1,128,2]{1,2,0:T(2,128)S(1)}, s32[1,128,2]{1,2,0:T(2,128)}, u32[]{:S(2)}) copy-start(s32[1,128,2]{1,2,0:T(2,128)} %param.14) | copy-start | bytes 3076
  7.2 10.3 %copy-start.7 = (bf16[1024]{0:T(1024)(128)(2,1)S(1)}, bf16[1024]{0:T(1024)(128)(2,1)}, u32[]{:S(2)}) copy-start(bf16[1024]{0:T(1024)(128)(2,1)} %param.15) | copy-start | bytes 6148
  7.2 10.3 %copy-start.5 = (bf16[1,128,1024]{2,1,0:T(8,128)(2,1)S(1)}, bf16[1,128,1024]{2,1,0:T(8,128)(2,1)}, u32[]{:S(2)}) copy-start(bf16[1,128,1024]{2,1,0:T(8,128)(2,1)} %param.10) | copy-start | bytes 786436
  7.2 117.0 %all-gather.2.cloned.1.call-start = ((), (), s32[]{:S(2)}) async-start(), calls=%async_computation.2 | async-start | bytes 4325376 | tf_op jit(solution)/shard_map/all_gather | solution.py:70
  12.3 25.1 %collective-permute-start = (bf16[3,192,1024]{2,1,0:T(8,128)(2,1)}, bf16[3,192,1024]{2,1,0:T(8,128)(2,1)S(1)}, u32[]{:S(2)}, u32[]{:S(2)}) collective-permute-start(bf16[3,192,1024]{2,1,0:T(8,128)(2,1)} %pad_maximum_fusion.2), channel_id=1, source_target_pairs={{0,2},{1,3},{2,0},{3,1},{4,6},{5,7},{6,4},{7,5},{8,10},{9,11},{10,... | collective-permute-start | bytes 3538952 | tf_op jit(solution)/shard_map/ppermute | solution.py:13
  17.2 20.3 %copy-start.2 = (bf16[192,1024]{1,0:T(8,128)(2,1)S(1)}, bf16[192,1024]{1,0:T(8,128)(2,1)}, u32[]{:S(2)}) copy-start(bf16[192,1024]{1,0:T(8,128)(2,1)} %param.19) | copy-start | bytes 1179652
  40.2 71.3 %collective-permute-start.1 = (bf16[3,384,1024]{2,1,0:T(8,128)(2,1)}, bf16[3,384,1024]{2,1,0:T(8,128)(2,1)}, u32[]{:S(2)}, u32[]{:S(2)}) collective-permute-start(bf16[3,384,1024]{2,1,0:T(8,128)(2,1)} %pad_maximum_fusion.1), channel_id=1, source_target_pairs={{0,1},{1,0},{2,3},{3,2},{4,5},{5,4},{6,7},{7,6},{8,9},{9,8},{10,11... | collective-permute-start | bytes 7077896 | tf_op jit(solution)/shard_map/ppermute | solution.py:13
  53.4 54.7 %all-to-all-start = ((bf16[512,2,512]{2,1,0:T(2,128)(2,1)}), bf16[512,2,512]{2,1,0:T(2,128)(2,1)S(1)}, u32[]{:S(2)}, u32[]{:S(2)}) async-start(bf16[512,2,512]{2,1,0:T(2,128)(2,1)} %reshape.186), calls=%async_computation | async-start | bytes 2097152 | tf_op jit(solution)/shard_map/all_to_all | solution.py:173
  111.5 4.5 %copy-start.3 = (bf16[512,1,1024]{2,1,0:T(2,128)(2,1)S(1)}, bf16[512,1,1024]{2,1,0:T(2,128)(2,1)}, u32[]{:S(2)}) copy-start(bf16[512,1,1024]{2,1,0:T(2,128)(2,1)} %reshape.187) | copy-start | bytes 3145732
  113.9 2.1 %copy-start.1 = (bf16[3,768,1024]{2,1,0:T(8,128)(2,1)}, bf16[3,768,1024]{2,1,0:T(8,128)(2,1)S(1)}, u32[]{:S(2)}) copy-start(bf16[3,768,1024]{2,1,0:T(8,128)(2,1)S(1)} %pad_maximum_fusion) | copy-start | bytes 14155780
  116.0 2.2 %copy-start.4 = (bf16[512,1,1024]{2,1,0:T(2,128)(2,1)S(1)}, bf16[512,1,1024]{2,1,0:T(2,128)(2,1)}, u32[]{:S(2)}) copy-start(bf16[512,1,1024]{2,1,0:T(2,128)(2,1)} %reshape.187) | copy-start | bytes 3145732
  128.5 54.8 %all-to-all-start.1 = ((bf16[512,2,512]{2,1,0:T(2,128)(2,1)}), bf16[512,2,512]{2,1,0:T(2,128)(2,1)}, u32[]{:S(2)}, u32[]{:S(2)}) async-start(bf16[512,2,512]{2,1,0:T(2,128)(2,1)} %reshape.188), calls=%async_computation.1 | async-start | bytes 2097152 | tf_op jit(solution)/shard_map/all_to_all | solution.py:177
Sparse Core Ops, SparseCore 0:
  11.7 112.4 all-gather.1

commit v6 on v5

--- a/solution.py
+++ b/solution.py
@@ -145,6 +145,7 @@
     attention_inputs = gather_attention_inputs(queries, key_rows, value_rows)
     stacked = jnp.stack([gate_weight, up_weight, down_weight], axis=0)
     across = from_partner(stacked, "exp", 2)
+    own_beside = from_partner(stacked, "exp", 1)
 
     widened = stream[0].astype(jnp.float32)
     mean_square = jnp.mean(widened * widened, axis=-1, keepdims=True)
@@ -161,17 +162,18 @@
     earlier = jnp.cumsum(onehot, axis=0) - onehot
     slot_index = jnp.sum(earlier * onehot, axis=1)
     target = flat_ids * capacity + slot_index
-    source_rows = jnp.repeat(normed, top_count, axis=0)
-    outgoing = (
-        jnp.zeros((expert_total * capacity, features), jnp.bfloat16).at[target].set(source_rows)
-    )
-    across, outgoing = lax.optimization_barrier((across, outgoing))
-    pair = jnp.concatenate([stacked, across], axis=1)
-    beside = from_partner(pair, "exp", 1)
-    held = jnp.concatenate([pair, beside], axis=1)
+    tile_rows = 8
+    tile = (tile_rows, features // tile_rows)
+    source_rows = jnp.repeat(normed, top_count, axis=0).reshape(-1, *tile)
+    outgoing = jnp.zeros((expert_total * capacity, *tile), jnp.bfloat16).at[target].set(source_rows)
     grid_axes = ("ctx", "exp")
     received = lax.all_to_all(outgoing, grid_axes, split_axis=0, concat_axis=0, tiled=True)
+    across, received = lax.optimization_barrier((across, received))
+    across_beside = from_partner(across, "exp", 1)
+    held = jnp.concatenate([stacked, across, own_beside, across_beside], axis=1)
+    received = received.reshape(-1, features)
     computed = expert_rows(received, held[0], held[1], held[2]).astype(jnp.bfloat16)
+    computed = computed.reshape(-1, *tile)
     attention_inputs, computed = lax.optimization_barrier((attention_inputs, computed))
     attended = attention(*attention_inputs)
     came_back = lax.all_to_all(computed, grid_axes, split_axis=0, concat_axis=0, tiled=True)

time: 204 us -> 194 us (0.951)
  waiting for transfers between devices: 64.1 us -> 53.2 us
  local copies, waits for them, and re-layouts: 40.1 us -> 48.2 us
  other arithmetic: 16.1 us -> 11.1 us
  matrix products: 9.14 us -> 7.03 us
    all_to_all x1, waiting for transfers between devices: 29.8 us -> 0.01 us  [local(): lax.all_to_all(outgoing, grid_axes, split_axis=0, concat_axis=0, tiled=True)]
    scatter x1, local copies, waits for them, and re-layouts: 2.42 us -> 24.3 us  [local(): jnp.zeros((expert_total * capacity, *tile), jnp.bfloat16).at[target]]
    ppermute x2 -> x3, waiting for transfers between devices: 15.8 us -> 34.9 us  [from_partner(): lax.ppermute(value, axis, [(i, i ^ flip) for i in range(lax.axis_size(axi...]
    unnamed x25 -> x22, local copies, waits for them, and re-layouts: 21.4 us -> 7.71 us
    all_to_all x2 -> x0, other arithmetic: 4.8 us -> none  [the longest x1 2.68 us: local(): lax.all_to_all(computed, grid_axes, split_axis=0, concat_axis=0, tiled=True)]
    all_to_all x1, starting transfers between devices: 20.9 us -> 24.3 us  [local(): lax.all_to_all(outgoing, grid_axes, split_axis=0, concat_axis=0, tiled=True)]
    all_to_all x1, starting transfers between devices: 23.1 us -> 20.2 us  [local(): lax.all_to_all(computed, grid_axes, split_axis=0, concat_axis=0, tiled=True)]
    concatenate x2 -> x1, other arithmetic: 5.1 us -> 3.85 us  [local(): held = jnp.concatenate([stacked, across, own_beside, across_beside], axis=1)]
  transfers between devices with their start and end apart: 5 -> 6, of which waited for: 4 -> 2; matrix products, arithmetic and copies ran while one was open for 21% -> 29% of each run, Pallas kernels for 2% -> 2%
where the time goes in v6:
time: 194 us; the launch traced here: 193 us
  starting transfers between devices  55.5 us (29%)
  waiting for transfers between devices  53.2 us (27%)
  local copies, waits for them, and re-layouts  48.2 us (25%)
  between operations  14.3 us (7%)
  other arithmetic  11.1 us (6%)
  matrix products  7.03 us (4%)
  Pallas kernels  3.59 us (2%)
    ppermute x3, waiting for transfers between devices, from_partner(): lax.ppermute(value, axis, [(i, i ^ flip) for i in range(lax.axis_size(axi...  34.9 us
    scatter x1, local copies, waits for them, and re-layouts, local(): jnp.zeros((expert_total * capacity, *tile), jnp.bfloat16).at[target]  24.3 us
    all_to_all x1, starting transfers between devices, local(): lax.all_to_all(outgoing, grid_axes, split_axis=0, concat_axis=0, tiled=True)  24.3 us
    all_to_all x1, starting transfers between devices, local(): lax.all_to_all(computed, grid_axes, split_axis=0, concat_axis=0, tiled=True)  20.2 us
    all_to_all x1, waiting for transfers between devices, local(): lax.all_to_all(computed, grid_axes, split_axis=0, concat_axis=0, tiled=True)  18.3 us
    ppermute x3, starting transfers between devices, from_partner(): lax.ppermute(value, axis, [(i, i ^ flip) for i in range(lax.axis_size(axi...  11 us
    unnamed x22, local copies, waits for them, and re-layouts  7.71 us
    dot_general x1, matrix products, expert_rows(): return jnp.dot(hidden, down_rows, preferred_element_type=jnp.float32)  4.57 us
  transfers between devices with their start and end apart: 6, of which 2 were waited for; matrix products, arithmetic and copies ran while one was open for 29% of the time, Pallas kernels for 2%

profile of v6, /device:TPU:1, one launch (start us, length us, event | category | flops | bytes accessed | tf_op | source)
XLA Modules:
  0.0 192.9 jit_solution(5755972751204344698)
XLA Ops:
  7.2 1.0 copy.45
  8.3 1.0 copy.46
  9.3 0.7 maximum_bitcast_fusion
  9.9 0.8 copy.48
  10.7 0.1 eq.31
  10.9 0.1 eq.27
  11.0 0.1 copy.50
  11.1 0.2 fusion.17
  11.4 0.7 broadcast_multiply_fusion
  12.1 0.1 copy.47
  12.2 0.1 mul.62
  12.4 0.7 convert_element_type.46
  13.1 1.1 fusion.14
  14.2 0.1 fusion.16
  14.3 0.3 broadcast_in_dim.27
  14.6 0.3 reshape.184
  14.9 0.2 fusion.19
  15.1 1.1 broadcast_in_dim.26
  16.2 24.3 %scatter_fusion = bf16[512,8,128]{2,1,0:T(8,128)(2,1)} fusion(bf16[512,8,128]{2,1,0:T(8,128)(2,1)} %broadcast_in_dim.26, s32[256]{0:T(256)S(1)} %bitcast.109, bf16[256,8,128]{2,1,0:T(8,128)(2,1)S(1)} %reshape.184), kind=kCustom, calls=%fused_computation.2 | custom fusion | bytes 1573888 | tf_op jit(solution)/shard_map/scatter | solution.py:168
  40.6 24.3 %all-to-all-start = ((bf16[512,8,128]{2,1,0:T(8,128)(2,1)}), bf16[512,8,128]{2,1,0:T(8,128)(2,1)}, u32[]{:S(2)}, u32[]{:S(2)}) async-start(bf16[512,8,128]{2,1,0:T(8,128)(2,1)} %scatter_fusion), calls=%async_computation | async-start | bytes 2097152 | tf_op jit(solution)/shard_map/all_to_all | solution.py:170
  64.9 1.1 pad_maximum_fusion.1
  66.1 3.3 %collective-permute-start = (bf16[3,192,1024]{2,1,0:T(8,128)(2,1)}, bf16[3,192,1024]{2,1,0:T(8,128)(2,1)}, u32[]{:S(2)}, u32[]{:S(2)}) collective-permute-start(bf16[3,192,1024]{2,1,0:T(8,128)(2,1)} %pad_maximum_fusion.1), channel_id=1, source_target_pairs={{0,2},{1,3},{2,0},{3,1},{4,6},{5,7},{6,4},{7,5},{8,10},{9,11},{10,... | collective-permute-start | bytes 3538952 | tf_op jit(solution)/shard_map/ppermute | solution.py:13
  69.4 4.9 %collective-permute-start.1 = (bf16[3,192,1024]{2,1,0:T(8,128)(2,1)}, bf16[3,192,1024]{2,1,0:T(8,128)(2,1)}, u32[]{:S(2)}, u32[]{:S(2)}) collective-permute-start(bf16[3,192,1024]{2,1,0:T(8,128)(2,1)} %pad_maximum_fusion.1), channel_id=1, source_target_pairs={{0,1},{1,0},{2,3},{3,2},{4,5},{5,4},{6,7},{7,6},{8,9},{9,8},{10,11... | collective-permute-start | bytes 3538952 | tf_op jit(solution)/shard_map/ppermute | solution.py:13
  74.3 34.8 %collective-permute-done = bf16[3,192,1024]{2,1,0:T(8,128)(2,1)} collective-permute-done((bf16[3,192,1024]{2,1,0:T(8,128)(2,1)}, bf16[3,192,1024]{2,1,0:T(8,128)(2,1)}, u32[]{:S(2)}, u32[]{:S(2)}) %collective-permute-start) | collective-permute-done | bytes 1179680 | tf_op jit(solution)/shard_map/ppermute | solution.py:13
  109.1 2.8 %collective-permute-start.2 = (bf16[3,192,1024]{2,1,0:T(8,128)(2,1)}, bf16[3,192,1024]{2,1,0:T(8,128)(2,1)}, u32[]{:S(2)}, u32[]{:S(2)}) collective-permute-start(bf16[3,192,1024]{2,1,0:T(8,128)(2,1)} %collective-permute-done), channel_id=1, source_target_pairs={{0,1},{1,0},{2,3},{3,2},{4,5},{5,4},{6,7},{7,6},{8,9},{9,8},{10,11... | collective-permute-start | bytes 3538952 | tf_op jit(solution)/shard_map/ppermute | solution.py:13
  111.9 0.1 reduce_sum.34
  112.2 0.1 copy.58
  112.4 0.1 reshape.174
  112.6 0.2 fusion.28
  112.8 1.9 gather_fusion.1
  114.7 0.1 reshape.177
  114.9 3.9 %pad_maximum_fusion = bf16[3,768,1024]{2,1,0:T(8,128)(2,1)S(1)} fusion(bf16[3,192,1024]{2,1,0:T(8,128)(2,1)} %collective-permute-done.2, bf16[3,192,1024]{2,1,0:T(8,128)(2,1)} %collective-permute-done.1, bf16[3,192,1024]{2,1,0:T(8,128)(2,1)} %collective-permute-done, bf16[1,192,1024]{2,1,0:T(8,128)(2,1)S(1)} %bitcast.99, ...), kind=kLoop, calls=%fused_computation.3 | loop fusion | flops 28311552 | bytes 9437184 | tf_op jit(solution)/shard_map/concatenate | solution.py:173
  118.8 2.1 %copy-done.1 = bf16[3,768,1024]{2,1,0:T(8,128)(2,1)} copy-done((bf16[3,768,1024]{2,1,0:T(8,128)(2,1)}, bf16[3,768,1024]{2,1,0:T(8,128)(2,1)S(1)}, u32[]{:S(2)}) %copy-start.1) | copy-done | bytes 4718616
  120.9 2.2 %fusion.2 = f32[512,768]{1,0:T(8,128)S(1)} fusion(bf16[3,768,1024]{2,1,0:T(8,128)(2,1)S(1)} %pad_maximum_fusion, bf16[64,8,8,128]{3,2,1,0:T(8,128)(2,1)} %bitcast.31), kind=kOutput, calls=%fused_computation.11 | convolution fusion | flops 805306368 | bytes 4194304 | tf_op jit(solution)/shard_map/dot_general | solution.py:18
  123.1 4.6 %fusion.4 = bf16[64,8,8,128]{3,1,2,0:T(8,128)(2,1)S(1)} fusion(bf16[3,768,1024]{2,1,0:T(8,128)(2,1)} %copy-done.1, f32[512,768]{1,0:T(8,128)S(1)} %fusion.2, bf16[64,8,8,128]{3,2,1,0:T(8,128)(2,1)} %bitcast.31), kind=kOutput, calls=%fused_computation.14 | convolution fusion | flops 1613496320 | bytes 6815744 | tf_op jit(solution)/shard_map/dot_general | solution.py:21
  127.7 1.3 copy.63
  129.0 20.2 %all-to-all-start.1 = ((bf16[512,8,128]{2,1,0:T(8,128)(2,1)}), bf16[512,8,128]{2,1,0:T(8,128)(2,1)}, u32[]{:S(2)}, u32[]{:S(2)}) async-start(bf16[512,8,128]{2,1,0:T(8,128)(2,1)} %bitcast.34), calls=%async_computation.1 | async-start | bytes 2097152 | tf_op jit(solution)/shard_map/all_to_all | solution.py:179
  149.3 3.9 %slice_bitcast_fusion = (bf16[2,128,4096]{2,1,0:T(8,128)(2,1)}, bf16[2,4096,128]{1,2,0:T(8,128)(2,1)S(1)}) fusion(bf16[2,2,4096,128]{2,3,1,0:T(8,128)(2,1)} %all-gather.2.cloned.1.call-done), kind=kLoop, calls=%fused_computation.4 | loop fusion | bytes 8388608 | tf_op jit(solution)/shard_map/transpose | solution.py:89
  153.3 2.4 %copy.54.k_ref = bf16[2,4096,128]{2,1,0:T(8,128)(2,1)} copy(bf16[2,4096,128]{1,2,0:T(8,128)(2,1)S(1)} %get-tuple-element.17) | data formatting | bytes 4194304 | tf_op jit(solution)/shard_map/squeeze | solution.py:88
  155.8 1.0 copy.53.qt_ref
  156.8 3.6 %shard_map.113 = bf16[2,128,1024]{2,1,0:T(8,128)(2,1)} custom-call(s32[1]{0:T(128)} %bitcast.c_ref, bf16[2,128,1024]{2,1,0:T(8,128)(2,1)} %copy.53.qt_ref, bf16[2,4096,128]{2,1,0:T(8,128)(2,1)} %copy.54.k_ref, bf16[2,128,4096]{2,1,0:T(8,128)(2,1)} %get-tuple-element.16.vt_ref), custom_call_target="tpu_custom_call" | custom-call | flops 2147483648 | bytes 5242880 | tf_op jit(solution)/shard_map/pallas_call | solution.py:92
  160.4 1.3 copy.55
  161.7 0.9 copy_bitcast_fusion.1
  162.6 18.3 %all-to-all-done.1 = bf16[512,8,128]{2,1,0:T(8,128)(2,1)} async-done(((bf16[512,8,128]{2,1,0:T(8,128)(2,1)}), bf16[512,8,128]{2,1,0:T(8,128)(2,1)}, u32[]{:S(2)}, u32[]{:S(2)}) %all-to-all-start.1) | async-done | bytes 1048608 | tf_op jit(solution)/shard_map/all_to_all | solution.py:179
  180.9 1.5 copy.80
  182.4 1.2 gather_fusion
  183.6 0.2 gather.11
  183.8 2.3 %multiply_reduce_fusion = bf16[128,1024]{1,0:T(8,128)(2,1)} fusion(bf16[128,2,1024]{2,1,0:T(2,128)(2,1)S(1)} %gather.11, pred[128,2]{1,0:T(8,128)(4,1)S(1)} %copy.58, f32[128,2]{1,0:T(8,128)S(1)} %copy.61), kind=kLoop, calls=%fused_computation.19 | loop fusion | flops 917504 | bytes 787712 | tf_op jit(solution)/shard_map/reduce_sum | solution.py:185
  (38 shorter events, 0.6 us)
Async XLA Ops:
  7.2 148.6 %copy-start = (bf16[1,128,16,128]{3,2,1,0:T(8,128)(2,1)S(1)}, bf16[1,128,16,128]{3,2,1,0:T(8,128)(2,1)}, u32[]{:S(2)}) copy-start(bf16[1,128,16,128]{3,2,1,0:T(8,128)(2,1)} %param.11) | copy-start | bytes 1572868
  7.2 7.0 %copy-start.5 = (bf16[1,128,1024]{2,1,0:T(8,128)(2,1)S(1)}, bf16[1,128,1024]{2,1,0:T(8,128)(2,1)}, u32[]{:S(2)}) copy-start(bf16[1,128,1024]{2,1,0:T(8,128)(2,1)} %param.10) | copy-start | bytes 786436
  7.2 121.8 %all-gather.2.cloned.1.call-start = ((), (), s32[]{:S(2)}) async-start(), calls=%async_computation.2 | async-start | bytes 4325376 | tf_op jit(solution)/shard_map/all_gather | solution.py:70
  16.2 48.7 %copy-start.2 = (bf16[192,1024]{1,0:T(8,128)(2,1)S(1)}, bf16[192,1024]{1,0:T(8,128)(2,1)}, u32[]{:S(2)}) copy-start(bf16[192,1024]{1,0:T(8,128)(2,1)} %param.19) | copy-start | bytes 1179652
  16.2 48.7 %copy-start.3 = (bf16[192,1024]{1,0:T(8,128)(2,1)S(1)}, bf16[192,1024]{1,0:T(8,128)(2,1)}, u32[]{:S(2)}) copy-start(bf16[192,1024]{1,0:T(8,128)(2,1)} %param.18) | copy-start | bytes 1179652
  16.2 48.7 %copy-start.4 = (bf16[192,1024]{1,0:T(8,128)(2,1)S(1)}, bf16[192,1024]{1,0:T(8,128)(2,1)}, u32[]{:S(2)}) copy-start(bf16[192,1024]{1,0:T(8,128)(2,1)} %param.17) | copy-start | bytes 1179652
  40.6 71.6 %copy-start.7 = (s32[1,128,2]{1,2,0:T(2,128)S(1)}, s32[1,128,2]{1,2,0:T(2,128)}, u32[]{:S(2)}) copy-start(s32[1,128,2]{1,2,0:T(2,128)} %param.14) | copy-start | bytes 3076
  40.6 72.0 %copy-start.6 = (bf16[1024,128]{1,0:T(8,128)(2,1)S(1)}, bf16[1024,128]{1,0:T(8,128)(2,1)}, u32[]{:S(2)}) copy-start(bf16[1024,128]{1,0:T(8,128)(2,1)} %param.16) | copy-start | bytes 786436
  40.6 68.6 %all-to-all-start = ((bf16[512,8,128]{2,1,0:T(8,128)(2,1)}), bf16[512,8,128]{2,1,0:T(8,128)(2,1)}, u32[]{:S(2)}, u32[]{:S(2)}) async-start(bf16[512,8,128]{2,1,0:T(8,128)(2,1)} %scatter_fusion), calls=%async_computation | async-start | bytes 2097152 | tf_op jit(solution)/shard_map/all_to_all | solution.py:170
  66.1 43.1 %collective-permute-start = (bf16[3,192,1024]{2,1,0:T(8,128)(2,1)}, bf16[3,192,1024]{2,1,0:T(8,128)(2,1)}, u32[]{:S(2)}, u32[]{:S(2)}) collective-permute-start(bf16[3,192,1024]{2,1,0:T(8,128)(2,1)} %pad_maximum_fusion.1), channel_id=1, source_target_pairs={{0,2},{1,3},{2,0},{3,1},{4,6},{5,7},{6,4},{7,5},{8,10},{9,11},{10,... | collective-permute-start | bytes 3538952 | tf_op jit(solution)/shard_map/ppermute | solution.py:13
  69.4 45.5 %collective-permute-start.1 = (bf16[3,192,1024]{2,1,0:T(8,128)(2,1)}, bf16[3,192,1024]{2,1,0:T(8,128)(2,1)}, u32[]{:S(2)}, u32[]{:S(2)}) collective-permute-start(bf16[3,192,1024]{2,1,0:T(8,128)(2,1)} %pad_maximum_fusion.1), channel_id=1, source_target_pairs={{0,1},{1,0},{2,3},{3,2},{4,5},{5,4},{6,7},{7,6},{8,9},{9,8},{10,11... | collective-permute-start | bytes 3538952 | tf_op jit(solution)/shard_map/ppermute | solution.py:13
  109.1 5.8 %collective-permute-start.2 = (bf16[3,192,1024]{2,1,0:T(8,128)(2,1)}, bf16[3,192,1024]{2,1,0:T(8,128)(2,1)}, u32[]{:S(2)}, u32[]{:S(2)}) collective-permute-start(bf16[3,192,1024]{2,1,0:T(8,128)(2,1)} %collective-permute-done), channel_id=1, source_target_pairs={{0,1},{1,0},{2,3},{3,2},{4,5},{5,4},{6,7},{7,6},{8,9},{9,8},{10,11... | collective-permute-start | bytes 3538952 | tf_op jit(solution)/shard_map/ppermute | solution.py:13
  118.8 2.1 %copy-start.1 = (bf16[3,768,1024]{2,1,0:T(8,128)(2,1)}, bf16[3,768,1024]{2,1,0:T(8,128)(2,1)S(1)}, u32[]{:S(2)}) copy-start(bf16[3,768,1024]{2,1,0:T(8,128)(2,1)S(1)} %pad_maximum_fusion) | copy-start | bytes 14155780
  129.0 51.9 %all-to-all-start.1 = ((bf16[512,8,128]{2,1,0:T(8,128)(2,1)}), bf16[512,8,128]{2,1,0:T(8,128)(2,1)}, u32[]{:S(2)}, u32[]{:S(2)}) async-start(bf16[512,8,128]{2,1,0:T(8,128)(2,1)} %bitcast.34), calls=%async_computation.1 | async-start | bytes 2097152 | tf_op jit(solution)/shard_map/all_to_all | solution.py:179
Sparse Core Ops, SparseCore 0:
  11.6 105.8 all-gather.1

commit v7 on v6

--- a/solution.py
+++ b/solution.py
@@ -164,8 +164,11 @@
     target = flat_ids * capacity + slot_index
     tile_rows = 8
     tile = (tile_rows, features // tile_rows)
-    source_rows = jnp.repeat(normed, top_count, axis=0).reshape(-1, *tile)
-    outgoing = jnp.zeros((expert_total * capacity, *tile), jnp.bfloat16).at[target].set(source_rows)
+    source_rows = jnp.repeat(normed, top_count, axis=0)
+    outgoing = (
+        jnp.zeros((expert_total * capacity, features), jnp.bfloat16).at[target].set(source_rows)
+    )
+    outgoing = outgoing.reshape(-1, *tile)
     grid_axes = ("ctx", "exp")
     received = lax.all_to_all(outgoing, grid_axes, split_axis=0, concat_axis=0, tiled=True)
     across, received = lax.optimization_barrier((across, received))

time: 194 us -> 189 us (0.974)
  local copies, waits for them, and re-layouts: 48.2 us -> 26 us
  waiting for transfers between devices: 53.2 us -> 71.5 us
    scatter x1, local copies, waits for them, and re-layouts: 24.3 us -> 1.91 us  [local(): jnp.zeros((expert_total * capacity, features), jnp.bfloat16).at[target]]
    all_gather x1, waiting for transfers between devices: 0.01 us -> 16.5 us  [gather_attention_inputs(): gathered = lax.all_gather(local_kv, 'ctx', axis=2, tiled=True)]
    ppermute x3, waiting for transfers between devices: 34.9 us -> 37 us  [from_partner(): lax.ppermute(value, axis, [(i, i ^ flip) for i in range(lax.axis_size(axi...]
    all_to_all x1, starting transfers between devices: 24.3 us -> 22.2 us  [local(): lax.all_to_all(outgoing, grid_axes, split_axis=0, concat_axis=0, tiled=True)]
    unnamed x22 -> x33, local copies, waits for them, and re-layouts: 7.71 us -> 9 us
  transfers between devices with their start and end apart: 6 -> 6, of which waited for: 2 -> 3; matrix products, arithmetic and copies ran while one was open for 29% -> 18% of each run, Pallas kernels for 2% -> 2%
where the time goes in v7:
time: 189 us
  waiting for transfers between devices  71.5 us (38%)
  starting transfers between devices  54.7 us (29%)
  local copies, waits for them, and re-layouts  26 us (14%)
  between operations  14.4 us (8%)
  other arithmetic  11.2 us (6%)
  matrix products  7.2 us (4%)
  Pallas kernels  3.6 us (2%)
    ppermute x3, waiting for transfers between devices, from_partner(): lax.ppermute(value, axis, [(i, i ^ flip) for i in range(lax.axis_size(axi...  37 us
    all_to_all x1, starting transfers between devices, local(): lax.all_to_all(outgoing, grid_axes, split_axis=0, concat_axis=0, tiled=True)  22.2 us
    all_to_all x1, starting transfers between devices, local(): lax.all_to_all(computed, grid_axes, split_axis=0, concat_axis=0, tiled=True)  21.6 us
    all_to_all x1, waiting for transfers between devices, local(): lax.all_to_all(computed, grid_axes, split_axis=0, concat_axis=0, tiled=True)  17.9 us
    all_gather x1, waiting for transfers between devices, gather_attention_inputs(): gathered = lax.all_gather(local_kv, 'ctx', axis=2, tiled=True)  16.5 us
    ppermute x3, starting transfers between devices, from_partner(): lax.ppermute(value, axis, [(i, i ^ flip) for i in range(lax.axis_size(axi...  10.9 us
    unnamed x33, local copies, waits for them, and re-layouts  9 us
    dot_general x1, matrix products, expert_rows(): return jnp.dot(hidden, down_rows, preferred_element_type=jnp.float32)  4.79 us
  transfers between devices with their start and end apart: 6, of which 3 were waited for; matrix products, arithmetic and copies ran while one was open for 18% of the time, Pallas kernels for 2%

profile of v7, /device:TPU:1, one launch (start us, length us, event | category | flops | bytes accessed | tf_op | source)
XLA Modules:
  0.0 188.6 jit_solution(8496153256154184902)
XLA Ops:
  7.2 1.0 copy.45
  8.3 1.0 copy.46
  9.3 0.7 maximum_bitcast_fusion
  9.9 0.8 copy.48
  10.7 0.1 eq.31
  10.9 0.1 eq.27
  11.1 0.2 fusion.19
  11.4 0.7 broadcast_multiply_fusion
  12.1 0.1 copy.47
  12.2 0.1 mul.62
  12.4 0.7 convert_element_type.46
  13.1 1.1 fusion.14
  14.2 0.1 fusion.16
  14.3 0.3 broadcast_in_dim.27
  14.6 0.2 reshape.192
  14.8 0.2 fusion.21
  15.0 1.9 %scatter_custom_fusion = bf16[512,1024]{1,0:T(8,128)(2,1)S(1)} fusion(s32[256]{0:T(256)S(1)} %bitcast.114, bf16[256,1024]{1,0:T(8,128)(2,1)S(1)} %reshape.192, bf16[]{:T(256)} %constant.29.clone.1), kind=kCustom, calls=%fused_computation.31 | custom fusion | bytes 1048578 | tf_op jit(solution)/shard_map/scatter | solution.py:169
  17.0 1.2 copy.62
  18.2 22.2 %all-to-all-start = ((bf16[512,8,128]{2,1,0:T(8,128)(2,1)}), bf16[512,8,128]{2,1,0:T(8,128)(2,1)S(1)}, u32[]{:S(2)}, u32[]{:S(2)}) async-start(bf16[512,8,128]{2,1,0:T(8,128)(2,1)} %bitcast.32), calls=%async_computation | async-start | bytes 2097152 | tf_op jit(solution)/shard_map/all_to_all | solution.py:173
  40.4 1.1 pad_maximum_fusion.1
  41.5 3.3 %collective-permute-start = (bf16[3,192,1024]{2,1,0:T(8,128)(2,1)}, bf16[3,192,1024]{2,1,0:T(8,128)(2,1)}, u32[]{:S(2)}, u32[]{:S(2)}) collective-permute-start(bf16[3,192,1024]{2,1,0:T(8,128)(2,1)} %pad_maximum_fusion.1), channel_id=1, source_target_pairs={{0,2},{1,3},{2,0},{3,1},{4,6},{5,7},{6,4},{7,5},{8,10},{9,11},{10,... | collective-permute-start | bytes 3538952 | tf_op jit(solution)/shard_map/ppermute | solution.py:13
  44.8 4.8 %collective-permute-start.1 = (bf16[3,192,1024]{2,1,0:T(8,128)(2,1)}, bf16[3,192,1024]{2,1,0:T(8,128)(2,1)}, u32[]{:S(2)}, u32[]{:S(2)}) collective-permute-start(bf16[3,192,1024]{2,1,0:T(8,128)(2,1)} %pad_maximum_fusion.1), channel_id=1, source_target_pairs={{0,1},{1,0},{2,3},{3,2},{4,5},{5,4},{6,7},{7,6},{8,9},{9,8},{10,11... | collective-permute-start | bytes 3538952 | tf_op jit(solution)/shard_map/ppermute | solution.py:13
  49.7 37.0 %collective-permute-done = bf16[3,192,1024]{2,1,0:T(8,128)(2,1)} collective-permute-done((bf16[3,192,1024]{2,1,0:T(8,128)(2,1)}, bf16[3,192,1024]{2,1,0:T(8,128)(2,1)}, u32[]{:S(2)}, u32[]{:S(2)}) %collective-permute-start) | collective-permute-done | bytes 1179680 | tf_op jit(solution)/shard_map/ppermute | solution.py:13
  86.7 2.8 %collective-permute-start.2 = (bf16[3,192,1024]{2,1,0:T(8,128)(2,1)}, bf16[3,192,1024]{2,1,0:T(8,128)(2,1)}, u32[]{:S(2)}, u32[]{:S(2)}) collective-permute-start(bf16[3,192,1024]{2,1,0:T(8,128)(2,1)} %collective-permute-done), channel_id=1, source_target_pairs={{0,1},{1,0},{2,3},{3,2},{4,5},{5,4},{6,7},{7,6},{8,9},{9,8},{10,11... | collective-permute-start | bytes 3538952 | tf_op jit(solution)/shard_map/ppermute | solution.py:13
  89.5 0.1 reduce_sum.34
  89.7 0.1 copy.58
  90.0 0.1 reshape.182
  90.1 0.2 fusion.30
  90.4 1.9 %gather_fusion.1 = f32[256]{0:T(256)S(1)} fusion(f32[128,128]{1,0:T(8,128)S(1)} %fusion.30, s32[256]{0:T(256)S(1)} %reshape.182), kind=kCustom, calls=%fused_computation.1 | custom fusion | bytes 4096 | tf_op jit(solution)/shard_map/jit(take_along_axis)/gather | solution.py:157
  92.3 0.1 reshape.185
  92.5 4.0 %pad_maximum_fusion = bf16[3,768,1024]{2,1,0:T(8,128)(2,1)S(1)} fusion(bf16[3,192,1024]{2,1,0:T(8,128)(2,1)} %collective-permute-done.2, bf16[3,192,1024]{2,1,0:T(8,128)(2,1)} %collective-permute-done.1, bf16[3,192,1024]{2,1,0:T(8,128)(2,1)} %collective-permute-done, bf16[1,192,1024]{2,1,0:T(8,128)(2,1)S(1)} %bitcast.102, ...), kind=kLoop, calls=%fused_computation.3 | loop fusion | flops 28311552 | bytes 9437184 | tf_op jit(solution)/shard_map/concatenate | solution.py:176
  96.5 2.1 %copy-done.1 = bf16[3,768,1024]{2,1,0:T(8,128)(2,1)} copy-done((bf16[3,768,1024]{2,1,0:T(8,128)(2,1)}, bf16[3,768,1024]{2,1,0:T(8,128)(2,1)S(1)}, u32[]{:S(2)}) %copy-start.1) | copy-done | bytes 4718616
  98.6 2.2 %fusion.2 = f32[512,768]{1,0:T(8,128)} fusion(bf16[3,768,1024]{2,1,0:T(8,128)(2,1)S(1)} %pad_maximum_fusion, bf16[64,8,8,128]{3,2,1,0:T(8,128)(2,1)S(1)} %bitcast.107), kind=kOutput, calls=%fused_computation.11 | convolution fusion | flops 805306368 | bytes 4194304 | tf_op jit(solution)/shard_map/dot_general | solution.py:18
  100.8 4.8 %fusion.4 = bf16[64,8,8,128]{3,1,2,0:T(8,128)(2,1)S(1)} fusion(bf16[3,768,1024]{2,1,0:T(8,128)(2,1)} %copy-done.1, f32[512,768]{1,0:T(8,128)} %fusion.2, bf16[64,8,8,128]{3,2,1,0:T(8,128)(2,1)S(1)} %bitcast.108), kind=kOutput, calls=%fused_computation.14 | convolution fusion | flops 1613496320 | bytes 6815744 | tf_op jit(solution)/shard_map/dot_general | solution.py:21
  105.6 1.3 copy.64
  106.9 16.5 %all-gather.2.cloned.1.call-done = bf16[2,2,4096,128]{2,3,1,0:T(8,128)(2,1)} async-done(((bf16[2,2,128,128]{2,3,1,0:T(8,128)(2,1)}), bf16[2,2,4096,128]{2,3,1,0:T(8,128)(2,1)}) %all-gather.2.cloned.1.call-update) | async-done | bytes 4194320 | tf_op jit(solution)/shard_map/all_gather | solution.py:70
  123.4 21.6 %all-to-all-start.1 = ((bf16[512,8,128]{2,1,0:T(8,128)(2,1)}), bf16[512,8,128]{2,1,0:T(8,128)(2,1)}, u32[]{:S(2)}, u32[]{:S(2)}) async-start(bf16[512,8,128]{2,1,0:T(8,128)(2,1)} %bitcast.36), calls=%async_computation.1 | async-start | bytes 2097152 | tf_op jit(solution)/shard_map/all_to_all | solution.py:182
  145.2 4.1 %slice_bitcast_fusion = (bf16[2,128,4096]{2,1,0:T(8,128)(2,1)}, bf16[2,4096,128]{1,2,0:T(8,128)(2,1)S(1)}) fusion(bf16[2,2,4096,128]{2,3,1,0:T(8,128)(2,1)} %all-gather.2.cloned.1.call-done), kind=kLoop, calls=%fused_computation.4 | loop fusion | bytes 8388608 | tf_op jit(solution)/shard_map/transpose | solution.py:89
  149.2 2.4 %copy.54.k_ref = bf16[2,4096,128]{2,1,0:T(8,128)(2,1)} copy(bf16[2,4096,128]{1,2,0:T(8,128)(2,1)S(1)} %get-tuple-element.17) | data formatting | bytes 4194304 | tf_op jit(solution)/shard_map/squeeze | solution.py:88
  151.7 1.0 copy.53.qt_ref
  152.7 3.6 %shard_map.113 = bf16[2,128,1024]{2,1,0:T(8,128)(2,1)} custom-call(s32[1]{0:T(128)} %bitcast.c_ref, bf16[2,128,1024]{2,1,0:T(8,128)(2,1)} %copy.53.qt_ref, bf16[2,4096,128]{2,1,0:T(8,128)(2,1)} %copy.54.k_ref, bf16[2,128,4096]{2,1,0:T(8,128)(2,1)} %get-tuple-element.16.vt_ref), custom_call_target="tpu_custom_call" | custom-call | flops 2147483648 | bytes 5242880 | tf_op jit(solution)/shard_map/pallas_call | solution.py:92
  156.3 1.4 copy.55
  157.7 0.9 copy_bitcast_fusion.1
  158.6 17.9 %all-to-all-done.1 = bf16[512,8,128]{2,1,0:T(8,128)(2,1)} async-done(((bf16[512,8,128]{2,1,0:T(8,128)(2,1)}), bf16[512,8,128]{2,1,0:T(8,128)(2,1)}, u32[]{:S(2)}, u32[]{:S(2)}) %all-to-all-start.1) | async-done | bytes 1048608 | tf_op jit(solution)/shard_map/all_to_all | solution.py:182
  176.5 1.5 copy.81
  178.0 1.2 gather_fusion
  179.2 0.2 gather.11
  179.4 2.3 %multiply_reduce_fusion = bf16[128,1024]{1,0:T(8,128)(2,1)} fusion(bf16[128,2,1024]{2,1,0:T(2,128)(2,1)S(1)} %gather.11, pred[128,2]{1,0:T(8,128)(4,1)S(1)} %copy.58, f32[128,2]{1,0:T(8,128)S(1)} %copy.61), kind=kLoop, calls=%fused_computation.19 | loop fusion | flops 917504 | bytes 787712 | tf_op jit(solution)/shard_map/reduce_sum | solution.py:188
  (48 shorter events, 0.8 us)
Async XLA Ops:
  7.2 144.5 %copy-start = (bf16[1,128,16,128]{3,2,1,0:T(8,128)(2,1)S(1)}, bf16[1,128,16,128]{3,2,1,0:T(8,128)(2,1)}, u32[]{:S(2)}) copy-start(bf16[1,128,16,128]{3,2,1,0:T(8,128)(2,1)} %param.11) | copy-start | bytes 1572868
  7.2 7.0 %copy-start.5 = (bf16[1,128,1024]{2,1,0:T(8,128)(2,1)S(1)}, bf16[1,128,1024]{2,1,0:T(8,128)(2,1)}, u32[]{:S(2)}) copy-start(bf16[1,128,1024]{2,1,0:T(8,128)(2,1)} %param.10) | copy-start | bytes 786436
  7.2 116.2 %all-gather.2.cloned.1.call-start = ((), (), s32[]{:S(2)}) async-start(), calls=%async_computation.2 | async-start | bytes 4325376 | tf_op jit(solution)/shard_map/all_gather | solution.py:70
  15.0 3.2 %copy-start.11 = (s32[256,1]{0,1:T(1,128)}, s32[256,1]{0,1:T(1,128)S(1)}, u32[]{:S(2)}) copy-start(s32[256,1]{0,1:T(1,128)S(1)} %compare_select_fusion) | copy-start | bytes 3076
  16.9 23.5 %copy-start.2 = (bf16[192,1024]{1,0:T(8,128)(2,1)S(1)}, bf16[192,1024]{1,0:T(8,128)(2,1)}, u32[]{:S(2)}) copy-start(bf16[192,1024]{1,0:T(8,128)(2,1)} %param.19) | copy-start | bytes 1179652
  16.9 23.4 %copy-start.3 = (bf16[192,1024]{1,0:T(8,128)(2,1)S(1)}, bf16[192,1024]{1,0:T(8,128)(2,1)}, u32[]{:S(2)}) copy-start(bf16[192,1024]{1,0:T(8,128)(2,1)} %param.18) | copy-start | bytes 1179652
  16.9 23.4 %copy-start.4 = (bf16[192,1024]{1,0:T(8,128)(2,1)S(1)}, bf16[192,1024]{1,0:T(8,128)(2,1)}, u32[]{:S(2)}) copy-start(bf16[192,1024]{1,0:T(8,128)(2,1)} %param.17) | copy-start | bytes 1179652
  18.2 71.5 %copy-start.9 = (s32[1,128,2]{1,2,0:T(2,128)S(1)}, s32[1,128,2]{1,2,0:T(2,128)}, u32[]{:S(2)}) copy-start(s32[1,128,2]{1,2,0:T(2,128)} %param.14) | copy-start | bytes 3076
  18.2 71.9 %copy-start.8 = (bf16[1024,128]{1,0:T(8,128)(2,1)S(1)}, bf16[1024,128]{1,0:T(8,128)(2,1)}, u32[]{:S(2)}) copy-start(bf16[1024,128]{1,0:T(8,128)(2,1)} %param.16) | copy-start | bytes 786436
  18.2 68.5 %all-to-all-start = ((bf16[512,8,128]{2,1,0:T(8,128)(2,1)}), bf16[512,8,128]{2,1,0:T(8,128)(2,1)S(1)}, u32[]{:S(2)}, u32[]{:S(2)}) async-start(bf16[512,8,128]{2,1,0:T(8,128)(2,1)} %bitcast.32), calls=%async_computation | async-start | bytes 2097152 | tf_op jit(solution)/shard_map/all_to_all | solution.py:173
  41.5 45.1 %collective-permute-start = (bf16[3,192,1024]{2,1,0:T(8,128)(2,1)}, bf16[3,192,1024]{2,1,0:T(8,128)(2,1)}, u32[]{:S(2)}, u32[]{:S(2)}) collective-permute-start(bf16[3,192,1024]{2,1,0:T(8,128)(2,1)} %pad_maximum_fusion.1), channel_id=1, source_target_pairs={{0,2},{1,3},{2,0},{3,1},{4,6},{5,7},{6,4},{7,5},{8,10},{9,11},{10,... | collective-permute-start | bytes 3538952 | tf_op jit(solution)/shard_map/ppermute | solution.py:13
  44.8 47.6 %collective-permute-start.1 = (bf16[3,192,1024]{2,1,0:T(8,128)(2,1)}, bf16[3,192,1024]{2,1,0:T(8,128)(2,1)}, u32[]{:S(2)}, u32[]{:S(2)}) collective-permute-start(bf16[3,192,1024]{2,1,0:T(8,128)(2,1)} %pad_maximum_fusion.1), channel_id=1, source_target_pairs={{0,1},{1,0},{2,3},{3,2},{4,5},{5,4},{6,7},{7,6},{8,9},{9,8},{10,11... | collective-permute-start | bytes 3538952 | tf_op jit(solution)/shard_map/ppermute | solution.py:13
  86.7 3.2 %copy-start.6 = (bf16[512,8,128]{2,1,0:T(8,128)(2,1)}, bf16[512,8,128]{2,1,0:T(8,128)(2,1)S(1)}, u32[]{:S(2)}) copy-start(bf16[512,8,128]{2,1,0:T(8,128)(2,1)S(1)} %all-to-all-done) | copy-start | bytes 3145732
  86.7 5.8 %collective-permute-start.2 = (bf16[3,192,1024]{2,1,0:T(8,128)(2,1)}, bf16[3,192,1024]{2,1,0:T(8,128)(2,1)}, u32[]{:S(2)}, u32[]{:S(2)}) collective-permute-start(bf16[3,192,1024]{2,1,0:T(8,128)(2,1)} %collective-permute-done), channel_id=1, source_target_pairs={{0,1},{1,0},{2,3},{3,2},{4,5},{5,4},{6,7},{7,6},{8,9},{9,8},{10,11... | collective-permute-start | bytes 3538952 | tf_op jit(solution)/shard_map/ppermute | solution.py:13
  92.5 6.1 %copy-start.7 = (bf16[512,8,128]{2,1,0:T(8,128)(2,1)S(1)}, bf16[512,8,128]{2,1,0:T(8,128)(2,1)}, u32[]{:S(2)}) copy-start(bf16[512,8,128]{2,1,0:T(8,128)(2,1)} %copy-done.6) | copy-start | bytes 3145732
  96.5 2.1 %copy-start.1 = (bf16[3,768,1024]{2,1,0:T(8,128)(2,1)}, bf16[3,768,1024]{2,1,0:T(8,128)(2,1)S(1)}, u32[]{:S(2)}) copy-start(bf16[3,768,1024]{2,1,0:T(8,128)(2,1)S(1)} %pad_maximum_fusion) | copy-start | bytes 14155780
  105.6 39.4 %copy-start.10 = (s32[1,128,2]{1,2,0:T(2,128)S(1)}, s32[1,128,2]{1,2,0:T(2,128)}, u32[]{:S(2)}) copy-start(s32[1,128,2]{1,2,0:T(2,128)} %param.14) | copy-start | bytes 3076
  105.6 39.5 %copy-start.12 = (s32[256,1]{0,1:T(1,128)S(1)}, s32[256,1]{0,1:T(1,128)}, u32[]{:S(2)}) copy-start(s32[256,1]{0,1:T(1,128)} %copy-done.11) | copy-start | bytes 3076
  123.4 53.1 %all-to-all-start.1 = ((bf16[512,8,128]{2,1,0:T(8,128)(2,1)}), bf16[512,8,128]{2,1,0:T(8,128)(2,1)}, u32[]{:S(2)}, u32[]{:S(2)}) async-start(bf16[512,8,128]{2,1,0:T(8,128)(2,1)} %bitcast.36), calls=%async_computation.1 | async-start | bytes 2097152 | tf_op jit(solution)/shard_map/all_to_all | solution.py:182
Sparse Core Ops, SparseCore 0:
  11.6 111.7 all-gather.1

commit v8 on v7

--- a/solution.py
+++ b/solution.py
@@ -177,8 +177,8 @@
     received = received.reshape(-1, features)
     computed = expert_rows(received, held[0], held[1], held[2]).astype(jnp.bfloat16)
     computed = computed.reshape(-1, *tile)
-    attention_inputs, computed = lax.optimization_barrier((attention_inputs, computed))
-    attended = attention(*attention_inputs)
+    queries_held, computed = lax.optimization_barrier((attention_inputs[0], computed))
+    attended = attention(queries_held, attention_inputs[1])
     came_back = lax.all_to_all(computed, grid_axes, split_axis=0, concat_axis=0, tiled=True)
     attended, came_back = lax.optimization_barrier((attended, came_back))
     flat_back = came_back.reshape(expert_total * capacity, features)

time: 189 us -> 183 us (0.968)
  the two profiles are of different devices: /device:TPU:1 before, /device:TPU:510 now
where the time goes in v8:
time: 183 us
  waiting for transfers between devices  55.9 us (31%)
  starting transfers between devices  46 us (25%)
  local copies, waits for them, and re-layouts  26 us (14%)
  Pallas kernels  22.3 us (12%)
  between operations  14.4 us (8%)
  other arithmetic  11.2 us (6%)
  matrix products  7.11 us (4%)
    ppermute x3, waiting for transfers between devices, from_partner(): lax.ppermute(value, axis, [(i, i ^ flip) for i in range(lax.axis_size(axi...  40.3 us
    pallas_call x1, Pallas kernels, attention(): pl.pallas_call(functools.partial(_flash_kernel, seq_rows, group_size, sca...  22.3 us
    all_to_all x1, starting transfers between devices, local(): lax.all_to_all(computed, grid_axes, split_axis=0, concat_axis=0, tiled=True)  20.7 us
    all_to_all x1, starting transfers between devices, local(): lax.all_to_all(outgoing, grid_axes, split_axis=0, concat_axis=0, tiled=True)  18.1 us
    all_gather x1, waiting for transfers between devices, gather_attention_inputs(): gathered = lax.all_gather(local_kv, 'ctx', axis=2, tiled=True)  15.6 us
    unnamed x33, local copies, waits for them, and re-layouts  9 us
    ppermute x3, starting transfers between devices, from_partner(): lax.ppermute(value, axis, [(i, i ^ flip) for i in range(lax.axis_size(axi...  7.12 us
    dot_general x1, matrix products, expert_rows(): return jnp.dot(hidden, down_rows, preferred_element_type=jnp.float32)  4.71 us
  transfers between devices with their start and end apart: 6, of which 3 were waited for; matrix products, arithmetic and copies ran while one was open for 19% of the time, Pallas kernels for 12%

profile of v8, /device:TPU:510, one launch (start us, length us, event | category | flops | bytes accessed | tf_op | source)
XLA Modules:
  0.0 182.9 jit_solution(12926895614421795005)
XLA Ops:
  7.2 1.0 copy.51
  8.3 1.0 copy.52
  9.3 0.7 maximum_bitcast_fusion
  9.9 0.8 copy.46
  10.7 0.1 eq.31
  10.9 0.1 eq.27
  11.1 0.2 fusion.19
  11.4 0.7 broadcast_multiply_fusion
  12.1 0.1 copy.45
  12.2 0.1 mul.62
  12.4 0.7 convert_element_type.46
  13.1 1.1 fusion.14
  14.2 0.1 fusion.16
  14.3 0.3 broadcast_in_dim.27
  14.6 0.2 reshape.192
  14.8 0.2 fusion.21
  15.0 1.9 %scatter_custom_fusion = bf16[512,1024]{1,0:T(8,128)(2,1)S(1)} fusion(s32[256]{0:T(256)S(1)} %bitcast.114, bf16[256,1024]{1,0:T(8,128)(2,1)S(1)} %reshape.192, bf16[]{:T(256)} %constant.29.clone.1), kind=kCustom, calls=%fused_computation.31 | custom fusion | bytes 1048578 | tf_op jit(solution)/shard_map/scatter | solution.py:169
  17.0 1.2 copy.62
  18.2 18.1 %all-to-all-start = ((bf16[512,8,128]{2,1,0:T(8,128)(2,1)}), bf16[512,8,128]{2,1,0:T(8,128)(2,1)S(1)}, u32[]{:S(2)}, u32[]{:S(2)}) async-start(bf16[512,8,128]{2,1,0:T(8,128)(2,1)} %bitcast.32), calls=%async_computation | async-start | bytes 2097152 | tf_op jit(solution)/shard_map/all_to_all | solution.py:173
  36.4 1.1 pad_maximum_fusion.1
  37.5 3.3 %collective-permute-start = (bf16[3,192,1024]{2,1,0:T(8,128)(2,1)}, bf16[3,192,1024]{2,1,0:T(8,128)(2,1)}, u32[]{:S(2)}, u32[]{:S(2)}) collective-permute-start(bf16[3,192,1024]{2,1,0:T(8,128)(2,1)} %pad_maximum_fusion.1), channel_id=1, source_target_pairs={{0,2},{1,3},{2,0},{3,1},{4,6},{5,7},{6,4},{7,5},{8,10},{9,11},{10,... | collective-permute-start | bytes 3538952 | tf_op jit(solution)/shard_map/ppermute | solution.py:13
  40.8 1.9 %collective-permute-start.1 = (bf16[3,192,1024]{2,1,0:T(8,128)(2,1)}, bf16[3,192,1024]{2,1,0:T(8,128)(2,1)}, u32[]{:S(2)}, u32[]{:S(2)}) collective-permute-start(bf16[3,192,1024]{2,1,0:T(8,128)(2,1)} %pad_maximum_fusion.1), channel_id=1, source_target_pairs={{0,1},{1,0},{2,3},{3,2},{4,5},{5,4},{6,7},{7,6},{8,9},{9,8},{10,11... | collective-permute-start | bytes 3538952 | tf_op jit(solution)/shard_map/ppermute | solution.py:13
  42.7 40.1 %collective-permute-done = bf16[3,192,1024]{2,1,0:T(8,128)(2,1)} collective-permute-done((bf16[3,192,1024]{2,1,0:T(8,128)(2,1)}, bf16[3,192,1024]{2,1,0:T(8,128)(2,1)}, u32[]{:S(2)}, u32[]{:S(2)}) %collective-permute-start) | collective-permute-done | bytes 1179680 | tf_op jit(solution)/shard_map/ppermute | solution.py:13
  82.9 1.9 %collective-permute-start.2 = (bf16[3,192,1024]{2,1,0:T(8,128)(2,1)}, bf16[3,192,1024]{2,1,0:T(8,128)(2,1)}, u32[]{:S(2)}, u32[]{:S(2)}) collective-permute-start(bf16[3,192,1024]{2,1,0:T(8,128)(2,1)} %collective-permute-done), channel_id=1, source_target_pairs={{0,1},{1,0},{2,3},{3,2},{4,5},{5,4},{6,7},{7,6},{8,9},{9,8},{10,11... | collective-permute-start | bytes 3538952 | tf_op jit(solution)/shard_map/ppermute | solution.py:13
  84.8 0.1 reduce_sum.34
  85.0 0.1 copy.58
  85.3 0.1 reshape.182
  85.5 0.2 fusion.30
  85.7 1.9 %gather_fusion.1 = f32[256]{0:T(256)S(1)} fusion(f32[128,128]{1,0:T(8,128)S(1)} %fusion.30, s32[256]{0:T(256)S(1)} %reshape.182), kind=kCustom, calls=%fused_computation.1 | custom fusion | bytes 4096 | tf_op jit(solution)/shard_map/jit(take_along_axis)/gather | solution.py:157
  87.6 0.1 reshape.185
  87.8 0.2 collective-permute-done.2
  88.0 3.9 %pad_maximum_fusion = bf16[3,768,1024]{2,1,0:T(8,128)(2,1)S(1)} fusion(bf16[3,192,1024]{2,1,0:T(8,128)(2,1)} %collective-permute-done.2, bf16[3,192,1024]{2,1,0:T(8,128)(2,1)} %collective-permute-done.1, bf16[3,192,1024]{2,1,0:T(8,128)(2,1)} %collective-permute-done, bf16[1,192,1024]{2,1,0:T(8,128)(2,1)S(1)} %bitcast.102, ...), kind=kLoop, calls=%fused_computation.3 | loop fusion | flops 28311552 | bytes 9437184 | tf_op jit(solution)/shard_map/concatenate | solution.py:176
  91.9 2.1 %copy-done.1 = bf16[3,768,1024]{2,1,0:T(8,128)(2,1)} copy-done((bf16[3,768,1024]{2,1,0:T(8,128)(2,1)}, bf16[3,768,1024]{2,1,0:T(8,128)(2,1)S(1)}, u32[]{:S(2)}) %copy-start.1) | copy-done | bytes 4718616
  94.0 2.2 %fusion.2 = f32[512,768]{1,0:T(8,128)} fusion(bf16[3,768,1024]{2,1,0:T(8,128)(2,1)S(1)} %pad_maximum_fusion, bf16[64,8,8,128]{3,2,1,0:T(8,128)(2,1)S(1)} %bitcast.107), kind=kOutput, calls=%fused_computation.11 | convolution fusion | flops 805306368 | bytes 4194304 | tf_op jit(solution)/shard_map/dot_general | solution.py:18
  96.2 4.7 %fusion.4 = bf16[64,8,8,128]{3,1,2,0:T(8,128)(2,1)S(1)} fusion(bf16[3,768,1024]{2,1,0:T(8,128)(2,1)} %copy-done.1, f32[512,768]{1,0:T(8,128)} %fusion.2, bf16[64,8,8,128]{3,2,1,0:T(8,128)(2,1)S(1)} %bitcast.108), kind=kOutput, calls=%fused_computation.14 | convolution fusion | flops 1613496320 | bytes 6815744 | tf_op jit(solution)/shard_map/dot_general | solution.py:21
  101.0 1.3 copy.64
  102.2 20.7 %all-to-all-start.1 = ((bf16[512,8,128]{2,1,0:T(8,128)(2,1)}), bf16[512,8,128]{2,1,0:T(8,128)(2,1)}, u32[]{:S(2)}, u32[]{:S(2)}) async-start(bf16[512,8,128]{2,1,0:T(8,128)(2,1)} %bitcast.36), calls=%async_computation.1 | async-start | bytes 2097152 | tf_op jit(solution)/shard_map/all_to_all | solution.py:182
  123.2 1.0 copy.53.qt_ref
  124.2 15.6 %all-gather.2.cloned.1.call-done = bf16[2,2,4096,128]{2,3,1,0:T(8,128)(2,1)} async-done(((bf16[2,2,128,128]{2,3,1,0:T(8,128)(2,1)}), bf16[2,2,4096,128]{2,3,1,0:T(8,128)(2,1)}) %all-gather.2.cloned.1.call-update) | async-done | bytes 4194320 | tf_op jit(solution)/shard_map/all_gather | solution.py:70
  139.8 4.1 %slice_bitcast_fusion = (bf16[2,128,4096]{2,1,0:T(8,128)(2,1)}, bf16[2,4096,128]{1,2,0:T(8,128)(2,1)S(1)}) fusion(bf16[2,2,4096,128]{2,3,1,0:T(8,128)(2,1)} %all-gather.2.cloned.1.call-done), kind=kLoop, calls=%fused_computation.4 | loop fusion | bytes 8388608 | tf_op jit(solution)/shard_map/transpose | solution.py:89
  143.8 2.4 %copy.54.k_ref = bf16[2,4096,128]{2,1,0:T(8,128)(2,1)} copy(bf16[2,4096,128]{1,2,0:T(8,128)(2,1)S(1)} %get-tuple-element.15) | data formatting | bytes 4194304 | tf_op jit(solution)/shard_map/squeeze | solution.py:88
  146.3 22.3 %shard_map.113 = bf16[2,128,1024]{2,1,0:T(8,128)(2,1)} custom-call(s32[1]{0:T(128)} %bitcast.c_ref, bf16[2,128,1024]{2,1,0:T(8,128)(2,1)} %copy.53.qt_ref, bf16[2,4096,128]{2,1,0:T(8,128)(2,1)} %copy.54.k_ref, bf16[2,128,4096]{2,1,0:T(8,128)(2,1)} %get-tuple-element.14.vt_ref), custom_call_target="tpu_custom_call" | custom-call | flops 2147483648 | bytes 5242880 | tf_op jit(solution)/shard_map/pallas_call | solution.py:92
  168.6 1.4 copy.55
  170.0 0.9 copy_bitcast_fusion.1
  170.9 1.5 copy.81
  172.3 1.2 gather_fusion
  173.5 0.2 gather.11
  173.7 2.3 %multiply_reduce_fusion = bf16[128,1024]{1,0:T(8,128)(2,1)} fusion(bf16[128,2,1024]{2,1,0:T(2,128)(2,1)S(1)} %gather.11, pred[128,2]{1,0:T(8,128)(4,1)S(1)} %copy.58, f32[128,2]{1,0:T(8,128)S(1)} %copy.61), kind=kLoop, calls=%fused_computation.19 | loop fusion | flops 917504 | bytes 787712 | tf_op jit(solution)/shard_map/reduce_sum | solution.py:188
  (48 shorter events, 0.8 us)
Async XLA Ops:
  7.2 116.0 %copy-start = (bf16[1,128,16,128]{3,2,1,0:T(8,128)(2,1)S(1)}, bf16[1,128,16,128]{3,2,1,0:T(8,128)(2,1)}, u32[]{:S(2)}) copy-start(bf16[1,128,16,128]{3,2,1,0:T(8,128)(2,1)} %param.11) | copy-start | bytes 1572868
  7.2 7.0 %copy-start.5 = (bf16[1,128,1024]{2,1,0:T(8,128)(2,1)S(1)}, bf16[1,128,1024]{2,1,0:T(8,128)(2,1)}, u32[]{:S(2)}) copy-start(bf16[1,128,1024]{2,1,0:T(8,128)(2,1)} %param.10) | copy-start | bytes 786436
  7.2 132.6 %all-gather.2.cloned.1.call-start = ((), (), s32[]{:S(2)}) async-start(), calls=%async_computation.2 | async-start | bytes 4325376 | tf_op jit(solution)/shard_map/all_gather | solution.py:70
  15.0 3.2 %copy-start.11 = (s32[256,1]{0,1:T(1,128)}, s32[256,1]{0,1:T(1,128)S(1)}, u32[]{:S(2)}) copy-start(s32[256,1]{0,1:T(1,128)S(1)} %compare_select_fusion) | copy-start | bytes 3076
  16.9 19.4 %copy-start.2 = (bf16[192,1024]{1,0:T(8,128)(2,1)S(1)}, bf16[192,1024]{1,0:T(8,128)(2,1)}, u32[]{:S(2)}) copy-start(bf16[192,1024]{1,0:T(8,128)(2,1)} %param.19) | copy-start | bytes 1179652
  16.9 19.4 %copy-start.3 = (bf16[192,1024]{1,0:T(8,128)(2,1)S(1)}, bf16[192,1024]{1,0:T(8,128)(2,1)}, u32[]{:S(2)}) copy-start(bf16[192,1024]{1,0:T(8,128)(2,1)} %param.18) | copy-start | bytes 1179652
  16.9 19.4 %copy-start.4 = (bf16[192,1024]{1,0:T(8,128)(2,1)S(1)}, bf16[192,1024]{1,0:T(8,128)(2,1)}, u32[]{:S(2)}) copy-start(bf16[192,1024]{1,0:T(8,128)(2,1)} %param.17) | copy-start | bytes 1179652
  18.2 66.8 %copy-start.9 = (s32[1,128,2]{1,2,0:T(2,128)S(1)}, s32[1,128,2]{1,2,0:T(2,128)}, u32[]{:S(2)}) copy-start(s32[1,128,2]{1,2,0:T(2,128)} %param.14) | copy-start | bytes 3076
  18.2 67.3 %copy-start.8 = (bf16[1024,128]{1,0:T(8,128)(2,1)S(1)}, bf16[1024,128]{1,0:T(8,128)(2,1)}, u32[]{:S(2)}) copy-start(bf16[1024,128]{1,0:T(8,128)(2,1)} %param.16) | copy-start | bytes 786436
  18.2 64.7 %all-to-all-start = ((bf16[512,8,128]{2,1,0:T(8,128)(2,1)}), bf16[512,8,128]{2,1,0:T(8,128)(2,1)S(1)}, u32[]{:S(2)}, u32[]{:S(2)}) async-start(bf16[512,8,128]{2,1,0:T(8,128)(2,1)} %bitcast.32), calls=%async_computation | async-start | bytes 2097152 | tf_op jit(solution)/shard_map/all_to_all | solution.py:173
  37.5 45.4 %collective-permute-start = (bf16[3,192,1024]{2,1,0:T(8,128)(2,1)}, bf16[3,192,1024]{2,1,0:T(8,128)(2,1)}, u32[]{:S(2)}, u32[]{:S(2)}) collective-permute-start(bf16[3,192,1024]{2,1,0:T(8,128)(2,1)} %pad_maximum_fusion.1), channel_id=1, source_target_pairs={{0,2},{1,3},{2,0},{3,1},{4,6},{5,7},{6,4},{7,5},{8,10},{9,11},{10,... | collective-permute-start | bytes 3538952 | tf_op jit(solution)/shard_map/ppermute | solution.py:13
  40.8 47.0 %collective-permute-start.1 = (bf16[3,192,1024]{2,1,0:T(8,128)(2,1)}, bf16[3,192,1024]{2,1,0:T(8,128)(2,1)}, u32[]{:S(2)}, u32[]{:S(2)}) collective-permute-start(bf16[3,192,1024]{2,1,0:T(8,128)(2,1)} %pad_maximum_fusion.1), channel_id=1, source_target_pairs={{0,1},{1,0},{2,3},{3,2},{4,5},{5,4},{6,7},{7,6},{8,9},{9,8},{10,11... | collective-permute-start | bytes 3538952 | tf_op jit(solution)/shard_map/ppermute | solution.py:13
  82.9 2.3 %copy-start.6 = (bf16[512,8,128]{2,1,0:T(8,128)(2,1)}, bf16[512,8,128]{2,1,0:T(8,128)(2,1)S(1)}, u32[]{:S(2)}) copy-start(bf16[512,8,128]{2,1,0:T(8,128)(2,1)S(1)} %all-to-all-done) | copy-start | bytes 3145732
  82.9 5.1 %collective-permute-start.2 = (bf16[3,192,1024]{2,1,0:T(8,128)(2,1)}, bf16[3,192,1024]{2,1,0:T(8,128)(2,1)}, u32[]{:S(2)}, u32[]{:S(2)}) collective-permute-start(bf16[3,192,1024]{2,1,0:T(8,128)(2,1)} %collective-permute-done), channel_id=1, source_target_pairs={{0,1},{1,0},{2,3},{3,2},{4,5},{5,4},{6,7},{7,6},{8,9},{9,8},{10,11... | collective-permute-start | bytes 3538952 | tf_op jit(solution)/shard_map/ppermute | solution.py:13
  87.8 6.2 %copy-start.7 = (bf16[512,8,128]{2,1,0:T(8,128)(2,1)S(1)}, bf16[512,8,128]{2,1,0:T(8,128)(2,1)}, u32[]{:S(2)}) copy-start(bf16[512,8,128]{2,1,0:T(8,128)(2,1)} %copy-done.6) | copy-start | bytes 3145732
  91.9 2.1 %copy-start.1 = (bf16[3,768,1024]{2,1,0:T(8,128)(2,1)}, bf16[3,768,1024]{2,1,0:T(8,128)(2,1)S(1)}, u32[]{:S(2)}) copy-start(bf16[3,768,1024]{2,1,0:T(8,128)(2,1)S(1)} %pad_maximum_fusion) | copy-start | bytes 14155780
  100.9 22.0 %copy-start.10 = (s32[1,128,2]{1,2,0:T(2,128)S(1)}, s32[1,128,2]{1,2,0:T(2,128)}, u32[]{:S(2)}) copy-start(s32[1,128,2]{1,2,0:T(2,128)} %param.14) | copy-start | bytes 3076
  100.9 22.2 %copy-start.12 = (s32[256,1]{0,1:T(1,128)S(1)}, s32[256,1]{0,1:T(1,128)}, u32[]{:S(2)}) copy-start(s32[256,1]{0,1:T(1,128)} %copy-done.11) | copy-start | bytes 3076
  102.2 68.6 %all-to-all-start.1 = ((bf16[512,8,128]{2,1,0:T(8,128)(2,1)}), bf16[512,8,128]{2,1,0:T(8,128)(2,1)}, u32[]{:S(2)}, u32[]{:S(2)}) async-start(bf16[512,8,128]{2,1,0:T(8,128)(2,1)} %bitcast.36), calls=%async_computation.1 | async-start | bytes 2097152 | tf_op jit(solution)/shard_map/all_to_all | solution.py:182
Sparse Core Ops, SparseCore 0:
  11.6 128.0 all-gather.1

commit v9 on v8

--- a/solution.py
+++ b/solution.py
@@ -21,7 +21,7 @@
     return jnp.dot(hidden, down_rows, preferred_element_type=jnp.float32)
 
 
-def _flash_kernel(block, group, scaling, c_ref, qt_ref, k_ref, vt_ref, o_ref, m_sc, l_sc, acc_sc):
+def _flash_kernel(block, group, scaling, c_ref, qt_ref, k_ref, v_ref, o_ref, m_sc, l_sc, acc_sc):
     c = c_ref[0]
     qt = qt_ref[0]
     width = qt.shape[1]
@@ -31,8 +31,8 @@
 
     def update(j, masked, size=block):
         start = pl.multiple_of(j * size, size)
-        k = k_ref[0, pl.ds(start, size), :]
-        vt = vt_ref[0, :, pl.ds(start, size)]
+        k = k_ref[0, 0, pl.ds(start, size), :]
+        v = v_ref[0, 0, pl.ds(start, size), :]
         s = jnp.dot(k, qt, preferred_element_type=jnp.float32) * scaling
         if masked:
             kpos = lax.broadcasted_iota(jnp.int32, (block, width), 0)
@@ -43,8 +43,8 @@
         alpha = jnp.exp(m_prev - m_new)
         p = jnp.exp(s - m_new)
         l_sc[...] = alpha * l_sc[...] + jnp.sum(p, axis=0, keepdims=True)
-        acc_sc[...] = alpha * acc_sc[...] + jnp.dot(
-            vt, p.astype(jnp.bfloat16), preferred_element_type=jnp.float32
+        acc_sc[...] = alpha * acc_sc[...] + lax.dot_general(
+            v, p.astype(jnp.bfloat16), (((0,), (0,)), ((), ())), preferred_element_type=jnp.float32
         )
         m_sc[...] = m_new
 
@@ -85,9 +85,7 @@
         .transpose(1, 3, 0, 2)
         .reshape(kv_count, head_size, width)
     )
-    keys_all = gathered[0]
-    values_t = gathered[1].transpose(0, 2, 1)
-    total_rows = keys_all.shape[1]
+    total_rows = gathered.shape[2]
     me = lax.axis_index("ctx").astype(jnp.int32).reshape(1)
     out = pl.pallas_call(
         functools.partial(_flash_kernel, seq_rows, group_size, scaling),
@@ -96,8 +94,8 @@
             grid=(kv_count,),
             in_specs=[
                 pl.BlockSpec((1, head_size, width), lambda g, c: (g, 0, 0)),
-                pl.BlockSpec((1, total_rows, head_size), lambda g, c: (g, 0, 0)),
-                pl.BlockSpec((1, head_size, total_rows), lambda g, c: (g, 0, 0)),
+                pl.BlockSpec((1, 1, total_rows, head_size), lambda g, c: (0, g, 0, 0)),
+                pl.BlockSpec((1, 1, total_rows, head_size), lambda g, c: (1, g, 0, 0)),
             ],
             out_specs=pl.BlockSpec((1, head_size, width), lambda g, c: (g, 0, 0)),
             scratch_shapes=[
@@ -112,7 +110,7 @@
             transcendentals=kv_count * width * total_rows // 2,
             bytes_accessed=4 * kv_count * total_rows * head_size + 4 * kv_count * width * head_size,
         ),
-    )(me, grouped_t, keys_all, values_t)
+    )(me, grouped_t, gathered, gathered)
     return (
         out.reshape(kv_count, head_size, seq_rows, group_size)
         .transpose(2, 0, 3, 1)

time: 183 us -> 169 us (0.923)
  the two profiles are of different devices: /device:TPU:510 before, /device:TPU:1 now
where the time goes in v9:
time: 169 us; the launch traced here: 166 us
  waiting for transfers between devices  60.8 us (36%)
  starting transfers between devices  53.6 us (32%)
  local copies, waits for them, and re-layouts  17.9 us (11%)
  between operations  14.4 us (9%)
  other arithmetic  8.37 us (5%)
  matrix products  7.11 us (4%)
  Pallas kernels  3.59 us (2%)
    ppermute x3, waiting for transfers between devices, from_partner(): lax.ppermute(value, axis, [(i, i ^ flip) for i in range(lax.axis_size(axi...  37.2 us
    all_to_all x1, starting transfers between devices, local(): lax.all_to_all(outgoing, grid_axes, split_axis=0, concat_axis=0, tiled=True)  24.2 us
    all_to_all x1, waiting for transfers between devices, local(): lax.all_to_all(computed, grid_axes, split_axis=0, concat_axis=0, tiled=True)  23.6 us
    all_to_all x1, starting transfers between devices, local(): lax.all_to_all(computed, grid_axes, split_axis=0, concat_axis=0, tiled=True)  18.3 us
    ppermute x3, starting transfers between devices, from_partner(): lax.ppermute(value, axis, [(i, i ^ flip) for i in range(lax.axis_size(axi...  11 us
    unnamed x25, local copies, waits for them, and re-layouts  7.49 us
    dot_general x1, matrix products, expert_rows(): return jnp.dot(hidden, down_rows, preferred_element_type=jnp.float32)  4.65 us
    pallas_call x1, Pallas kernels, attention(): pl.pallas_call(functools.partial(_flash_kernel, seq_rows, group_size, sca...  3.59 us
  transfers between devices with their start and end apart: 6, of which 3 were waited for; matrix products, arithmetic and copies ran while one was open for 15% of the time, Pallas kernels for 2%

profile of v9, /device:TPU:1, one launch (start us, length us, event | category | flops | bytes accessed | tf_op | source)
XLA Modules:
  0.0 165.8 jit_solution(4669228229794972698)
XLA Ops:
  7.3 0.9 copy.48
  8.2 0.9 copy.49
  9.0 0.7 maximum_bitcast_fusion
  9.7 0.8 copy.43
  10.5 0.1 eq.31
  10.7 0.1 eq.27
  10.8 0.1 copy.45
  10.9 0.2 fusion.19
  11.2 0.1 copy.42
  11.4 0.1 mul.62
  11.5 0.1 fusion.14
  11.7 0.1 fusion.16
  11.8 0.3 broadcast_in_dim.27
  12.1 0.2 reshape.192
  12.3 0.2 fusion.21
  12.5 1.9 %scatter_custom_fusion = bf16[512,1024]{1,0:T(8,128)(2,1)S(1)} fusion(s32[256]{0:T(256)S(1)} %bitcast.107, bf16[256,1024]{1,0:T(8,128)(2,1)S(1)} %reshape.192, bf16[]{:T(256)} %constant.29.clone.1), kind=kCustom, calls=%fused_computation.29 | custom fusion | bytes 1048578 | tf_op jit(solution)/shard_map/scatter | solution.py:167
  14.4 1.3 copy.58
  15.7 24.2 %all-to-all-start = ((bf16[512,8,128]{2,1,0:T(8,128)(2,1)}), bf16[512,8,128]{2,1,0:T(8,128)(2,1)}, u32[]{:S(2)}, u32[]{:S(2)}) async-start(bf16[512,8,128]{2,1,0:T(8,128)(2,1)} %bitcast.28), calls=%async_computation | async-start | bytes 2097152 | tf_op jit(solution)/shard_map/all_to_all | solution.py:171
  40.0 1.1 pad_maximum_fusion.1
  41.1 3.3 %collective-permute-start = (bf16[3,192,1024]{2,1,0:T(8,128)(2,1)}, bf16[3,192,1024]{2,1,0:T(8,128)(2,1)S(1)}, u32[]{:S(2)}, u32[]{:S(2)}) collective-permute-start(bf16[3,192,1024]{2,1,0:T(8,128)(2,1)} %pad_maximum_fusion.1), channel_id=1, source_target_pairs={{0,2},{1,3},{2,0},{3,1},{4,6},{5,7},{6,4},{7,5},{8,10},{9,11},{10,... | collective-permute-start | bytes 3538952 | tf_op jit(solution)/shard_map/ppermute | solution.py:13
  44.4 4.9 %collective-permute-start.1 = (bf16[3,192,1024]{2,1,0:T(8,128)(2,1)}, bf16[3,192,1024]{2,1,0:T(8,128)(2,1)}, u32[]{:S(2)}, u32[]{:S(2)}) collective-permute-start(bf16[3,192,1024]{2,1,0:T(8,128)(2,1)} %pad_maximum_fusion.1), channel_id=1, source_target_pairs={{0,1},{1,0},{2,3},{3,2},{4,5},{5,4},{6,7},{7,6},{8,9},{9,8},{10,11... | collective-permute-start | bytes 3538952 | tf_op jit(solution)/shard_map/ppermute | solution.py:13
  49.3 34.7 %collective-permute-done = bf16[3,192,1024]{2,1,0:T(8,128)(2,1)S(1)} collective-permute-done((bf16[3,192,1024]{2,1,0:T(8,128)(2,1)}, bf16[3,192,1024]{2,1,0:T(8,128)(2,1)S(1)}, u32[]{:S(2)}, u32[]{:S(2)}) %collective-permute-start) | collective-permute-done | bytes 1179680 | tf_op jit(solution)/shard_map/ppermute | solution.py:13
  84.1 2.8 %collective-permute-start.2 = (bf16[3,192,1024]{2,1,0:T(8,128)(2,1)S(1)}, bf16[3,192,1024]{2,1,0:T(8,128)(2,1)S(1)}, u32[]{:S(2)}, u32[]{:S(2)}) collective-permute-start(bf16[3,192,1024]{2,1,0:T(8,128)(2,1)S(1)} %collective-permute-done), channel_id=1, source_target_pairs={{0,1},{1,0},{2,3},{3,2},{4,5},{5,4},{6,7},{7,6},{8,9},{9,8},{10,11... | collective-permute-start | bytes 3538952 | tf_op jit(solution)/shard_map/ppermute | solution.py:13
  86.9 2.4 %collective-permute-done.2 = bf16[3,192,1024]{2,1,0:T(8,128)(2,1)S(1)} collective-permute-done((bf16[3,192,1024]{2,1,0:T(8,128)(2,1)S(1)}, bf16[3,192,1024]{2,1,0:T(8,128)(2,1)S(1)}, u32[]{:S(2)}, u32[]{:S(2)}) %collective-permute-start.2) | collective-permute-done | bytes 1179680 | tf_op jit(solution)/shard_map/ppermute | solution.py:13
  89.3 3.4 %pad_maximum_fusion = bf16[3,768,1024]{2,1,0:T(8,128)(2,1)S(1)} fusion(bf16[3,192,1024]{2,1,0:T(8,128)(2,1)S(1)} %collective-permute-done.2, bf16[3,192,1024]{2,1,0:T(8,128)(2,1)} %collective-permute-done.1, bf16[3,192,1024]{2,1,0:T(8,128)(2,1)S(1)} %collective-permute-done, bf16[1,192,1024]{2,1,0:T(8,128)(2,1)S(1)} %bitcast.97, ...), kind=kLoop, calls=%fused_computation.3 | loop fusion | flops 28311552 | bytes 9437184 | tf_op jit(solution)/shard_map/concatenate | solution.py:174
  92.7 2.1 %copy-done.1 = bf16[3,768,1024]{2,1,0:T(8,128)(2,1)} copy-done((bf16[3,768,1024]{2,1,0:T(8,128)(2,1)}, bf16[3,768,1024]{2,1,0:T(8,128)(2,1)S(1)}, u32[]{:S(2)}) %copy-start.1) | copy-done | bytes 4718616
  94.8 2.2 %fusion.2 = f32[512,768]{1,0:T(8,128)S(1)} fusion(bf16[3,768,1024]{2,1,0:T(8,128)(2,1)S(1)} %pad_maximum_fusion, bf16[64,8,8,128]{3,2,1,0:T(8,128)(2,1)} %bitcast.29), kind=kOutput, calls=%fused_computation.9 | convolution fusion | flops 805306368 | bytes 4194304 | tf_op jit(solution)/shard_map/dot_general | solution.py:18
  97.1 4.7 %fusion.4 = bf16[64,8,8,128]{3,1,2,0:T(8,128)(2,1)S(1)} fusion(bf16[3,768,1024]{2,1,0:T(8,128)(2,1)} %copy-done.1, f32[512,768]{1,0:T(8,128)S(1)} %fusion.2, bf16[64,8,8,128]{3,2,1,0:T(8,128)(2,1)} %bitcast.29), kind=kOutput, calls=%fused_computation.12 | convolution fusion | flops 1613496320 | bytes 6815744 | tf_op jit(solution)/shard_map/dot_general | solution.py:21
  101.7 1.3 copy.60
  103.0 18.3 %all-to-all-start.1 = ((bf16[512,8,128]{2,1,0:T(8,128)(2,1)}), bf16[512,8,128]{2,1,0:T(8,128)(2,1)S(1)}, u32[]{:S(2)}, u32[]{:S(2)}) async-start(bf16[512,8,128]{2,1,0:T(8,128)(2,1)} %bitcast.32), calls=%async_computation.1 | async-start | bytes 2097152 | tf_op jit(solution)/shard_map/all_to_all | solution.py:180
  121.3 0.1 reduce_sum.34
  121.5 0.1 copy.53
  121.6 0.1 copy.54
  121.7 0.1 copy.55
  121.8 0.1 reshape.182
  122.0 0.2 fusion.30
  122.2 1.9 %gather_fusion.1 = f32[256]{0:T(256)S(1)} fusion(f32[128,128]{1,0:T(8,128)S(1)} %fusion.30, s32[256]{0:T(256)S(1)} %reshape.182), kind=kCustom, calls=%fused_computation.1 | custom fusion | bytes 4096 | tf_op jit(solution)/shard_map/jit(take_along_axis)/gather | solution.py:155
  124.1 0.1 reshape.185
  124.4 0.1 copy.57
  124.6 1.0 copy.50.qt_ref
  125.6 3.6 %shard_map.113 = bf16[2,128,1024]{2,1,0:T(8,128)(2,1)} custom-call(s32[1]{0:T(128)} %bitcast.c_ref, bf16[2,128,1024]{2,1,0:T(8,128)(2,1)} %copy.50.qt_ref, bf16[2,2,4096,128]{3,2,1,0:T(8,128)(2,1)} %all-gather.2.cloned.1.call-done.k_ref.v_ref, bf16[2,2,4096,128]{3,2,1,0:T(8,128)(2,1)} %all-gather.2.cloned.1.call-done.k_ref.v_ref), custom_call_target="tpu_custom_call" | custom-call | flops 2147483648 | bytes 5242880 | tf_op jit(solution)/shard_map/pallas_call | solution.py:90
  129.2 1.3 copy.51
  130.5 0.9 copy_bitcast_fusion.1
  131.4 23.6 %all-to-all-done.1 = bf16[512,8,128]{2,1,0:T(8,128)(2,1)S(1)} async-done(((bf16[512,8,128]{2,1,0:T(8,128)(2,1)}), bf16[512,8,128]{2,1,0:T(8,128)(2,1)S(1)}, u32[]{:S(2)}, u32[]{:S(2)}) %all-to-all-start.1) | async-done | bytes 1048608 | tf_op jit(solution)/shard_map/all_to_all | solution.py:180
  155.0 0.3 copy.77
  155.2 1.2 gather_fusion
  156.4 0.2 gather.11
  156.6 2.3 %multiply_reduce_fusion = bf16[128,1024]{1,0:T(8,128)(2,1)} fusion(bf16[128,2,1024]{2,1,0:T(2,128)(2,1)S(1)} %gather.11, pred[128,2]{1,0:T(8,128)(4,1)S(1)} %copy.54, f32[128,2]{1,0:T(8,128)S(1)} %copy.57), kind=kLoop, calls=%fused_computation.17 | loop fusion | flops 917504 | bytes 787712 | tf_op jit(solution)/shard_map/reduce_sum | solution.py:186
  (38 shorter events, 0.4 us)
Async XLA Ops:
  7.2 117.3 %copy-start = (bf16[1,128,16,128]{3,2,1,0:T(8,128)(2,1)S(1)}, bf16[1,128,16,128]{3,2,1,0:T(8,128)(2,1)}, u32[]{:S(2)}) copy-start(bf16[1,128,16,128]{3,2,1,0:T(8,128)(2,1)} %param.11) | copy-start | bytes 1572868
  7.2 4.0 %copy-start.7 = (s32[1,128,2]{1,2,0:T(2,128)S(1)}, s32[1,128,2]{1,2,0:T(2,128)}, u32[]{:S(2)}) copy-start(s32[1,128,2]{1,2,0:T(2,128)} %param.14) | copy-start | bytes 3076
  7.2 4.3 %copy-start.8 = (bf16[1024]{0:T(1024)(128)(2,1)S(1)}, bf16[1024]{0:T(1024)(128)(2,1)}, u32[]{:S(2)}) copy-start(bf16[1024]{0:T(1024)(128)(2,1)} %param.15) | copy-start | bytes 6148
  7.2 4.3 %copy-start.5 = (bf16[1,128,1024]{2,1,0:T(8,128)(2,1)S(1)}, bf16[1,128,1024]{2,1,0:T(8,128)(2,1)}, u32[]{:S(2)}) copy-start(bf16[1,128,1024]{2,1,0:T(8,128)(2,1)} %param.10) | copy-start | bytes 786436
  7.2 118.4 %all-gather.2.cloned.1.call-start = ((), (), s32[]{:S(2)}) async-start(), calls=%async_computation.2 | async-start | bytes 4325376 | tf_op jit(solution)/shard_map/all_gather | solution.py:70
  15.7 24.3 %copy-start.2 = (bf16[192,1024]{1,0:T(8,128)(2,1)S(1)}, bf16[192,1024]{1,0:T(8,128)(2,1)}, u32[]{:S(2)}) copy-start(bf16[192,1024]{1,0:T(8,128)(2,1)} %param.19) | copy-start | bytes 1179652
  15.7 24.3 %copy-start.3 = (bf16[192,1024]{1,0:T(8,128)(2,1)S(1)}, bf16[192,1024]{1,0:T(8,128)(2,1)}, u32[]{:S(2)}) copy-start(bf16[192,1024]{1,0:T(8,128)(2,1)} %param.18) | copy-start | bytes 1179652
  15.7 24.3 %copy-start.4 = (bf16[192,1024]{1,0:T(8,128)(2,1)S(1)}, bf16[192,1024]{1,0:T(8,128)(2,1)}, u32[]{:S(2)}) copy-start(bf16[192,1024]{1,0:T(8,128)(2,1)} %param.17) | copy-start | bytes 1179652
  15.7 68.4 %all-to-all-start = ((bf16[512,8,128]{2,1,0:T(8,128)(2,1)}), bf16[512,8,128]{2,1,0:T(8,128)(2,1)}, u32[]{:S(2)}, u32[]{:S(2)}) async-start(bf16[512,8,128]{2,1,0:T(8,128)(2,1)} %bitcast.28), calls=%async_computation | async-start | bytes 2097152 | tf_op jit(solution)/shard_map/all_to_all | solution.py:171
  41.1 43.0 %collective-permute-start = (bf16[3,192,1024]{2,1,0:T(8,128)(2,1)}, bf16[3,192,1024]{2,1,0:T(8,128)(2,1)S(1)}, u32[]{:S(2)}, u32[]{:S(2)}) collective-permute-start(bf16[3,192,1024]{2,1,0:T(8,128)(2,1)} %pad_maximum_fusion.1), channel_id=1, source_target_pairs={{0,2},{1,3},{2,0},{3,1},{4,6},{5,7},{6,4},{7,5},{8,10},{9,11},{10,... | collective-permute-start | bytes 3538952 | tf_op jit(solution)/shard_map/ppermute | solution.py:13
  44.4 42.4 %collective-permute-start.1 = (bf16[3,192,1024]{2,1,0:T(8,128)(2,1)}, bf16[3,192,1024]{2,1,0:T(8,128)(2,1)}, u32[]{:S(2)}, u32[]{:S(2)}) collective-permute-start(bf16[3,192,1024]{2,1,0:T(8,128)(2,1)} %pad_maximum_fusion.1), channel_id=1, source_target_pairs={{0,1},{1,0},{2,3},{3,2},{4,5},{5,4},{6,7},{7,6},{8,9},{9,8},{10,11... | collective-permute-start | bytes 3538952 | tf_op jit(solution)/shard_map/ppermute | solution.py:13
  84.1 5.2 %collective-permute-start.2 = (bf16[3,192,1024]{2,1,0:T(8,128)(2,1)S(1)}, bf16[3,192,1024]{2,1,0:T(8,128)(2,1)S(1)}, u32[]{:S(2)}, u32[]{:S(2)}) collective-permute-start(bf16[3,192,1024]{2,1,0:T(8,128)(2,1)S(1)} %collective-permute-done), channel_id=1, source_target_pairs={{0,1},{1,0},{2,3},{3,2},{4,5},{5,4},{6,7},{7,6},{8,9},{9,8},{10,11... | collective-permute-start | bytes 3538952 | tf_op jit(solution)/shard_map/ppermute | solution.py:13
  92.7 2.1 %copy-start.1 = (bf16[3,768,1024]{2,1,0:T(8,128)(2,1)}, bf16[3,768,1024]{2,1,0:T(8,128)(2,1)S(1)}, u32[]{:S(2)}) copy-start(bf16[3,768,1024]{2,1,0:T(8,128)(2,1)S(1)} %pad_maximum_fusion) | copy-start | bytes 14155780
  103.0 19.0 %copy-start.6 = (bf16[1024,128]{1,0:T(8,128)(2,1)S(1)}, bf16[1024,128]{1,0:T(8,128)(2,1)}, u32[]{:S(2)}) copy-start(bf16[1024,128]{1,0:T(8,128)(2,1)} %param.16) | copy-start | bytes 786436
  103.0 52.0 %all-to-all-start.1 = ((bf16[512,8,128]{2,1,0:T(8,128)(2,1)}), bf16[512,8,128]{2,1,0:T(8,128)(2,1)S(1)}, u32[]{:S(2)}, u32[]{:S(2)}) async-start(bf16[512,8,128]{2,1,0:T(8,128)(2,1)} %bitcast.32), calls=%async_computation.1 | async-start | bytes 2097152 | tf_op jit(solution)/shard_map/all_to_all | solution.py:180
Sparse Core Ops, SparseCore 0:
  11.8 108.9 all-gather.1

commit v10 on v9

--- a/solution.py
+++ b/solution.py
@@ -48,7 +48,7 @@
         )
         m_sc[...] = m_new
 
-    wide = 4 * block
+    wide = 8 * block
     span = wide // block
 
     def body_wide(j, carry):

time: 169 us -> 169 us (level)
  no operation moved by 1% of the time
where the time goes in v10:
time: 169 us; the launch traced here: 166 us
  waiting for transfers between devices  60.8 us (36%)
  starting transfers between devices  53.6 us (32%)
  local copies, waits for them, and re-layouts  17.9 us (11%)
  between operations  14.4 us (9%)
  other arithmetic  8.37 us (5%)
  matrix products  7.11 us (4%)
  Pallas kernels  3.59 us (2%)
    ppermute x3, waiting for transfers between devices, from_partner(): lax.ppermute(value, axis, [(i, i ^ flip) for i in range(lax.axis_size(axi...  37.2 us
    all_to_all x1, starting transfers between devices, local(): lax.all_to_all(outgoing, grid_axes, split_axis=0, concat_axis=0, tiled=True)  24.2 us
    all_to_all x1, waiting for transfers between devices, local(): lax.all_to_all(computed, grid_axes, split_axis=0, concat_axis=0, tiled=True)  23.6 us
    all_to_all x1, starting transfers between devices, local(): lax.all_to_all(computed, grid_axes, split_axis=0, concat_axis=0, tiled=True)  18.3 us
    ppermute x3, starting transfers between devices, from_partner(): lax.ppermute(value, axis, [(i, i ^ flip) for i in range(lax.axis_size(axi...  11 us
    unnamed x25, local copies, waits for them, and re-layouts  7.49 us
    dot_general x1, matrix products, expert_rows(): return jnp.dot(hidden, down_rows, preferred_element_type=jnp.float32)  4.65 us
    pallas_call x1, Pallas kernels, attention(): pl.pallas_call(functools.partial(_flash_kernel, seq_rows, group_size, sca...  3.59 us
  transfers between devices with their start and end apart: 6, of which 3 were waited for; matrix products, arithmetic and copies ran while one was open for 15% of the time, Pallas kernels for 2%

profile of v10, /device:TPU:1, one launch (start us, length us, event | category | flops | bytes accessed | tf_op | source)
XLA Modules:
  0.0 165.8 jit_solution(8839799661995291522)
XLA Ops:
  7.3 0.9 copy.48
  8.2 0.9 copy.49
  9.0 0.7 maximum_bitcast_fusion
  9.7 0.8 copy.43
  10.5 0.1 eq.31
  10.7 0.1 eq.27
  10.8 0.1 copy.45
  10.9 0.2 fusion.19
  11.2 0.1 copy.42
  11.4 0.1 mul.62
  11.5 0.1 fusion.14
  11.7 0.1 fusion.16
  11.8 0.3 broadcast_in_dim.27
  12.1 0.2 reshape.192
  12.3 0.2 fusion.21
  12.5 1.9 %scatter_custom_fusion = bf16[512,1024]{1,0:T(8,128)(2,1)S(1)} fusion(s32[256]{0:T(256)S(1)} %bitcast.107, bf16[256,1024]{1,0:T(8,128)(2,1)S(1)} %reshape.192, bf16[]{:T(256)} %constant.29.clone.1), kind=kCustom, calls=%fused_computation.29 | custom fusion | bytes 1048578 | tf_op jit(solution)/shard_map/scatter | solution.py:167
  14.4 1.3 copy.58
  15.7 24.2 %all-to-all-start = ((bf16[512,8,128]{2,1,0:T(8,128)(2,1)}), bf16[512,8,128]{2,1,0:T(8,128)(2,1)}, u32[]{:S(2)}, u32[]{:S(2)}) async-start(bf16[512,8,128]{2,1,0:T(8,128)(2,1)} %bitcast.28), calls=%async_computation | async-start | bytes 2097152 | tf_op jit(solution)/shard_map/all_to_all | solution.py:171
  40.0 1.1 pad_maximum_fusion.1
  41.1 3.3 %collective-permute-start = (bf16[3,192,1024]{2,1,0:T(8,128)(2,1)}, bf16[3,192,1024]{2,1,0:T(8,128)(2,1)S(1)}, u32[]{:S(2)}, u32[]{:S(2)}) collective-permute-start(bf16[3,192,1024]{2,1,0:T(8,128)(2,1)} %pad_maximum_fusion.1), channel_id=1, source_target_pairs={{0,2},{1,3},{2,0},{3,1},{4,6},{5,7},{6,4},{7,5},{8,10},{9,11},{10,... | collective-permute-start | bytes 3538952 | tf_op jit(solution)/shard_map/ppermute | solution.py:13
  44.4 4.9 %collective-permute-start.1 = (bf16[3,192,1024]{2,1,0:T(8,128)(2,1)}, bf16[3,192,1024]{2,1,0:T(8,128)(2,1)}, u32[]{:S(2)}, u32[]{:S(2)}) collective-permute-start(bf16[3,192,1024]{2,1,0:T(8,128)(2,1)} %pad_maximum_fusion.1), channel_id=1, source_target_pairs={{0,1},{1,0},{2,3},{3,2},{4,5},{5,4},{6,7},{7,6},{8,9},{9,8},{10,11... | collective-permute-start | bytes 3538952 | tf_op jit(solution)/shard_map/ppermute | solution.py:13
  49.3 34.7 %collective-permute-done = bf16[3,192,1024]{2,1,0:T(8,128)(2,1)S(1)} collective-permute-done((bf16[3,192,1024]{2,1,0:T(8,128)(2,1)}, bf16[3,192,1024]{2,1,0:T(8,128)(2,1)S(1)}, u32[]{:S(2)}, u32[]{:S(2)}) %collective-permute-start) | collective-permute-done | bytes 1179680 | tf_op jit(solution)/shard_map/ppermute | solution.py:13
  84.1 2.8 %collective-permute-start.2 = (bf16[3,192,1024]{2,1,0:T(8,128)(2,1)S(1)}, bf16[3,192,1024]{2,1,0:T(8,128)(2,1)S(1)}, u32[]{:S(2)}, u32[]{:S(2)}) collective-permute-start(bf16[3,192,1024]{2,1,0:T(8,128)(2,1)S(1)} %collective-permute-done), channel_id=1, source_target_pairs={{0,1},{1,0},{2,3},{3,2},{4,5},{5,4},{6,7},{7,6},{8,9},{9,8},{10,11... | collective-permute-start | bytes 3538952 | tf_op jit(solution)/shard_map/ppermute | solution.py:13
  86.9 2.4 %collective-permute-done.2 = bf16[3,192,1024]{2,1,0:T(8,128)(2,1)S(1)} collective-permute-done((bf16[3,192,1024]{2,1,0:T(8,128)(2,1)S(1)}, bf16[3,192,1024]{2,1,0:T(8,128)(2,1)S(1)}, u32[]{:S(2)}, u32[]{:S(2)}) %collective-permute-start.2) | collective-permute-done | bytes 1179680 | tf_op jit(solution)/shard_map/ppermute | solution.py:13
  89.3 3.4 %pad_maximum_fusion = bf16[3,768,1024]{2,1,0:T(8,128)(2,1)S(1)} fusion(bf16[3,192,1024]{2,1,0:T(8,128)(2,1)S(1)} %collective-permute-done.2, bf16[3,192,1024]{2,1,0:T(8,128)(2,1)} %collective-permute-done.1, bf16[3,192,1024]{2,1,0:T(8,128)(2,1)S(1)} %collective-permute-done, bf16[1,192,1024]{2,1,0:T(8,128)(2,1)S(1)} %bitcast.97, ...), kind=kLoop, calls=%fused_computation.3 | loop fusion | flops 28311552 | bytes 9437184 | tf_op jit(solution)/shard_map/concatenate | solution.py:174
  92.7 2.1 %copy-done.1 = bf16[3,768,1024]{2,1,0:T(8,128)(2,1)} copy-done((bf16[3,768,1024]{2,1,0:T(8,128)(2,1)}, bf16[3,768,1024]{2,1,0:T(8,128)(2,1)S(1)}, u32[]{:S(2)}) %copy-start.1) | copy-done | bytes 4718616
  94.8 2.2 %fusion.2 = f32[512,768]{1,0:T(8,128)S(1)} fusion(bf16[3,768,1024]{2,1,0:T(8,128)(2,1)S(1)} %pad_maximum_fusion, bf16[64,8,8,128]{3,2,1,0:T(8,128)(2,1)} %bitcast.29), kind=kOutput, calls=%fused_computation.9 | convolution fusion | flops 805306368 | bytes 4194304 | tf_op jit(solution)/shard_map/dot_general | solution.py:18
  97.1 4.7 %fusion.4 = bf16[64,8,8,128]{3,1,2,0:T(8,128)(2,1)S(1)} fusion(bf16[3,768,1024]{2,1,0:T(8,128)(2,1)} %copy-done.1, f32[512,768]{1,0:T(8,128)S(1)} %fusion.2, bf16[64,8,8,128]{3,2,1,0:T(8,128)(2,1)} %bitcast.29), kind=kOutput, calls=%fused_computation.12 | convolution fusion | flops 1613496320 | bytes 6815744 | tf_op jit(solution)/shard_map/dot_general | solution.py:21
  101.7 1.3 copy.60
  103.0 18.3 %all-to-all-start.1 = ((bf16[512,8,128]{2,1,0:T(8,128)(2,1)}), bf16[512,8,128]{2,1,0:T(8,128)(2,1)S(1)}, u32[]{:S(2)}, u32[]{:S(2)}) async-start(bf16[512,8,128]{2,1,0:T(8,128)(2,1)} %bitcast.32), calls=%async_computation.1 | async-start | bytes 2097152 | tf_op jit(solution)/shard_map/all_to_all | solution.py:180
  121.3 0.1 reduce_sum.34
  121.5 0.1 copy.53
  121.6 0.1 copy.54
  121.7 0.1 copy.55
  121.8 0.1 reshape.182
  122.0 0.2 fusion.30
  122.2 1.9 %gather_fusion.1 = f32[256]{0:T(256)S(1)} fusion(f32[128,128]{1,0:T(8,128)S(1)} %fusion.30, s32[256]{0:T(256)S(1)} %reshape.182), kind=kCustom, calls=%fused_computation.1 | custom fusion | bytes 4096 | tf_op jit(solution)/shard_map/jit(take_along_axis)/gather | solution.py:155
  124.1 0.1 reshape.185
  124.4 0.1 copy.57
  124.6 1.0 copy.50.qt_ref
  125.6 3.6 %shard_map.113 = bf16[2,128,1024]{2,1,0:T(8,128)(2,1)} custom-call(s32[1]{0:T(128)} %bitcast.c_ref, bf16[2,128,1024]{2,1,0:T(8,128)(2,1)} %copy.50.qt_ref, bf16[2,2,4096,128]{3,2,1,0:T(8,128)(2,1)} %all-gather.2.cloned.1.call-done.k_ref.v_ref, bf16[2,2,4096,128]{3,2,1,0:T(8,128)(2,1)} %all-gather.2.cloned.1.call-done.k_ref.v_ref), custom_call_target="tpu_custom_call" | custom-call | flops 2147483648 | bytes 5242880 | tf_op jit(solution)/shard_map/pallas_call | solution.py:90
  129.2 1.3 copy.51
  130.5 0.9 copy_bitcast_fusion.1
  131.4 23.6 %all-to-all-done.1 = bf16[512,8,128]{2,1,0:T(8,128)(2,1)S(1)} async-done(((bf16[512,8,128]{2,1,0:T(8,128)(2,1)}), bf16[512,8,128]{2,1,0:T(8,128)(2,1)S(1)}, u32[]{:S(2)}, u32[]{:S(2)}) %all-to-all-start.1) | async-done | bytes 1048608 | tf_op jit(solution)/shard_map/all_to_all | solution.py:180
  155.0 0.3 copy.77
  155.2 1.2 gather_fusion
  156.4 0.2 gather.11
  156.6 2.3 %multiply_reduce_fusion = bf16[128,1024]{1,0:T(8,128)(2,1)} fusion(bf16[128,2,1024]{2,1,0:T(2,128)(2,1)S(1)} %gather.11, pred[128,2]{1,0:T(8,128)(4,1)S(1)} %copy.54, f32[128,2]{1,0:T(8,128)S(1)} %copy.57), kind=kLoop, calls=%fused_computation.17 | loop fusion | flops 917504 | bytes 787712 | tf_op jit(solution)/shard_map/reduce_sum | solution.py:186
  (38 shorter events, 0.4 us)
Async XLA Ops:
  7.2 117.3 %copy-start = (bf16[1,128,16,128]{3,2,1,0:T(8,128)(2,1)S(1)}, bf16[1,128,16,128]{3,2,1,0:T(8,128)(2,1)}, u32[]{:S(2)}) copy-start(bf16[1,128,16,128]{3,2,1,0:T(8,128)(2,1)} %param.11) | copy-start | bytes 1572868
  7.2 4.0 %copy-start.7 = (s32[1,128,2]{1,2,0:T(2,128)S(1)}, s32[1,128,2]{1,2,0:T(2,128)}, u32[]{:S(2)}) copy-start(s32[1,128,2]{1,2,0:T(2,128)} %param.14) | copy-start | bytes 3076
  7.2 4.3 %copy-start.8 = (bf16[1024]{0:T(1024)(128)(2,1)S(1)}, bf16[1024]{0:T(1024)(128)(2,1)}, u32[]{:S(2)}) copy-start(bf16[1024]{0:T(1024)(128)(2,1)} %param.15) | copy-start | bytes 6148
  7.2 4.3 %copy-start.5 = (bf16[1,128,1024]{2,1,0:T(8,128)(2,1)S(1)}, bf16[1,128,1024]{2,1,0:T(8,128)(2,1)}, u32[]{:S(2)}) copy-start(bf16[1,128,1024]{2,1,0:T(8,128)(2,1)} %param.10) | copy-start | bytes 786436
  7.2 118.4 %all-gather.2.cloned.1.call-start = ((), (), s32[]{:S(2)}) async-start(), calls=%async_computation.2 | async-start | bytes 4325376 | tf_op jit(solution)/shard_map/all_gather | solution.py:70
  15.7 24.3 %copy-start.2 = (bf16[192,1024]{1,0:T(8,128)(2,1)S(1)}, bf16[192,1024]{1,0:T(8,128)(2,1)}, u32[]{:S(2)}) copy-start(bf16[192,1024]{1,0:T(8,128)(2,1)} %param.19) | copy-start | bytes 1179652
  15.7 24.3 %copy-start.3 = (bf16[192,1024]{1,0:T(8,128)(2,1)S(1)}, bf16[192,1024]{1,0:T(8,128)(2,1)}, u32[]{:S(2)}) copy-start(bf16[192,1024]{1,0:T(8,128)(2,1)} %param.18) | copy-start | bytes 1179652
  15.7 24.3 %copy-start.4 = (bf16[192,1024]{1,0:T(8,128)(2,1)S(1)}, bf16[192,1024]{1,0:T(8,128)(2,1)}, u32[]{:S(2)}) copy-start(bf16[192,1024]{1,0:T(8,128)(2,1)} %param.17) | copy-start | bytes 1179652
  15.7 68.4 %all-to-all-start = ((bf16[512,8,128]{2,1,0:T(8,128)(2,1)}), bf16[512,8,128]{2,1,0:T(8,128)(2,1)}, u32[]{:S(2)}, u32[]{:S(2)}) async-start(bf16[512,8,128]{2,1,0:T(8,128)(2,1)} %bitcast.28), calls=%async_computation | async-start | bytes 2097152 | tf_op jit(solution)/shard_map/all_to_all | solution.py:171
  41.1 43.0 %collective-permute-start = (bf16[3,192,1024]{2,1,0:T(8,128)(2,1)}, bf16[3,192,1024]{2,1,0:T(8,128)(2,1)S(1)}, u32[]{:S(2)}, u32[]{:S(2)}) collective-permute-start(bf16[3,192,1024]{2,1,0:T(8,128)(2,1)} %pad_maximum_fusion.1), channel_id=1, source_target_pairs={{0,2},{1,3},{2,0},{3,1},{4,6},{5,7},{6,4},{7,5},{8,10},{9,11},{10,... | collective-permute-start | bytes 3538952 | tf_op jit(solution)/shard_map/ppermute | solution.py:13
  44.4 42.4 %collective-permute-start.1 = (bf16[3,192,1024]{2,1,0:T(8,128)(2,1)}, bf16[3,192,1024]{2,1,0:T(8,128)(2,1)}, u32[]{:S(2)}, u32[]{:S(2)}) collective-permute-start(bf16[3,192,1024]{2,1,0:T(8,128)(2,1)} %pad_maximum_fusion.1), channel_id=1, source_target_pairs={{0,1},{1,0},{2,3},{3,2},{4,5},{5,4},{6,7},{7,6},{8,9},{9,8},{10,11... | collective-permute-start | bytes 3538952 | tf_op jit(solution)/shard_map/ppermute | solution.py:13
  84.1 5.2 %collective-permute-start.2 = (bf16[3,192,1024]{2,1,0:T(8,128)(2,1)S(1)}, bf16[3,192,1024]{2,1,0:T(8,128)(2,1)S(1)}, u32[]{:S(2)}, u32[]{:S(2)}) collective-permute-start(bf16[3,192,1024]{2,1,0:T(8,128)(2,1)S(1)} %collective-permute-done), channel_id=1, source_target_pairs={{0,1},{1,0},{2,3},{3,2},{4,5},{5,4},{6,7},{7,6},{8,9},{9,8},{10,11... | collective-permute-start | bytes 3538952 | tf_op jit(solution)/shard_map/ppermute | solution.py:13
  92.7 2.1 %copy-start.1 = (bf16[3,768,1024]{2,1,0:T(8,128)(2,1)}, bf16[3,768,1024]{2,1,0:T(8,128)(2,1)S(1)}, u32[]{:S(2)}) copy-start(bf16[3,768,1024]{2,1,0:T(8,128)(2,1)S(1)} %pad_maximum_fusion) | copy-start | bytes 14155780
  103.0 19.0 %copy-start.6 = (bf16[1024,128]{1,0:T(8,128)(2,1)S(1)}, bf16[1024,128]{1,0:T(8,128)(2,1)}, u32[]{:S(2)}) copy-start(bf16[1024,128]{1,0:T(8,128)(2,1)} %param.16) | copy-start | bytes 786436
  103.0 52.0 %all-to-all-start.1 = ((bf16[512,8,128]{2,1,0:T(8,128)(2,1)}), bf16[512,8,128]{2,1,0:T(8,128)(2,1)S(1)}, u32[]{:S(2)}, u32[]{:S(2)}) async-start(bf16[512,8,128]{2,1,0:T(8,128)(2,1)} %bitcast.32), calls=%async_computation.1 | async-start | bytes 2097152 | tf_op jit(solution)/shard_map/all_to_all | solution.py:180
Sparse Core Ops, SparseCore 0:
  11.8 108.9 all-gather.1

commit v11 on v9

--- a/solution.py
+++ b/solution.py
@@ -62,7 +62,8 @@
     lax.fori_loop(0, c // span, body_wide, 0)
     lax.fori_loop(c // span * span, c, body, 0)
     update(c, True)
-    o_ref[0] = (acc_sc[...] / l_sc[...]).astype(o_ref.dtype)
+    result = (acc_sc[...] / l_sc[...]).T
+    o_ref[...] = result.reshape(o_ref.shape).astype(o_ref.dtype)
 
 
 def gather_attention_inputs(queries, key_rows, value_rows):
@@ -97,25 +98,21 @@
                 pl.BlockSpec((1, 1, total_rows, head_size), lambda g, c: (0, g, 0, 0)),
                 pl.BlockSpec((1, 1, total_rows, head_size), lambda g, c: (1, g, 0, 0)),
             ],
-            out_specs=pl.BlockSpec((1, head_size, width), lambda g, c: (g, 0, 0)),
+            out_specs=pl.BlockSpec((seq_rows, group_size, head_size), lambda g, c: (0, g, 0)),
             scratch_shapes=[
                 pltpu.VMEM((1, width), jnp.float32),
                 pltpu.VMEM((1, width), jnp.float32),
                 pltpu.VMEM((head_size, width), jnp.float32),
             ],
         ),
-        out_shape=jax.ShapeDtypeStruct((kv_count, head_size, width), jnp.bfloat16),
+        out_shape=jax.ShapeDtypeStruct((seq_rows, head_count, head_size), jnp.bfloat16),
         cost_estimate=pl.CostEstimate(
             flops=2 * kv_count * width * total_rows * head_size,
             transcendentals=kv_count * width * total_rows // 2,
             bytes_accessed=4 * kv_count * total_rows * head_size + 4 * kv_count * width * head_size,
         ),
     )(me, grouped_t, gathered, gathered)
-    return (
-        out.reshape(kv_count, head_size, seq_rows, group_size)
-        .transpose(2, 0, 3, 1)
-        .reshape(1, seq_rows, head_count, head_size)
-    )
+    return out[None]
 
 
 def local(

time: 169 us -> 167 us (0.988); the launches traced: 166 us -> 166 us
  waiting for transfers between devices: 60.8 us -> 63.3 us
  local copies, waits for them, and re-layouts: 17.9 us -> 15.7 us
    all_to_all x1, waiting for transfers between devices: 23.6 us -> 25.7 us  [local(): lax.all_to_all(computed, grid_axes, split_axis=0, concat_axis=0, tiled=True)]
  transfers between devices with their start and end apart: 6 -> 6, of which waited for: 3 -> 3; matrix products, arithmetic and copies ran while one was open for 15% -> 14% of each run, Pallas kernels for 2% -> 2%
where the time goes in v11:
time: 167 us; the launch traced here: 166 us
  waiting for transfers between devices  63.3 us (38%)
  starting transfers between devices  53.6 us (32%)
  local copies, waits for them, and re-layouts  15.7 us (9%)
  between operations  14.4 us (9%)
  other arithmetic  8.58 us (5%)
  matrix products  7.11 us (4%)
  Pallas kernels  3.65 us (2%)
    ppermute x3, waiting for transfers between devices, from_partner(): lax.ppermute(value, axis, [(i, i ^ flip) for i in range(lax.axis_size(axi...  37.5 us
    all_to_all x1, waiting for transfers between devices, local(): lax.all_to_all(computed, grid_axes, split_axis=0, concat_axis=0, tiled=True)  25.7 us
    all_to_all x1, starting transfers between devices, local(): lax.all_to_all(outgoing, grid_axes, split_axis=0, concat_axis=0, tiled=True)  24.2 us
    all_to_all x1, starting transfers between devices, local(): lax.all_to_all(computed, grid_axes, split_axis=0, concat_axis=0, tiled=True)  18.4 us
    ppermute x3, starting transfers between devices, from_partner(): lax.ppermute(value, axis, [(i, i ^ flip) for i in range(lax.axis_size(axi...  11 us
    unnamed x25, local copies, waits for them, and re-layouts  7.47 us
    dot_general x1, matrix products, expert_rows(): return jnp.dot(hidden, down_rows, preferred_element_type=jnp.float32)  4.65 us
    pallas_call x1, Pallas kernels, attention(): pl.pallas_call(functools.partial(_flash_kernel, seq_rows, group_size, sca...  3.65 us
  transfers between devices with their start and end apart: 6, of which 3 were waited for; matrix products, arithmetic and copies ran while one was open for 14% of the time, Pallas kernels for 2%

profile of v11, /device:TPU:1, one launch (start us, length us, event | category | flops | bytes accessed | tf_op | source)
XLA Modules:
  0.0 166.4 jit_solution(13989371770825124655)
XLA Ops:
  7.2 0.0 all-gather.2.cloned.1.call-start
  7.3 0.9 copy.44
  8.2 0.9 copy.45
  9.0 0.7 maximum_bitcast_fusion
  9.7 0.8 copy.39
  10.5 0.1 eq.31
  10.7 0.1 eq.27
  10.8 0.1 copy.41
  10.9 0.2 fusion.19
  11.2 0.1 copy.38
  11.4 0.1 mul.62
  11.5 0.1 fusion.14
  11.7 0.1 fusion.16
  11.8 0.3 broadcast_in_dim.30
  12.1 0.2 reshape.184
  12.3 0.2 fusion.21
  12.5 1.9 %scatter_custom_fusion = bf16[512,1024]{1,0:T(8,128)(2,1)S(1)} fusion(s32[256]{0:T(256)S(1)} %bitcast.102, bf16[256,1024]{1,0:T(8,128)(2,1)S(1)} %reshape.184, bf16[]{:T(256)} %constant.29.clone.1), kind=kCustom, calls=%fused_computation.28 | custom fusion | bytes 1048578 | tf_op jit(solution)/shard_map/scatter | solution.py:164
  14.4 1.2 copy.52
  15.7 24.2 %all-to-all-start = ((bf16[512,8,128]{2,1,0:T(8,128)(2,1)}), bf16[512,8,128]{2,1,0:T(8,128)(2,1)}, u32[]{:S(2)}, u32[]{:S(2)}) async-start(bf16[512,8,128]{2,1,0:T(8,128)(2,1)} %bitcast.25), calls=%async_computation | async-start | bytes 2097152 | tf_op jit(solution)/shard_map/all_to_all | solution.py:168
  39.9 1.1 pad_maximum_fusion.1
  41.1 3.3 %collective-permute-start = (bf16[3,192,1024]{2,1,0:T(8,128)(2,1)}, bf16[3,192,1024]{2,1,0:T(8,128)(2,1)}, u32[]{:S(2)}, u32[]{:S(2)}) collective-permute-start(bf16[3,192,1024]{2,1,0:T(8,128)(2,1)} %pad_maximum_fusion.1), channel_id=1, source_target_pairs={{0,2},{1,3},{2,0},{3,1},{4,6},{5,7},{6,4},{7,5},{8,10},{9,11},{10,... | collective-permute-start | bytes 3538952 | tf_op jit(solution)/shard_map/ppermute | solution.py:13
  44.4 4.9 %collective-permute-start.1 = (bf16[3,192,1024]{2,1,0:T(8,128)(2,1)}, bf16[3,192,1024]{2,1,0:T(8,128)(2,1)}, u32[]{:S(2)}, u32[]{:S(2)}) collective-permute-start(bf16[3,192,1024]{2,1,0:T(8,128)(2,1)} %pad_maximum_fusion.1), channel_id=1, source_target_pairs={{0,1},{1,0},{2,3},{3,2},{4,5},{5,4},{6,7},{7,6},{8,9},{9,8},{10,11... | collective-permute-start | bytes 3538952 | tf_op jit(solution)/shard_map/ppermute | solution.py:13
  49.3 34.8 %collective-permute-done = bf16[3,192,1024]{2,1,0:T(8,128)(2,1)} collective-permute-done((bf16[3,192,1024]{2,1,0:T(8,128)(2,1)}, bf16[3,192,1024]{2,1,0:T(8,128)(2,1)}, u32[]{:S(2)}, u32[]{:S(2)}) %collective-permute-start) | collective-permute-done | bytes 1179680 | tf_op jit(solution)/shard_map/ppermute | solution.py:13
  84.2 2.8 %collective-permute-start.2 = (bf16[3,192,1024]{2,1,0:T(8,128)(2,1)}, bf16[3,192,1024]{2,1,0:T(8,128)(2,1)S(1)}, u32[]{:S(2)}, u32[]{:S(2)}) collective-permute-start(bf16[3,192,1024]{2,1,0:T(8,128)(2,1)} %collective-permute-done), channel_id=1, source_target_pairs={{0,1},{1,0},{2,3},{3,2},{4,5},{5,4},{6,7},{7,6},{8,9},{9,8},{10,11... | collective-permute-start | bytes 3538952 | tf_op jit(solution)/shard_map/ppermute | solution.py:13
  86.9 2.7 %collective-permute-done.2 = bf16[3,192,1024]{2,1,0:T(8,128)(2,1)S(1)} collective-permute-done((bf16[3,192,1024]{2,1,0:T(8,128)(2,1)}, bf16[3,192,1024]{2,1,0:T(8,128)(2,1)S(1)}, u32[]{:S(2)}, u32[]{:S(2)}) %collective-permute-start.2) | collective-permute-done | bytes 1179680 | tf_op jit(solution)/shard_map/ppermute | solution.py:13
  89.6 3.6 %pad_maximum_fusion = bf16[3,768,1024]{2,1,0:T(8,128)(2,1)S(1)} fusion(bf16[3,192,1024]{2,1,0:T(8,128)(2,1)S(1)} %collective-permute-done.2, bf16[3,192,1024]{2,1,0:T(8,128)(2,1)} %collective-permute-done.1, bf16[3,192,1024]{2,1,0:T(8,128)(2,1)} %collective-permute-done, bf16[1,192,1024]{2,1,0:T(8,128)(2,1)S(1)} %bitcast.91, ...), kind=kLoop, calls=%fused_computation.3 | loop fusion | flops 28311552 | bytes 9437184 | tf_op jit(solution)/shard_map/concatenate | solution.py:171
  93.2 2.1 %copy-done.1 = bf16[3,768,1024]{2,1,0:T(8,128)(2,1)} copy-done((bf16[3,768,1024]{2,1,0:T(8,128)(2,1)}, bf16[3,768,1024]{2,1,0:T(8,128)(2,1)S(1)}, u32[]{:S(2)}) %copy-start.1) | copy-done | bytes 4718616
  95.4 2.2 %fusion.2 = f32[512,768]{1,0:T(8,128)S(1)} fusion(bf16[3,768,1024]{2,1,0:T(8,128)(2,1)S(1)} %pad_maximum_fusion, bf16[64,8,8,128]{3,2,1,0:T(8,128)(2,1)} %bitcast.26), kind=kOutput, calls=%fused_computation.9 | convolution fusion | flops 805306368 | bytes 4194304 | tf_op jit(solution)/shard_map/dot_general | solution.py:18
  97.6 4.7 %fusion.4 = bf16[64,8,8,128]{3,1,2,0:T(8,128)(2,1)S(1)} fusion(bf16[3,768,1024]{2,1,0:T(8,128)(2,1)} %copy-done.1, f32[512,768]{1,0:T(8,128)S(1)} %fusion.2, bf16[64,8,8,128]{3,2,1,0:T(8,128)(2,1)} %bitcast.26), kind=kOutput, calls=%fused_computation.12 | convolution fusion | flops 1613496320 | bytes 6815744 | tf_op jit(solution)/shard_map/dot_general | solution.py:21
  102.3 1.3 copy.54
  103.5 18.4 %all-to-all-start.1 = ((bf16[512,8,128]{2,1,0:T(8,128)(2,1)}), bf16[512,8,128]{2,1,0:T(8,128)(2,1)S(1)}, u32[]{:S(2)}, u32[]{:S(2)}) async-start(bf16[512,8,128]{2,1,0:T(8,128)(2,1)} %bitcast.29), calls=%async_computation.1 | async-start | bytes 2097152 | tf_op jit(solution)/shard_map/all_to_all | solution.py:177
  121.9 0.1 reduce_sum.34
  122.0 0.1 copy.47
  122.1 0.1 copy.48
  122.3 0.1 copy.49
  122.4 0.1 reshape.174
  122.5 0.2 fusion.30
  122.8 1.9 %gather_fusion.1 = f32[256]{0:T(256)S(1)} fusion(f32[128,128]{1,0:T(8,128)S(1)} %fusion.30, s32[256]{0:T(256)S(1)} %reshape.174), kind=kCustom, calls=%fused_computation.1 | custom fusion | bytes 4096 | tf_op jit(solution)/shard_map/jit(take_along_axis)/gather | solution.py:152
  124.7 0.1 reshape.177
  124.8 0.1 copy.50
  124.9 0.1 copy.51
  125.1 1.0 copy.46.qt_ref
  126.1 3.7 %shard_map.113 = bf16[128,16,128]{2,1,0:T(8,128)(2,1)} custom-call(s32[1]{0:T(128)} %bitcast.c_ref, bf16[2,128,1024]{2,1,0:T(8,128)(2,1)} %copy.46.qt_ref, bf16[2,2,4096,128]{3,2,1,0:T(8,128)(2,1)} %all-gather.2.cloned.1.call-done.k_ref.v_ref, bf16[2,2,4096,128]{3,2,1,0:T(8,128)(2,1)} %all-gather.2.cloned.1.call-done.k_ref.v_ref), custom_call_target="tpu_custom_call" | custom-call | flops 2147483648 | bytes 5242880 | tf_op jit(solution)/shard_map/pallas_call | solution.py:91
  129.8 25.7 %all-to-all-done.1 = bf16[512,8,128]{2,1,0:T(8,128)(2,1)S(1)} async-done(((bf16[512,8,128]{2,1,0:T(8,128)(2,1)}), bf16[512,8,128]{2,1,0:T(8,128)(2,1)S(1)}, u32[]{:S(2)}, u32[]{:S(2)}) %all-to-all-start.1) | async-done | bytes 1048608 | tf_op jit(solution)/shard_map/all_to_all | solution.py:177
  155.5 0.3 copy.70
  155.8 1.2 gather_fusion
  157.0 0.2 gather.11
  157.2 2.3 %multiply_reduce_fusion = bf16[128,1024]{1,0:T(8,128)(2,1)} fusion(bf16[128,2,1024]{2,1,0:T(2,128)(2,1)S(1)} %gather.11, pred[128,2]{1,0:T(8,128)(4,1)S(1)} %copy.48, f32[128,2]{1,0:T(8,128)S(1)} %copy.51), kind=kLoop, calls=%fused_computation.17 | loop fusion | flops 917504 | bytes 787712 | tf_op jit(solution)/shard_map/reduce_sum | solution.py:183
  (36 shorter events, 0.3 us)
Async XLA Ops:
  7.2 117.9 %copy-start = (bf16[1,128,16,128]{3,2,1,0:T(8,128)(2,1)S(1)}, bf16[1,128,16,128]{3,2,1,0:T(8,128)(2,1)}, u32[]{:S(2)}) copy-start(bf16[1,128,16,128]{3,2,1,0:T(8,128)(2,1)} %param.11) | copy-start | bytes 1572868
  7.2 4.0 %copy-start.7 = (s32[1,128,2]{1,2,0:T(2,128)S(1)}, s32[1,128,2]{1,2,0:T(2,128)}, u32[]{:S(2)}) copy-start(s32[1,128,2]{1,2,0:T(2,128)} %param.14) | copy-start | bytes 3076
  7.2 4.3 %copy-start.8 = (bf16[1024]{0:T(1024)(128)(2,1)S(1)}, bf16[1024]{0:T(1024)(128)(2,1)}, u32[]{:S(2)}) copy-start(bf16[1024]{0:T(1024)(128)(2,1)} %param.15) | copy-start | bytes 6148
  7.2 4.3 %copy-start.5 = (bf16[1,128,1024]{2,1,0:T(8,128)(2,1)S(1)}, bf16[1,128,1024]{2,1,0:T(8,128)(2,1)}, u32[]{:S(2)}) copy-start(bf16[1,128,1024]{2,1,0:T(8,128)(2,1)} %param.10) | copy-start | bytes 786436
  7.2 118.9 %all-gather.2.cloned.1.call-start = ((), (), s32[]{:S(2)}) async-start(), calls=%async_computation.2 | async-start | bytes 4325376 | tf_op jit(solution)/shard_map/all_gather | solution.py:71
  15.7 24.3 %copy-start.2 = (bf16[192,1024]{1,0:T(8,128)(2,1)S(1)}, bf16[192,1024]{1,0:T(8,128)(2,1)}, u32[]{:S(2)}) copy-start(bf16[192,1024]{1,0:T(8,128)(2,1)} %param.19) | copy-start | bytes 1179652
  15.7 24.3 %copy-start.3 = (bf16[192,1024]{1,0:T(8,128)(2,1)S(1)}, bf16[192,1024]{1,0:T(8,128)(2,1)}, u32[]{:S(2)}) copy-start(bf16[192,1024]{1,0:T(8,128)(2,1)} %param.18) | copy-start | bytes 1179652
  15.7 24.3 %copy-start.4 = (bf16[192,1024]{1,0:T(8,128)(2,1)S(1)}, bf16[192,1024]{1,0:T(8,128)(2,1)}, u32[]{:S(2)}) copy-start(bf16[192,1024]{1,0:T(8,128)(2,1)} %param.17) | copy-start | bytes 1179652
  15.7 68.5 %all-to-all-start = ((bf16[512,8,128]{2,1,0:T(8,128)(2,1)}), bf16[512,8,128]{2,1,0:T(8,128)(2,1)}, u32[]{:S(2)}, u32[]{:S(2)}) async-start(bf16[512,8,128]{2,1,0:T(8,128)(2,1)} %bitcast.25), calls=%async_computation | async-start | bytes 2097152 | tf_op jit(solution)/shard_map/all_to_all | solution.py:168
  41.1 43.1 %collective-permute-start = (bf16[3,192,1024]{2,1,0:T(8,128)(2,1)}, bf16[3,192,1024]{2,1,0:T(8,128)(2,1)}, u32[]{:S(2)}, u32[]{:S(2)}) collective-permute-start(bf16[3,192,1024]{2,1,0:T(8,128)(2,1)} %pad_maximum_fusion.1), channel_id=1, source_target_pairs={{0,2},{1,3},{2,0},{3,1},{4,6},{5,7},{6,4},{7,5},{8,10},{9,11},{10,... | collective-permute-start | bytes 3538952 | tf_op jit(solution)/shard_map/ppermute | solution.py:13
  44.4 42.5 %collective-permute-start.1 = (bf16[3,192,1024]{2,1,0:T(8,128)(2,1)}, bf16[3,192,1024]{2,1,0:T(8,128)(2,1)}, u32[]{:S(2)}, u32[]{:S(2)}) collective-permute-start(bf16[3,192,1024]{2,1,0:T(8,128)(2,1)} %pad_maximum_fusion.1), channel_id=1, source_target_pairs={{0,1},{1,0},{2,3},{3,2},{4,5},{5,4},{6,7},{7,6},{8,9},{9,8},{10,11... | collective-permute-start | bytes 3538952 | tf_op jit(solution)/shard_map/ppermute | solution.py:13
  84.2 5.4 %collective-permute-start.2 = (bf16[3,192,1024]{2,1,0:T(8,128)(2,1)}, bf16[3,192,1024]{2,1,0:T(8,128)(2,1)S(1)}, u32[]{:S(2)}, u32[]{:S(2)}) collective-permute-start(bf16[3,192,1024]{2,1,0:T(8,128)(2,1)} %collective-permute-done), channel_id=1, source_target_pairs={{0,1},{1,0},{2,3},{3,2},{4,5},{5,4},{6,7},{7,6},{8,9},{9,8},{10,11... | collective-permute-start | bytes 3538952 | tf_op jit(solution)/shard_map/ppermute | solution.py:13
  93.2 2.1 %copy-start.1 = (bf16[3,768,1024]{2,1,0:T(8,128)(2,1)}, bf16[3,768,1024]{2,1,0:T(8,128)(2,1)S(1)}, u32[]{:S(2)}) copy-start(bf16[3,768,1024]{2,1,0:T(8,128)(2,1)S(1)} %pad_maximum_fusion) | copy-start | bytes 14155780
  103.5 19.0 %copy-start.6 = (bf16[1024,128]{1,0:T(8,128)(2,1)S(1)}, bf16[1024,128]{1,0:T(8,128)(2,1)}, u32[]{:S(2)}) copy-start(bf16[1024,128]{1,0:T(8,128)(2,1)} %param.16) | copy-start | bytes 786436
  103.5 52.0 %all-to-all-start.1 = ((bf16[512,8,128]{2,1,0:T(8,128)(2,1)}), bf16[512,8,128]{2,1,0:T(8,128)(2,1)S(1)}, u32[]{:S(2)}, u32[]{:S(2)}) async-start(bf16[512,8,128]{2,1,0:T(8,128)(2,1)} %bitcast.29), calls=%async_computation.1 | async-start | bytes 2097152 | tf_op jit(solution)/shard_map/all_to_all | solution.py:177
Sparse Core Ops, SparseCore 0:
  11.8 108.9 all-gather.1
